TPU v7x, 128 devices: a whole 4x4x4 slice. The times are simulated.
128 devices in a mesh: dp: 4 (over z), expert: 32 (over x, y, core).
Axes of the slice: x: 4, y: 4, z: 4, core: 2. Of those that a mesh axis runs over, the one named last changes fastest.
Arguments:
- tokens: bfloat16 [8192, 4096], P('expert', 'dp'), may hold values from -6 to 6
- targets: bfloat16 [8192, 4096], P('expert', 'dp'), may hold values from -4 to 4
- expert_ids: int32 [8192, 2], P('expert'), may hold values from 0 to 31, all different within a row; in each aligned block of 256 rows (0 to 255, 256 to 511, ...) at most 32 rows name the same one
- gate_weights: float32 [8192, 2], P('expert'), may hold values from 0.2 to 1
- level_weights: float32 [8192], P('expert'), may hold values from 0.2 to 2
- w_gate: bfloat16 [32, 4096, 1024], P('expert', 'dp'), may hold values from -0.09375 to 0.09375
- w_up: bfloat16 [32, 4096, 1024], P('expert', 'dp'), may hold values from -0.09375 to 0.09375
- w_down: bfloat16 [32, 1024, 4096], P('expert', None, 'dp'), may hold values from -0.1875 to 0.1875
Outputs:
- mixed: bfloat16 [8192, 4096], P('expert', 'dp')
- token_grad: bfloat16 [8192, 4096], P('expert', 'dp')
- gate_grads: float32 [32, 4096, 1024], P('expert', 'dp')
- up_grads: float32 [32, 4096, 1024], P('expert', 'dp')
- down_grads: float32 [32, 1024, 4096], P('expert', None, 'dp')
Inputs may be any that keep to these rules, and one draw needn't show every extreme that they name: `expert_ids`: each row names two different experts. Among the rows of one device no expert is named more than 32 times, a bound that some block reaches.
All inputs are finite; a program needn't handle non-finite values.
Results may differ from a plain program's by a relative error of at most 0.0065.
Values may be sent and summed in bfloat16 or wider, within the bound.
No kernel may reach another device: no remote copies, remote signals or barrier semaphores. Data moves between devices by JAX's collectives and lax.ppermute only.
A program may use at most 128 MiB of HBM per device.

v0:
```python
import jax
import jax.numpy as jnp
from jax import lax
from jax.sharding import PartitionSpec as P


def slot_ranks(routing, experts):
    listed = routing.reshape(routing.shape[0], -1)
    onehot = (listed[:, :, None] == jnp.arange(experts, dtype=jnp.int32)[None, None, :]).astype(
        jnp.int32
    )
    earlier = jnp.cumsum(onehot, axis=1) - onehot
    return jnp.sum(earlier * onehot, axis=2)


def contract(left, right, left_dim, right_dim):
    return lax.dot_general(
        left, right, (((left_dim,), (right_dim,)), ((), ())), preferred_element_type=jnp.float32
    )


def activate(gate_pre, up_pre):
    sigmoid_gate = jax.nn.sigmoid(gate_pre)
    return (sigmoid_gate, (gate_pre * sigmoid_gate * up_pre).astype(jnp.bfloat16))


def derivatives(hidden_grad, gate_pre, up_pre, sigmoid_gate):
    gate_delta = (
        hidden_grad * up_pre * sigmoid_gate * (1.0 + gate_pre * (1.0 - sigmoid_gate))
    ).astype(jnp.bfloat16)
    up_delta = (hidden_grad * gate_pre * sigmoid_gate).astype(jnp.bfloat16)
    return (gate_delta, up_delta)


def shards(tokens, targets, expert_ids, gate_weights, level_weights, w_gate, w_up, w_down):
    experts = lax.axis_size("expert")
    tok_rows = tokens.shape[0]
    quarter = tokens.shape[1]
    capacity = 4 * tok_rows // experts
    rows_all = experts * capacity
    gate_mat = w_gate[0]
    up_mat = w_up[0]
    down_mat = w_down[0]
    ranks = slot_ranks(expert_ids.reshape(1, tok_rows, 2), experts).reshape(-1)
    slot_rows = expert_ids.reshape(-1) * capacity + ranks
    spread = jnp.repeat(tokens, 2, axis=0)
    outgoing = jnp.zeros((rows_all, quarter), jnp.bfloat16).at[slot_rows].set(spread)
    arrived = lax.all_to_all(
        outgoing.reshape(experts, capacity, quarter),
        "expert",
        split_axis=0,
        concat_axis=0,
        tiled=True,
    ).reshape(rows_all, quarter)
    gate_pre, up_pre = lax.psum(
        (contract(arrived, gate_mat, 1, 0), contract(arrived, up_mat, 1, 0)), "dp"
    )
    sigmoid_gate, hidden = activate(gate_pre, up_pre)
    out_slots = (
        contract(hidden, down_mat, 1, 0).astype(jnp.bfloat16).reshape(experts, capacity, quarter)
    )
    returned = lax.all_to_all(out_slots, "expert", split_axis=0, concat_axis=0, tiled=True).reshape(
        rows_all, quarter
    )
    picked = returned[slot_rows].reshape(tok_rows, 2, quarter).astype(jnp.float32)
    combined = jnp.sum(gate_weights[:, :, None] * picked, axis=1)
    mixed = combined.astype(jnp.bfloat16)
    row_grad = level_weights[:, None] * (combined - targets.astype(jnp.float32))
    slot_grad = (
        (gate_weights[:, :, None] * row_grad[:, None, :])
        .astype(jnp.bfloat16)
        .reshape(2 * tok_rows, quarter)
    )
    grad_out = jnp.zeros((rows_all, quarter), jnp.bfloat16).at[slot_rows].set(slot_grad)
    grad_slots = lax.all_to_all(
        grad_out.reshape(experts, capacity, quarter),
        "expert",
        split_axis=0,
        concat_axis=0,
        tiled=True,
    ).reshape(rows_all, quarter)
    down_grad = contract(hidden, grad_slots, 0, 0)
    hidden_grad = lax.psum(contract(grad_slots, down_mat, 1, 1), "dp")
    gate_delta, up_delta = derivatives(hidden_grad, gate_pre, up_pre, sigmoid_gate)
    input_slots = (contract(gate_delta, gate_mat, 1, 1) + contract(up_delta, up_mat, 1, 1)).astype(
        jnp.bfloat16
    )
    gate_grad = contract(arrived, gate_delta, 0, 0)
    up_grad = contract(arrived, up_delta, 0, 0)
    input_back = lax.all_to_all(
        input_slots.reshape(experts, capacity, quarter),
        "expert",
        split_axis=0,
        concat_axis=0,
        tiled=True,
    ).reshape(rows_all, quarter)
    token_grad = jnp.sum(
        input_back[slot_rows].reshape(tok_rows, 2, quarter).astype(jnp.float32), axis=1
    ).astype(jnp.bfloat16)
    return (mixed, token_grad, gate_grad[None], up_grad[None], down_grad[None])


def solution(mesh):
    in_specs = (
        P("expert", "dp"),
        P("expert", "dp"),
        P("expert", None),
        P("expert", None),
        P("expert"),
        P("expert", "dp", None),
        P("expert", "dp", None),
        P("expert", None, "dp"),
    )
    out_specs = (
        P("expert", "dp"),
        P("expert", "dp"),
        P("expert", "dp", None),
        P("expert", "dp", None),
        P("expert", None, "dp"),
    )
    return jax.shard_map(shards, mesh=mesh, in_specs=in_specs, out_specs=out_specs, check_vma=False)
```

profile of v0, /device:TPU:1, one launch (start us, length us, event | category | flops | bytes accessed | tf_op | source)
XLA Modules:
  0.0 486.4 jit_solution(16088306791532774817)
XLA Ops:
  11.0 1.6 broadcast_in_dim.8
  12.5 1.2 reshape.231
  14.0 4.8 scatter_custom_fusion
  18.8 37.2 %all_to_all.20 = bf16[32,32,1024]{2,1,0:T(8,128)(2,1)S(1)} all-to-all(bf16[32,32,1024]{2,1,0:T(8,128)(2,1)} %bitcast.64), channel_id=1, replica_groups=mesh['dp'=4,'expert'=32] {'expert'}, dimensions={0} | all-to-all | bytes 4194304 | tf_op jit(solution)/shard_map/all_to_all | solution.py:48
  56.0 4.4 fusion.6
  60.3 4.4 fusion.10
  64.7 159.0 %all-reduce.6.cloned.1.call-done = (f32[1024,1024]{1,0:T(8,128)}, f32[1024,1024]{1,0:T(8,128)}) async-done(((f32[1024,1024]{1,0:T(8,128)}, f32[1024,1024]{1,0:T(8,128)}), (f32[1024,1024]{1,0:T(8,128)}, f32[1024,1024]{1,0:T(8,128)})) %all-reduce.6.cloned.1.call-update) | async-done | bytes 8388624 | tf_op jit(solution)/shard_map/psum | solution.py:55
  223.7 4.8 multiply_convert_fusion.2
  228.6 3.7 fusion.12
  232.2 7.9 %all-to-all-start.1 = ((bf16[32,32,1024]{2,1,0:T(8,128)(2,1)}), bf16[32,32,1024]{2,1,0:T(8,128)(2,1)}, u32[]{:S(2)}, u32[]{:S(2)}) async-start(bf16[32,32,1024]{2,1,0:T(8,128)(2,1)} %bitcast.72), calls=%async_computation.1 | async-start | bytes 4194304 | tf_op jit(solution)/shard_map/all_to_all | solution.py:62
  241.0 27.5 %all-to-all-done.1 = bf16[32,32,1024]{2,1,0:T(8,128)(2,1)} async-done(((bf16[32,32,1024]{2,1,0:T(8,128)(2,1)}), bf16[32,32,1024]{2,1,0:T(8,128)(2,1)}, u32[]{:S(2)}, u32[]{:S(2)}) %all-to-all-start.1) | async-done | bytes 2097184 | tf_op jit(solution)/shard_map/all_to_all | solution.py:62
  268.5 4.6 gather_fusion
  273.1 2.3 reshape.210
  275.4 4.3 multiply_reduce_fusion
  280.8 2.0 mul.89
  282.9 3.6 mul.90
  286.5 5.2 %scatter_custom_fusion.1 = bf16[1024,1024]{1,0:T(8,128)(2,1)} fusion(s32[512]{0:T(512)S(1)} %bitcast.79, f32[512,1024]{1,0:T(8,128)} %mul.90, f32[512]{0:T(512)S(1)} %mul.85, bf16[]{:T(256)} %constant.6.clone.1), kind=kCustom, calls=%fused_computation.27 | custom fusion | flops 1048576 | bytes 4196354 | tf_op jit(solution)/shard_map/scatter | solution.py:74
  291.7 32.9 %all_to_all.21 = bf16[32,32,1024]{2,1,0:T(8,128)(2,1)S(1)} all-to-all(bf16[32,32,1024]{2,1,0:T(8,128)(2,1)} %bitcast.63), channel_id=1, replica_groups=mesh['dp'=4,'expert'=32] {'expert'}, dimensions={0} | all-to-all | bytes 4194304 | tf_op jit(solution)/shard_map/all_to_all | solution.py:75
  324.6 1.3 copy-done.6
  325.9 4.4 fusion
  330.4 89.1 %all-reduce.4.cloned.1.call-done = f32[1024,1024]{1,0:T(8,128)} async-done(((f32[1024,1024]{1,0:T(8,128)}), f32[1024,1024]{1,0:T(8,128)}) %all-reduce.4.cloned.1.call-update) | async-done | bytes 4194320 | tf_op jit(solution)/shard_map/psum | solution.py:83
  419.5 6.0 %multiply_convert_fusion.1 = (bf16[1024,1024]{1,0:T(8,128)(2,1)S(1)}, bf16[1024,1024]{1,0:T(8,128)(2,1)S(1)}) fusion(f32[1024,1024]{1,0:T(8,128)} %get-tuple-element.6, f32[1024,1024]{1,0:T(8,128)} %all-reduce.4.cloned.1.call-done, f32[1024,1024]{1,0:T(8,128)} %get-tuple-element.5), kind=kLoop, calls=%fused_computation.6 | loop fusion | flops 13631488 | bytes 16777216 | tf_op jit(solution)/shard_map/convert_element_type | solution.py:30
  425.6 2.4 fusion.4
  428.6 3.7 add_convert_fusion
  432.3 8.3 %all-to-all-start.3 = ((bf16[32,32,1024]{2,1,0:T(8,128)(2,1)}), bf16[32,32,1024]{2,1,0:T(8,128)(2,1)}, u32[]{:S(2)}, u32[]{:S(2)}) async-start(bf16[32,32,1024]{2,1,0:T(8,128)(2,1)} %bitcast.71), calls=%async_computation.3 | async-start | bytes 4194304 | tf_op jit(solution)/shard_map/all_to_all | solution.py:90
  440.7 6.1 %convolution_bitcast_fusion = f32[1,1024,1024]{2,1,0:T(8,128)} fusion(bf16[1024,1024]{1,0:T(8,128)(2,1)S(1)} %copy-done.3, bf16[1024,1024]{1,0:T(8,128)(2,1)} %bitcast.70), kind=kOutput, calls=%fused_computation.9 | convolution fusion | flops 2147483648 | bytes 8388608 | tf_op jit(solution)/shard_map/dot_general | solution.py:17
  446.8 4.4 convolution_bitcast_fusion.2
  451.3 4.4 convolution_bitcast_fusion.1
  455.7 13.1 %all-to-all-done.3 = bf16[32,32,1024]{2,1,0:T(8,128)(2,1)} async-done(((bf16[32,32,1024]{2,1,0:T(8,128)(2,1)}), bf16[32,32,1024]{2,1,0:T(8,128)(2,1)}, u32[]{:S(2)}, u32[]{:S(2)}) %all-to-all-start.3) | async-done | bytes 2097184 | tf_op jit(solution)/shard_map/all_to_all | solution.py:90
  468.8 4.7 gather_fusion.1
  473.6 1.2 reshape.209
  474.8 4.6 reduce_sum.35
  (59 shorter events, 6.6 us)
Async XLA Ops:
  7.2 221.4 %copy-start = (bf16[1,1024,1024]{2,1,0:T(8,128)(2,1)S(1)}, bf16[1,1024,1024]{2,1,0:T(8,128)(2,1)}, u32[]{:S(2)}) copy-start(bf16[1,1024,1024]{2,1,0:T(8,128)(2,1)} %param.15) | copy-start | bytes 6291460
  7.2 216.5 %all-reduce.6.cloned.1.call-start = ((), (), s32[]{:S(2)}) async-start(), calls=%async_computation.5 | async-start | bytes 16777216 | tf_op jit(solution)/shard_map/psum | solution.py:55
  18.8 37.2 %copy-start.14 = (bf16[1,1024,1024]{2,1,0:T(8,128)(2,1)S(1)}, bf16[1,1024,1024]{2,1,0:T(8,128)(2,1)}, u32[]{:S(2)}) copy-start(bf16[1,1024,1024]{2,1,0:T(8,128)(2,1)} %param.14) | copy-start | bytes 6291460
  56.0 4.4 copy-start.4
  56.0 4.4 copy-start.16
  228.5 3.7 copy-start.2
  232.2 8.5 %copy-start.12 = (f32[256,2]{0,1:T(2,128)S(1)}, f32[256,2]{0,1:T(2,128)}, u32[]{:S(2)}) copy-start(f32[256,2]{0,1:T(2,128)} %param.11) | copy-start | bytes 6148
  232.2 36.3 %all-to-all-start.1 = ((bf16[32,32,1024]{2,1,0:T(8,128)(2,1)}), bf16[32,32,1024]{2,1,0:T(8,128)(2,1)}, u32[]{:S(2)}, u32[]{:S(2)}) async-start(bf16[32,32,1024]{2,1,0:T(8,128)(2,1)} %bitcast.72), calls=%async_computation.1 | async-start | bytes 4194304 | tf_op jit(solution)/shard_map/all_to_all | solution.py:62
  240.1 179.4 %all-reduce.4.cloned.1.call-start = ((), (), s32[]{:S(2)}) async-start(), calls=%async_computation.4 | async-start | bytes 8388608 | tf_op jit(solution)/shard_map/psum | solution.py:83
  275.4 4.3 copy-start.11
  275.4 4.4 copy-start.13
  324.6 1.3 copy-start.6
  419.5 6.0 %copy-start.15 = (bf16[1,1024,1024]{2,1,0:T(8,128)(2,1)S(1)}, bf16[1,1024,1024]{2,1,0:T(8,128)(2,1)}, u32[]{:S(2)}) copy-start(bf16[1,1024,1024]{2,1,0:T(8,128)(2,1)} %param.14) | copy-start | bytes 6291460
  425.5 2.5 copy-start.7
  425.5 2.5 copy-start.9
  425.5 3.1 copy-start.17
  432.3 8.3 %copy-start.3 = (bf16[1024,1024]{1,0:T(8,128)(2,1)S(1)}, bf16[1024,1024]{1,0:T(8,128)(2,1)}, u32[]{:S(2)}) copy-start(bf16[1024,1024]{1,0:T(8,128)(2,1)} %copy-done.2) | copy-start | bytes 6291460
  432.3 36.5 %all-to-all-start.3 = ((bf16[32,32,1024]{2,1,0:T(8,128)(2,1)}), bf16[32,32,1024]{2,1,0:T(8,128)(2,1)}, u32[]{:S(2)}, u32[]{:S(2)}) async-start(bf16[32,32,1024]{2,1,0:T(8,128)(2,1)} %bitcast.71), calls=%async_computation.3 | async-start | bytes 4194304 | tf_op jit(solution)/shard_map/all_to_all | solution.py:90
  440.6 6.2 %copy-start.5 = (bf16[32,32,1024]{2,1,0:T(8,128)(2,1)S(1)}, bf16[32,32,1024]{2,1,0:T(8,128)(2,1)}, u32[]{:S(2)}) copy-start(bf16[32,32,1024]{2,1,0:T(8,128)(2,1)} %copy-done.4) | copy-start | bytes 6291460
  440.6 6.2 %copy-start.10 = (bf16[1024,1024]{1,0:T(8,128)(2,1)S(1)}, bf16[1024,1024]{1,0:T(8,128)(2,1)}, u32[]{:S(2)}) copy-start(bf16[1024,1024]{1,0:T(8,128)(2,1)} %copy-done.9) | copy-start | bytes 6291460
  446.8 4.5 copy-start.8
  468.8 10.5 %copy-start.1 = (bf16[1,1024,1024]{2,1,0:T(8,128)(2,1)S(1)}, bf16[1,1024,1024]{2,1,0:T(8,128)(2,1)}, u32[]{:S(2)}) copy-start(bf16[1,1024,1024]{2,1,0:T(8,128)(2,1)} %param.15) | copy-start | bytes 6291460
Sparse Core Ops, SparseCore 0:
  64.8 158.8 all-reduce.5
  330.5 88.9 all-reduce.3
where the time goes:
time: 491 us; the launch traced here: 486 us
  waiting for transfers between devices  289 us (59%)
  blocking collectives  70.1 us (14%)
  matrix products  38 us (8%)
  local copies, waits for them, and re-layouts  30.1 us (6%)
  other arithmetic  28.2 us (6%)
  starting transfers between devices  16.8 us (3%)
  between operations  14.5 us (3%)
    psum x1, waiting for transfers between devices, shards(): lax.psum((contract(arrived, gate_mat, 1, 0), contract(arrived, up_mat, 1,...  159 us
    psum x1, waiting for transfers between devices, shards(): hidden_grad = lax.psum(contract(grad_slots, down_mat, 1, 1), 'dp')  89.1 us
    dot_general x9, matrix products, contract(): lax.dot_general(left, right, (((left_dim,), (right_dim,)), ((), ())), pre...  38 us
    all_to_all x1, blocking collectives, shards(): lax.all_to_all(outgoing.reshape(experts, capacity, quarter), 'expert', sp...  37.2 us
    all_to_all x1, blocking collectives, shards(): lax.all_to_all(grad_out.reshape(experts, capacity, quarter), 'expert', sp...  32.9 us
    all_to_all x1, waiting for transfers between devices, shards(): lax.all_to_all(out_slots, 'expert', split_axis=0, concat_axis=0, tiled=True)  27.5 us
    all_to_all x1, waiting for transfers between devices, shards(): lax.all_to_all(input_slots.reshape(experts, capacity, quarter), 'expert',...  13.1 us
  transfers between devices with their start and end apart: 4, of which 4 were waited for; matrix products, arithmetic and copies ran while one was open for 3% of the time, Pallas kernels for 0%

commit v1 on v0

--- a/solution.py
+++ b/solution.py
@@ -52,10 +52,14 @@
         concat_axis=0,
         tiled=True,
     ).reshape(rows_all, quarter)
-    gate_pre, up_pre = lax.psum(
-        (contract(arrived, gate_mat, 1, 0), contract(arrived, up_mat, 1, 0)), "dp"
+    gate_pre, up_pre = lax.psum_scatter(
+        (contract(arrived, gate_mat, 1, 0), contract(arrived, up_mat, 1, 0)),
+        "dp",
+        scatter_dimension=0,
+        tiled=True,
     )
-    sigmoid_gate, hidden = activate(gate_pre, up_pre)
+    sigmoid_gate, hidden_part = activate(gate_pre, up_pre)
+    hidden = lax.all_gather(hidden_part, "dp", axis=0, tiled=True)
     out_slots = (
         contract(hidden, down_mat, 1, 0).astype(jnp.bfloat16).reshape(experts, capacity, quarter)
     )
@@ -80,8 +84,11 @@
         tiled=True,
     ).reshape(rows_all, quarter)
     down_grad = contract(hidden, grad_slots, 0, 0)
-    hidden_grad = lax.psum(contract(grad_slots, down_mat, 1, 1), "dp")
-    gate_delta, up_delta = derivatives(hidden_grad, gate_pre, up_pre, sigmoid_gate)
+    hidden_grad = lax.psum_scatter(
+        contract(grad_slots, down_mat, 1, 1), "dp", scatter_dimension=0, tiled=True
+    )
+    gate_part, up_part = derivatives(hidden_grad, gate_pre, up_pre, sigmoid_gate)
+    gate_delta, up_delta = lax.all_gather((gate_part, up_part), "dp", axis=0, tiled=True)
     input_slots = (contract(gate_delta, gate_mat, 1, 1) + contract(up_delta, up_mat, 1, 1)).astype(
         jnp.bfloat16
     )

time: 491 us -> 473 us (0.963)
  waiting for transfers between devices: 289 us -> 260 us
  matrix products: 38 us -> 49.4 us
  other arithmetic: 28.2 us -> 22.8 us
    psum x2 -> x0, waiting for transfers between devices: 248 us -> none  [the longest x1 159 us: shards(): lax.psum((contract(arrived, gate_mat, 1, 0), contract(arrived, up_mat, 1,...]
    reduce_scatter x0 -> x3, waiting for transfers between devices: none -> 132 us  [the longest x2 88.6 us: shards(): lax.psum_scatter((contract(arrived, gate_mat, 1, 0), contract(arrived, up...]
    all_gather x0 -> x3, waiting for transfers between devices: none -> 87.1 us  [the longest x2 56.4 us: shards(): lax.all_gather((gate_part, up_part), 'dp', axis=0, tiled=True)]
    dot_general x9, matrix products: 38 us -> 49.4 us  [contract(): lax.dot_general(left, right, (((left_dim,), (right_dim,)), ((), ())), pre...]
  transfers between devices with their start and end apart: 4 -> 8, of which waited for: 4 -> 8; matrix products, arithmetic and copies ran while one was open for 3% -> 6% of each run, Pallas kernels for 0% -> 0%
where the time goes in v1:
time: 473 us; the launch traced here: 464 us
  waiting for transfers between devices  260 us (55%)
  blocking collectives  69.8 us (15%)
  matrix products  49.4 us (10%)
  local copies, waits for them, and re-layouts  30.8 us (7%)
  other arithmetic  22.8 us (5%)
  starting transfers between devices  16.5 us (3%)
  between operations  14.8 us (3%)
    reduce_scatter x2, waiting for transfers between devices, shards(): lax.psum_scatter((contract(arrived, gate_mat, 1, 0), contract(arrived, up...  88.6 us
    all_gather x2, waiting for transfers between devices, shards(): lax.all_gather((gate_part, up_part), 'dp', axis=0, tiled=True)  56.4 us
    dot_general x9, matrix products, contract(): lax.dot_general(left, right, (((left_dim,), (right_dim,)), ((), ())), pre...  49.4 us
    reduce_scatter x1, waiting for transfers between devices, shards(): lax.psum_scatter(contract(grad_slots, down_mat, 1, 1), 'dp', scatter_dime...  43.3 us
    all_to_all x1, blocking collectives, shards(): lax.all_to_all(outgoing.reshape(experts, capacity, quarter), 'expert', sp...  36.9 us
    all_to_all x1, blocking collectives, shards(): lax.all_to_all(grad_out.reshape(experts, capacity, quarter), 'expert', sp...  33 us
    all_gather x1, waiting for transfers between devices, shards(): hidden = lax.all_gather(hidden_part, 'dp', axis=0, tiled=True)  30.6 us
    all_to_all x1, waiting for transfers between devices, shards(): lax.all_to_all(out_slots, 'expert', split_axis=0, concat_axis=0, tiled=True)  27.9 us
  transfers between devices with their start and end apart: 8, of which 8 were waited for; matrix products, arithmetic and copies ran while one was open for 6% of the time, Pallas kernels for 0%

profile of v1, /device:TPU:1, one launch (start us, length us, event | category | flops | bytes accessed | tf_op | source)
XLA Modules:
  0.0 464.1 jit_solution(15432638927505919320)
XLA Ops:
  14.0 4.8 %scatter_custom_fusion = bf16[1024,1024]{1,0:T(8,128)(2,1)} fusion(s32[512]{0:T(512)S(1)} %bitcast.74, bf16[512,1024]{1,0:T(8,128)(2,1)} %reshape.231, bf16[]{:T(256)} %constant.6.clone.1), kind=kCustom, calls=%fused_computation.31 | custom fusion | bytes 2097664 | tf_op jit(solution)/shard_map/scatter | solution.py:47
  18.8 36.9 %all_to_all.20 = bf16[32,32,1024]{2,1,0:T(8,128)(2,1)S(1)} all-to-all(bf16[32,32,1024]{2,1,0:T(8,128)(2,1)} %bitcast.62), channel_id=1, replica_groups=mesh['dp'=4,'expert'=32] {'expert'}, dimensions={0} | all-to-all | bytes 4194304 | tf_op jit(solution)/shard_map/all_to_all | solution.py:48
  57.0 4.4 fusion.6
  61.4 6.6 %fusion.10 = f32[1024,1024]{1,0:T(8,128)} fusion(bf16[1024,1024]{1,0:T(8,128)(2,1)} %bitcast.64, bf16[1,1024,1024]{2,1,0:T(8,128)(2,1)} %param.13), kind=kOutput, calls=%fused_computation.18 | convolution fusion | flops 2147483648 | bytes 8388608 | tf_op jit(solution)/shard_map/dot_general | solution.py:17
  68.1 39.0 %reduce-scatter.6.cloned.1.call-done = f32[256,1024]{1,0:T(8,128)} async-done(((f32[1024,1024]{1,0:T(8,128)}), f32[256,1024]{1,0:T(8,128)}) %reduce-scatter.6.cloned.1.call-update) | async-done | bytes 1048592 | tf_op jit(solution)/shard_map/reduce_scatter | solution.py:55
  107.1 49.6 %reduce-scatter.4.cloned.1.call-done = f32[256,1024]{1,0:T(8,128)} async-done(((f32[1024,1024]{1,0:T(8,128)}), f32[256,1024]{1,0:T(8,128)}) %reduce-scatter.4.cloned.1.call-update) | async-done | bytes 1048592 | tf_op jit(solution)/shard_map/reduce_scatter | solution.py:55
  156.7 2.6 multiply_convert_fusion.4
  159.4 30.6 %all-gather.4.cloned.1.call-done = bf16[1024,1024]{1,0:T(8,128)(2,1)} async-done(((bf16[256,1024]{1,0:T(8,128)(2,1)}), bf16[1024,1024]{1,0:T(8,128)(2,1)}) %all-gather.4.cloned.1.call-update) | async-done | bytes 2097168 | tf_op jit(solution)/shard_map/all_gather | solution.py:62
  190.0 5.2 %fusion.12 = bf16[1024,1024]{1,0:T(8,128)(2,1)} fusion(bf16[1024,1024]{1,0:T(8,128)(2,1)} %all-gather.4.cloned.1.call-done, bf16[1,1024,1024]{2,1,0:T(8,128)(2,1)S(1)} %copy-done), kind=kOutput, calls=%fused_computation.22 | convolution fusion | flops 2148532224 | bytes 6291456 | tf_op jit(solution)/shard_map/dot_general | solution.py:17
  195.2 7.9 %all-to-all-start.1 = ((bf16[32,32,1024]{2,1,0:T(8,128)(2,1)}), bf16[32,32,1024]{2,1,0:T(8,128)(2,1)}, u32[]{:S(2)}, u32[]{:S(2)}) async-start(bf16[32,32,1024]{2,1,0:T(8,128)(2,1)} %bitcast.69), calls=%async_computation.3 | async-start | bytes 4194304 | tf_op jit(solution)/shard_map/all_to_all | solution.py:66
  203.7 27.9 %all-to-all-done.1 = bf16[32,32,1024]{2,1,0:T(8,128)(2,1)} async-done(((bf16[32,32,1024]{2,1,0:T(8,128)(2,1)}), bf16[32,32,1024]{2,1,0:T(8,128)(2,1)}, u32[]{:S(2)}, u32[]{:S(2)}) %all-to-all-start.1) | async-done | bytes 2097184 | tf_op jit(solution)/shard_map/all_to_all | solution.py:66
  231.5 4.6 gather_fusion
  236.1 2.3 reshape.210
  238.4 4.3 multiply_reduce_fusion
  243.8 2.0 mul.89
  245.9 3.6 mul.90
  249.5 5.2 %scatter_custom_fusion.1 = bf16[1024,1024]{1,0:T(8,128)(2,1)} fusion(s32[512]{0:T(512)S(1)} %bitcast.76, f32[512,1024]{1,0:T(8,128)} %mul.90, f32[512]{0:T(512)S(1)} %mul.85, bf16[]{:T(256)} %constant.6.clone.1), kind=kCustom, calls=%fused_computation.23 | custom fusion | flops 1048576 | bytes 4196354 | tf_op jit(solution)/shard_map/scatter | solution.py:78
  254.7 33.0 %all_to_all.21 = bf16[32,32,1024]{2,1,0:T(8,128)(2,1)S(1)} all-to-all(bf16[32,32,1024]{2,1,0:T(8,128)(2,1)} %bitcast.61), channel_id=1, replica_groups=mesh['dp'=4,'expert'=32] {'expert'}, dimensions={0} | all-to-all | bytes 4194304 | tf_op jit(solution)/shard_map/all_to_all | solution.py:79
  289.0 4.4 fusion
  293.5 43.3 %reduce-scatter.8.cloned.1.call-done = f32[256,1024]{1,0:T(8,128)} async-done(((f32[1024,1024]{1,0:T(8,128)}), f32[256,1024]{1,0:T(8,128)}) %reduce-scatter.8.cloned.1.call-update) | async-done | bytes 1048592 | tf_op jit(solution)/shard_map/reduce_scatter | solution.py:87
  336.8 2.8 multiply_convert_fusion.3
  340.3 30.0 %all-gather.8.cloned.1.call-done = bf16[1024,1024]{1,0:T(8,128)(2,1)} async-done(((bf16[256,1024]{1,0:T(8,128)(2,1)}), bf16[1024,1024]{1,0:T(8,128)(2,1)}) %all-gather.8.cloned.1.call-update) | async-done | bytes 2097168 | tf_op jit(solution)/shard_map/all_gather | solution.py:91
  370.3 6.6 %fusion.4 = f32[1024,1024]{1,0:T(8,128)} fusion(bf16[1024,1024]{1,0:T(8,128)(2,1)} %all-gather.8.cloned.1.call-done, bf16[1,1024,1024]{2,1,0:T(8,128)(2,1)} %param.14), kind=kOutput, calls=%fused_computation.12 | convolution fusion | flops 2147483648 | bytes 8388608 | tf_op jit(solution)/shard_map/dot_general | solution.py:17
  376.9 26.4 %all-gather.6.cloned.1.call-done = bf16[1024,1024]{1,0:T(8,128)(2,1)} async-done(((bf16[256,1024]{1,0:T(8,128)(2,1)}), bf16[1024,1024]{1,0:T(8,128)(2,1)}) %all-gather.6.cloned.1.call-update) | async-done | bytes 2097168 | tf_op jit(solution)/shard_map/all_gather | solution.py:91
  403.3 6.6 %add_convert_fusion = bf16[1024,1024]{1,0:T(8,128)(2,1)} fusion(f32[1024,1024]{1,0:T(8,128)} %fusion.4, bf16[1024,1024]{1,0:T(8,128)(2,1)} %all-gather.6.cloned.1.call-done, bf16[1,1024,1024]{2,1,0:T(8,128)(2,1)S(1)} %copy-done.11), kind=kOutput, calls=%fused_computation.4 | convolution fusion | flops 2149580800 | bytes 10485760 | tf_op jit(solution)/shard_map/dot_general | solution.py:17
  409.9 8.2 %all-to-all-start.3 = ((bf16[32,32,1024]{2,1,0:T(8,128)(2,1)}), bf16[32,32,1024]{2,1,0:T(8,128)(2,1)}, u32[]{:S(2)}, u32[]{:S(2)}) async-start(bf16[32,32,1024]{2,1,0:T(8,128)(2,1)} %bitcast.17), calls=%async_computation.6 | async-start | bytes 4194304 | tf_op jit(solution)/shard_map/all_to_all | solution.py:97
  418.1 6.8 %convolution_bitcast_fusion = f32[1,1024,1024]{2,1,0:T(8,128)} fusion(bf16[1024,1024]{1,0:T(8,128)(2,1)} %all-gather.4.cloned.1.call-done, bf16[1024,1024]{1,0:T(8,128)(2,1)} %bitcast.68), kind=kOutput, calls=%fused_computation.5 | convolution fusion | flops 2147483648 | bytes 8388608 | tf_op jit(solution)/shard_map/dot_general | solution.py:17
  424.9 4.4 convolution_bitcast_fusion.2
  429.3 4.4 convolution_bitcast_fusion.1
  433.7 12.5 %all-to-all-done.3 = bf16[32,32,1024]{2,1,0:T(8,128)(2,1)} async-done(((bf16[32,32,1024]{2,1,0:T(8,128)(2,1)}), bf16[32,32,1024]{2,1,0:T(8,128)(2,1)}, u32[]{:S(2)}, u32[]{:S(2)}) %all-to-all-start.3) | async-done | bytes 2097184 | tf_op jit(solution)/shard_map/all_to_all | solution.py:97
  446.2 4.7 %gather_fusion.1 = bf16[512,1024]{1,0:T(8,128)(2,1)S(1)} fusion(bf16[1024,1024]{1,0:T(8,128)(2,1)} %bitcast.18, s32[1024]{0:T(1024)S(1)} %pad_clamp_fusion), kind=kCustom, calls=%fused_computation.1 | custom fusion | bytes 2099200 | tf_op jit(solution)/shard_map/gather | solution.py:105
  452.2 4.6 reduce_sum.35
  (63 shorter events, 13.0 us)
Async XLA Ops:
  7.2 182.8 %copy-start = (bf16[1,1024,1024]{2,1,0:T(8,128)(2,1)S(1)}, bf16[1,1024,1024]{2,1,0:T(8,128)(2,1)}, u32[]{:S(2)}) copy-start(bf16[1,1024,1024]{2,1,0:T(8,128)(2,1)} %param.15) | copy-start | bytes 6291460
  7.2 99.9 %reduce-scatter.6.cloned.1.call-start = ((), (), s32[]{:S(2)}) async-start(), calls=%async_computation.8 | async-start | bytes 5242880 | tf_op jit(solution)/shard_map/reduce_scatter | solution.py:55
  18.8 38.2 %copy-start.10 = (bf16[1,1024,1024]{2,1,0:T(8,128)(2,1)S(1)}, bf16[1,1024,1024]{2,1,0:T(8,128)(2,1)}, u32[]{:S(2)}) copy-start(bf16[1,1024,1024]{2,1,0:T(8,128)(2,1)} %param.14) | copy-start | bytes 6291460
  55.7 1.3 copy-start.4
  61.4 95.3 %reduce-scatter.4.cloned.1.call-start = ((), (), s32[]{:S(2)}) async-start(), calls=%async_computation.7 | async-start | bytes 5242880 | tf_op jit(solution)/shard_map/reduce_scatter | solution.py:55
  68.0 122.0 %all-gather.4.cloned.1.call-start = ((), (), s32[]{:S(2)}) async-start(), calls=%async_computation.9 | async-start | bytes 2621440 | tf_op jit(solution)/shard_map/all_gather | solution.py:62
  195.2 8.1 %copy-start.8 = (f32[256,2]{0,1:T(2,128)S(1)}, f32[256,2]{0,1:T(2,128)}, u32[]{:S(2)}) copy-start(f32[256,2]{0,1:T(2,128)} %param.11) | copy-start | bytes 6148
  195.2 36.3 %all-to-all-start.1 = ((bf16[32,32,1024]{2,1,0:T(8,128)(2,1)}), bf16[32,32,1024]{2,1,0:T(8,128)(2,1)}, u32[]{:S(2)}, u32[]{:S(2)}) async-start(bf16[32,32,1024]{2,1,0:T(8,128)(2,1)} %bitcast.69), calls=%async_computation.3 | async-start | bytes 4194304 | tf_op jit(solution)/shard_map/all_to_all | solution.py:66
  203.1 133.7 %reduce-scatter.8.cloned.1.call-start = ((), (), s32[]{:S(2)}) async-start(), calls=%async_computation.10 | async-start | bytes 5242880 | tf_op jit(solution)/shard_map/reduce_scatter | solution.py:87
  238.4 4.3 copy-start.7
  238.4 4.4 copy-start.9
  287.7 1.3 copy-start.6
  293.5 43.4 %copy-start.2 = (f32[256,1024]{1,0:T(8,128)S(1)}, f32[256,1024]{1,0:T(8,128)}, u32[]{:S(2)}) copy-start(f32[256,1024]{1,0:T(8,128)} %reduce-scatter.6.cloned.1.call-done) | copy-start | bytes 3145732
  293.5 43.4 %copy-start.3 = (f32[256,1024]{1,0:T(8,128)S(1)}, f32[256,1024]{1,0:T(8,128)}, u32[]{:S(2)}) copy-start(f32[256,1024]{1,0:T(8,128)} %reduce-scatter.4.cloned.1.call-done) | copy-start | bytes 3145732
  293.5 76.8 %all-gather.8.cloned.1.call-start = ((), (), s32[]{:S(2)}) async-start(), calls=%async_computation.12 | async-start | bytes 2621440 | tf_op jit(solution)/shard_map/all_gather | solution.py:91
  339.7 63.6 %all-gather.6.cloned.1.call-start = ((), (), s32[]{:S(2)}) async-start(), calls=%async_computation.11 | async-start | bytes 2621440 | tf_op jit(solution)/shard_map/all_gather | solution.py:91
  340.3 63.0 %copy-start.11 = (bf16[1,1024,1024]{2,1,0:T(8,128)(2,1)S(1)}, bf16[1,1024,1024]{2,1,0:T(8,128)(2,1)}, u32[]{:S(2)}) copy-start(bf16[1,1024,1024]{2,1,0:T(8,128)(2,1)} %param.13) | copy-start | bytes 6291460
  409.9 36.4 %all-to-all-start.3 = ((bf16[32,32,1024]{2,1,0:T(8,128)(2,1)}), bf16[32,32,1024]{2,1,0:T(8,128)(2,1)}, u32[]{:S(2)}, u32[]{:S(2)}) async-start(bf16[32,32,1024]{2,1,0:T(8,128)(2,1)} %bitcast.17), calls=%async_computation.6 | async-start | bytes 4194304 | tf_op jit(solution)/shard_map/all_to_all | solution.py:97
  418.1 6.8 %copy-start.5 = (bf16[32,32,1024]{2,1,0:T(8,128)(2,1)S(1)}, bf16[32,32,1024]{2,1,0:T(8,128)(2,1)}, u32[]{:S(2)}) copy-start(bf16[32,32,1024]{2,1,0:T(8,128)(2,1)} %copy-done.4) | copy-start | bytes 6291460
  418.1 6.8 %copy-start.13 = (bf16[1024,1024]{1,0:T(8,128)(2,1)S(1)}, bf16[1024,1024]{1,0:T(8,128)(2,1)}, u32[]{:S(2)}) copy-start(bf16[1024,1024]{1,0:T(8,128)(2,1)} %all-gather.6.cloned.1.call-done) | copy-start | bytes 6291460
  424.9 4.4 copy-start.12
  446.2 10.5 %copy-start.1 = (bf16[1,1024,1024]{2,1,0:T(8,128)(2,1)S(1)}, bf16[1,1024,1024]{2,1,0:T(8,128)(2,1)}, u32[]{:S(2)}) copy-start(bf16[1,1024,1024]{2,1,0:T(8,128)(2,1)} %param.15) | copy-start | bytes 6291460
Sparse Core Ops, SparseCore 0:
  61.5 45.5 reduce-scatter.5
  110.0 46.6 reduce-scatter.3
  159.5 30.4 all-gather.3
  293.6 43.1 reduce-scatter.7
  339.8 30.4 all-gather.7
  372.4 30.8 all-gather.5

commit v2 on v1

--- a/solution.py
+++ b/solution.py
@@ -32,6 +32,13 @@
     return (gate_delta, up_delta)
 
 
+def dp_reduce_scatter(parts):
+    peers = lax.axis_size("dp")
+    pieces = parts.astype(jnp.bfloat16).reshape(peers, parts.shape[0] // peers, parts.shape[1])
+    got = lax.all_to_all(pieces, "dp", split_axis=0, concat_axis=0, tiled=True)
+    return jnp.sum(got.astype(jnp.float32), axis=0)
+
+
 def shards(tokens, targets, expert_ids, gate_weights, level_weights, w_gate, w_up, w_down):
     experts = lax.axis_size("expert")
     tok_rows = tokens.shape[0]
@@ -52,12 +59,11 @@
         concat_axis=0,
         tiled=True,
     ).reshape(rows_all, quarter)
-    gate_pre, up_pre = lax.psum_scatter(
-        (contract(arrived, gate_mat, 1, 0), contract(arrived, up_mat, 1, 0)),
-        "dp",
-        scatter_dimension=0,
-        tiled=True,
+    ff = gate_mat.shape[1]
+    both = dp_reduce_scatter(
+        jnp.concatenate([contract(arrived, gate_mat, 1, 0), contract(arrived, up_mat, 1, 0)], axis=1)
     )
+    gate_pre, up_pre = both[:, :ff], both[:, ff:]
     sigmoid_gate, hidden_part = activate(gate_pre, up_pre)
     hidden = lax.all_gather(hidden_part, "dp", axis=0, tiled=True)
     out_slots = (
@@ -84,9 +90,7 @@
         tiled=True,
     ).reshape(rows_all, quarter)
     down_grad = contract(hidden, grad_slots, 0, 0)
-    hidden_grad = lax.psum_scatter(
-        contract(grad_slots, down_mat, 1, 1), "dp", scatter_dimension=0, tiled=True
-    )
+    hidden_grad = dp_reduce_scatter(contract(grad_slots, down_mat, 1, 1))
     gate_part, up_part = derivatives(hidden_grad, gate_pre, up_pre, sigmoid_gate)
     gate_delta, up_delta = lax.all_gather((gate_part, up_part), "dp", axis=0, tiled=True)
     input_slots = (contract(gate_delta, gate_mat, 1, 1) + contract(up_delta, up_mat, 1, 1)).astype(

time: 473 us -> 406 us (0.86)
  waiting for transfers between devices: 260 us -> 122 us
  blocking collectives: 69.8 us -> 152 us
  matrix products: 49.4 us -> 41.2 us
    reduce_scatter x3 -> x0, waiting for transfers between devices: 132 us -> none  [the longest x2 88.6 us: shards(): lax.psum_scatter((contract(arrived, gate_mat, 1, 0), contract(arrived, up...]
    all_to_all x0 -> x2, blocking collectives: none -> 82 us  [dp_reduce_scatter(): got = lax.all_to_all(pieces, 'dp', split_axis=0, concat_axis=0, tiled=True)]
    dot_general x9, matrix products: 49.4 us -> 41.2 us  [contract(): lax.dot_general(left, right, (((left_dim,), (right_dim,)), ((), ())), pre...]
  transfers between devices with their start and end apart: 8 -> 5, of which waited for: 8 -> 5; matrix products, arithmetic and copies ran while one was open for 6% -> 6% of each run, Pallas kernels for 0% -> 0%
where the time goes in v2:
time: 406 us; the launch traced here: 398 us
  blocking collectives  152 us (37%)
  waiting for transfers between devices  122 us (30%)
  matrix products  41.2 us (10%)
  local copies, waits for them, and re-layouts  30.7 us (8%)
  other arithmetic  21.7 us (5%)
  starting transfers between devices  16.2 us (4%)
  between operations  14.5 us (4%)
    all_to_all x2, blocking collectives, dp_reduce_scatter(): got = lax.all_to_all(pieces, 'dp', split_axis=0, concat_axis=0, tiled=True)  82 us
    all_gather x2, waiting for transfers between devices, shards(): lax.all_gather((gate_part, up_part), 'dp', axis=0, tiled=True)  53.2 us
    dot_general x9, matrix products, contract(): lax.dot_general(left, right, (((left_dim,), (right_dim,)), ((), ())), pre...  41.2 us
    all_to_all x1, blocking collectives, shards(): lax.all_to_all(outgoing.reshape(experts, capacity, quarter), 'expert', sp...  36.9 us
    all_to_all x1, blocking collectives, shards(): lax.all_to_all(grad_out.reshape(experts, capacity, quarter), 'expert', sp...  33 us
    all_to_all x1, waiting for transfers between devices, shards(): lax.all_to_all(out_slots, 'expert', split_axis=0, concat_axis=0, tiled=True)  28 us
    all_gather x1, waiting for transfers between devices, shards(): hidden = lax.all_gather(hidden_part, 'dp', axis=0, tiled=True)  27.5 us
    all_to_all x1, waiting for transfers between devices, shards(): lax.all_to_all(input_slots.reshape(experts, capacity, quarter), 'expert',...  12.5 us
  transfers between devices with their start and end apart: 5, of which 5 were waited for; matrix products, arithmetic and copies ran while one was open for 6% of the time, Pallas kernels for 0%

profile of v2, /device:TPU:1, one launch (start us, length us, event | category | flops | bytes accessed | tf_op | source)
XLA Modules:
  0.0 398.0 jit_solution(3197770220481358459)
XLA Ops:
  11.0 1.6 broadcast_in_dim.8
  14.0 4.8 %scatter_custom_fusion = bf16[1024,1024]{1,0:T(8,128)(2,1)} fusion(s32[512]{0:T(512)S(1)} %bitcast.85, bf16[512,1024]{1,0:T(8,128)(2,1)} %reshape.242, bf16[]{:T(256)} %constant.6.clone.1), kind=kCustom, calls=%fused_computation.37 | custom fusion | bytes 2097664 | tf_op jit(solution)/shard_map/scatter | solution.py:54
  18.8 36.9 %all_to_all.30 = bf16[32,32,1024]{2,1,0:T(8,128)(2,1)S(1)} all-to-all(bf16[32,32,1024]{2,1,0:T(8,128)(2,1)} %bitcast.72), channel_id=1, replica_groups=mesh['dp'=4,'expert'=32] {'expert'}, dimensions={0} | all-to-all | bytes 4194304 | tf_op jit(solution)/shard_map/all_to_all | solution.py:55
  55.7 2.3 fusion.15
  58.0 2.3 fusion.12
  60.8 53.5 %all_to_all.31 = bf16[4,256,2048]{2,1,0:T(8,128)(2,1)S(1)} all-to-all(bf16[4,256,2048]{2,1,0:T(8,128)(2,1)S(1)} %pad_maximum_fusion), channel_id=1, replica_groups=mesh['dp'=4,'expert'=32] {'dp'}, dimensions={0} | all-to-all | bytes 8388608 | tf_op jit(solution)/shard_map/all_to_all | solution.py:38
  115.1 1.3 copy-done.2
  117.6 27.5 %all-gather.4.cloned.1.call-done = bf16[1024,1024]{1,0:T(8,128)(2,1)} async-done(((bf16[256,1024]{1,0:T(8,128)(2,1)}), bf16[1024,1024]{1,0:T(8,128)(2,1)}) %all-gather.4.cloned.1.call-update) | async-done | bytes 2097168 | tf_op jit(solution)/shard_map/all_gather | solution.py:68
  145.1 5.2 %fusion.18 = bf16[1024,1024]{1,0:T(8,128)(2,1)} fusion(bf16[1024,1024]{1,0:T(8,128)(2,1)} %all-gather.4.cloned.1.call-done, bf16[1,1024,1024]{2,1,0:T(8,128)(2,1)S(1)} %copy-done), kind=kOutput, calls=%fused_computation.27 | convolution fusion | flops 2148532224 | bytes 6291456 | tf_op jit(solution)/shard_map/dot_general | solution.py:17
  150.3 7.9 %all-to-all-start.2 = ((bf16[32,32,1024]{2,1,0:T(8,128)(2,1)}), bf16[32,32,1024]{2,1,0:T(8,128)(2,1)}, u32[]{:S(2)}, u32[]{:S(2)}) async-start(bf16[32,32,1024]{2,1,0:T(8,128)(2,1)} %bitcast.79), calls=%async_computation.2 | async-start | bytes 4194304 | tf_op jit(solution)/shard_map/all_to_all | solution.py:72
  158.6 28.0 %all-to-all-done.2 = bf16[32,32,1024]{2,1,0:T(8,128)(2,1)} async-done(((bf16[32,32,1024]{2,1,0:T(8,128)(2,1)}), bf16[32,32,1024]{2,1,0:T(8,128)(2,1)}, u32[]{:S(2)}, u32[]{:S(2)}) %all-to-all-start.2) | async-done | bytes 2097184 | tf_op jit(solution)/shard_map/all_to_all | solution.py:72
  186.6 4.6 %gather_fusion = bf16[512,1024]{1,0:T(8,128)(2,1)S(1)} fusion(bf16[1024,1024]{1,0:T(8,128)(2,1)} %bitcast.16, s32[1024]{0:T(1024)S(1)} %pad_clamp_fusion), kind=kCustom, calls=%fused_computation | custom fusion | bytes 2099200 | tf_op jit(solution)/shard_map/gather | solution.py:75
  191.2 2.3 reshape.221
  193.5 4.3 %multiply_reduce_fusion = f32[256,1024]{1,0:T(8,128)S(1)} fusion(f32[256,2,1024]{2,1,0:T(2,128)} %reshape.221, f32[256,2]{1,0:T(8,128)S(1)} %copy.14), kind=kLoop, calls=%fused_computation.24 | loop fusion | flops 786432 | bytes 3147776 | tf_op jit(solution)/shard_map/reduce_sum | solution.py:76
  198.9 2.0 mul.89
  201.0 3.6 mul.90
  204.6 5.2 %scatter_custom_fusion.1 = bf16[1024,1024]{1,0:T(8,128)(2,1)} fusion(s32[512]{0:T(512)S(1)} %bitcast.87, f32[512,1024]{1,0:T(8,128)} %mul.90, f32[512]{0:T(512)S(1)} %mul.85, bf16[]{:T(256)} %constant.6.clone.1), kind=kCustom, calls=%fused_computation.29 | custom fusion | flops 1048576 | bytes 4196354 | tf_op jit(solution)/shard_map/scatter | solution.py:84
  209.8 33.0 %all_to_all.32 = bf16[32,32,1024]{2,1,0:T(8,128)(2,1)S(1)} all-to-all(bf16[32,32,1024]{2,1,0:T(8,128)(2,1)} %bitcast.71), channel_id=1, replica_groups=mesh['dp'=4,'expert'=32] {'expert'}, dimensions={0} | all-to-all | bytes 4194304 | tf_op jit(solution)/shard_map/all_to_all | solution.py:85
  242.8 2.4 fusion.21
  245.2 28.5 %all_to_all.33 = bf16[4,256,1024]{2,1,0:T(8,128)(2,1)S(1)} all-to-all(bf16[4,256,1024]{2,1,0:T(8,128)(2,1)S(1)} %bitcast.80), channel_id=1, replica_groups=mesh['dp'=4,'expert'=32] {'dp'}, dimensions={0} | all-to-all | bytes 4194304 | tf_op jit(solution)/shard_map/all_to_all | solution.py:38
  275.4 1.6 multiply_convert_fusion.3
  277.7 26.7 %all-gather.8.cloned.1.call-done = bf16[1024,1024]{1,0:T(8,128)(2,1)} async-done(((bf16[256,1024]{1,0:T(8,128)(2,1)}), bf16[1024,1024]{1,0:T(8,128)(2,1)}) %all-gather.8.cloned.1.call-update) | async-done | bytes 2097168 | tf_op jit(solution)/shard_map/all_gather | solution.py:95
  304.4 6.6 %fusion.6 = f32[1024,1024]{1,0:T(8,128)} fusion(bf16[1024,1024]{1,0:T(8,128)(2,1)} %all-gather.8.cloned.1.call-done, bf16[1,1024,1024]{2,1,0:T(8,128)(2,1)} %param.14), kind=kOutput, calls=%fused_computation.17 | convolution fusion | flops 2147483648 | bytes 8388608 | tf_op jit(solution)/shard_map/dot_general | solution.py:17
  311.0 26.5 %all-gather.6.cloned.1.call-done = bf16[1024,1024]{1,0:T(8,128)(2,1)} async-done(((bf16[256,1024]{1,0:T(8,128)(2,1)}), bf16[1024,1024]{1,0:T(8,128)(2,1)}) %all-gather.6.cloned.1.call-update) | async-done | bytes 2097168 | tf_op jit(solution)/shard_map/all_gather | solution.py:95
  337.6 6.6 %add_convert_fusion = bf16[1024,1024]{1,0:T(8,128)(2,1)} fusion(f32[1024,1024]{1,0:T(8,128)} %fusion.6, bf16[1024,1024]{1,0:T(8,128)(2,1)} %all-gather.6.cloned.1.call-done, bf16[1,1024,1024]{2,1,0:T(8,128)(2,1)S(1)} %copy-done.12), kind=kOutput, calls=%fused_computation.6 | convolution fusion | flops 2149580800 | bytes 10485760 | tf_op jit(solution)/shard_map/dot_general | solution.py:17
  344.1 8.2 %all-to-all-start.5 = ((bf16[32,32,1024]{2,1,0:T(8,128)(2,1)}), bf16[32,32,1024]{2,1,0:T(8,128)(2,1)}, u32[]{:S(2)}, u32[]{:S(2)}) async-start(bf16[32,32,1024]{2,1,0:T(8,128)(2,1)} %bitcast.20), calls=%async_computation.5 | async-start | bytes 4194304 | tf_op jit(solution)/shard_map/all_to_all | solution.py:101
  352.3 6.8 %convolution_bitcast_fusion = f32[1,1024,1024]{2,1,0:T(8,128)} fusion(bf16[1024,1024]{1,0:T(8,128)(2,1)} %all-gather.4.cloned.1.call-done, bf16[1024,1024]{1,0:T(8,128)(2,1)} %bitcast.78), kind=kOutput, calls=%fused_computation.8 | convolution fusion | flops 2147483648 | bytes 8388608 | tf_op jit(solution)/shard_map/dot_general | solution.py:17
  359.1 4.4 %convolution_bitcast_fusion.2 = f32[1,1024,1024]{2,1,0:T(8,128)} fusion(bf16[1024,1024]{1,0:T(8,128)(2,1)S(1)} %bitcast.75, bf16[1024,1024]{1,0:T(8,128)(2,1)S(1)} %copy-done.14), kind=kOutput, calls=%fused_computation.10 | convolution fusion | flops 2147483648 | bytes 8388608 | tf_op jit(solution)/shard_map/dot_general | solution.py:17
  363.6 4.4 %convolution_bitcast_fusion.1 = f32[1,1024,1024]{2,1,0:T(8,128)} fusion(bf16[1024,1024]{1,0:T(8,128)(2,1)S(1)} %bitcast.76, bf16[1024,1024]{1,0:T(8,128)(2,1)S(1)} %copy-done.13), kind=kOutput, calls=%fused_computation.9 | convolution fusion | flops 2147483648 | bytes 8388608 | tf_op jit(solution)/shard_map/dot_general | solution.py:17
  368.0 12.5 %all-to-all-done.5 = bf16[32,32,1024]{2,1,0:T(8,128)(2,1)} async-done(((bf16[32,32,1024]{2,1,0:T(8,128)(2,1)}), bf16[32,32,1024]{2,1,0:T(8,128)(2,1)}, u32[]{:S(2)}, u32[]{:S(2)}) %all-to-all-start.5) | async-done | bytes 2097184 | tf_op jit(solution)/shard_map/all_to_all | solution.py:101
  380.5 4.7 %gather_fusion.1 = bf16[512,1024]{1,0:T(8,128)(2,1)S(1)} fusion(bf16[1024,1024]{1,0:T(8,128)(2,1)} %bitcast.21, s32[1024]{0:T(1024)S(1)} %pad_clamp_fusion), kind=kCustom, calls=%fused_computation.1 | custom fusion | bytes 2099200 | tf_op jit(solution)/shard_map/gather | solution.py:109
  386.5 4.6 %reduce_sum.55 = bf16[256,1024]{1,0:T(8,128)(2,1)} reduce(bf16[256,2,1024]{2,1,0:T(2,128)(2,1)} %reshape.219, bf16[]{:T(256)} %constant.6.clone.1), dimensions={1}, to_apply=%region_8.9 | reduce | flops 262144 | bytes 1572866 | tf_op jit(solution)/shard_map/reduce_sum | solution.py:108
  (61 shorter events, 12.5 us)
Async XLA Ops:
  7.2 137.9 %copy-start = (bf16[1,1024,1024]{2,1,0:T(8,128)(2,1)S(1)}, bf16[1,1024,1024]{2,1,0:T(8,128)(2,1)}, u32[]{:S(2)}) copy-start(bf16[1,1024,1024]{2,1,0:T(8,128)(2,1)} %param.15) | copy-start | bytes 6291460
  7.2 137.9 %all-gather.4.cloned.1.call-start = ((), (), s32[]{:S(2)}) async-start(), calls=%async_computation.6 | async-start | bytes 2621440 | tf_op jit(solution)/shard_map/all_gather | solution.py:68
  18.8 36.9 %copy-start.10 = (bf16[1,1024,1024]{2,1,0:T(8,128)(2,1)S(1)}, bf16[1,1024,1024]{2,1,0:T(8,128)(2,1)}, u32[]{:S(2)}) copy-start(bf16[1,1024,1024]{2,1,0:T(8,128)(2,1)} %param.14) | copy-start | bytes 6291460
  55.7 2.4 copy-start.4
  55.7 2.4 copy-start.11
  115.1 1.3 copy-start.2
  150.3 7.9 %copy-start.8 = (f32[256,2]{0,1:T(2,128)S(1)}, f32[256,2]{0,1:T(2,128)}, u32[]{:S(2)}) copy-start(f32[256,2]{0,1:T(2,128)} %param.11) | copy-start | bytes 6148
  150.3 36.3 %all-to-all-start.2 = ((bf16[32,32,1024]{2,1,0:T(8,128)(2,1)}), bf16[32,32,1024]{2,1,0:T(8,128)(2,1)}, u32[]{:S(2)}, u32[]{:S(2)}) async-start(bf16[32,32,1024]{2,1,0:T(8,128)(2,1)} %bitcast.79), calls=%async_computation.2 | async-start | bytes 4194304 | tf_op jit(solution)/shard_map/all_to_all | solution.py:72
  158.2 146.2 %all-gather.8.cloned.1.call-start = ((), (), s32[]{:S(2)}) async-start(), calls=%async_computation.8 | async-start | bytes 2621440 | tf_op jit(solution)/shard_map/all_gather | solution.py:95
  193.5 4.3 %copy-start.7 = (bf16[256,1024]{1,0:T(8,128)(2,1)S(1)}, bf16[256,1024]{1,0:T(8,128)(2,1)}, u32[]{:S(2)}) copy-start(bf16[256,1024]{1,0:T(8,128)(2,1)} %param.9) | copy-start | bytes 1572868
  193.5 4.4 %copy-start.9 = (f32[256]{0:T(256)S(1)}, f32[256]{0:T(256)}, u32[]{:S(2)}) copy-start(f32[256]{0:T(256)} %param.12) | copy-start | bytes 3076
  242.8 2.4 copy-start.6
  273.8 1.6 copy-start.3
  277.0 60.6 %all-gather.6.cloned.1.call-start = ((), (), s32[]{:S(2)}) async-start(), calls=%async_computation.7 | async-start | bytes 2621440 | tf_op jit(solution)/shard_map/all_gather | solution.py:95
  277.7 59.9 %copy-start.12 = (bf16[1,1024,1024]{2,1,0:T(8,128)(2,1)S(1)}, bf16[1,1024,1024]{2,1,0:T(8,128)(2,1)}, u32[]{:S(2)}) copy-start(bf16[1,1024,1024]{2,1,0:T(8,128)(2,1)} %param.13) | copy-start | bytes 6291460
  344.1 36.4 %all-to-all-start.5 = ((bf16[32,32,1024]{2,1,0:T(8,128)(2,1)}), bf16[32,32,1024]{2,1,0:T(8,128)(2,1)}, u32[]{:S(2)}, u32[]{:S(2)}) async-start(bf16[32,32,1024]{2,1,0:T(8,128)(2,1)} %bitcast.20), calls=%async_computation.5 | async-start | bytes 4194304 | tf_op jit(solution)/shard_map/all_to_all | solution.py:101
  352.3 6.8 %copy-start.5 = (bf16[32,32,1024]{2,1,0:T(8,128)(2,1)S(1)}, bf16[32,32,1024]{2,1,0:T(8,128)(2,1)}, u32[]{:S(2)}) copy-start(bf16[32,32,1024]{2,1,0:T(8,128)(2,1)} %copy-done.4) | copy-start | bytes 6291460
  352.3 6.8 %copy-start.14 = (bf16[1024,1024]{1,0:T(8,128)(2,1)S(1)}, bf16[1024,1024]{1,0:T(8,128)(2,1)}, u32[]{:S(2)}) copy-start(bf16[1024,1024]{1,0:T(8,128)(2,1)} %all-gather.6.cloned.1.call-done) | copy-start | bytes 6291460
  359.1 4.4 %copy-start.13 = (bf16[1024,1024]{1,0:T(8,128)(2,1)S(1)}, bf16[1024,1024]{1,0:T(8,128)(2,1)}, u32[]{:S(2)}) copy-start(bf16[1024,1024]{1,0:T(8,128)(2,1)} %all-gather.8.cloned.1.call-done) | copy-start | bytes 6291460
  380.5 10.5 %copy-start.1 = (bf16[1,1024,1024]{2,1,0:T(8,128)(2,1)S(1)}, bf16[1,1024,1024]{2,1,0:T(8,128)(2,1)}, u32[]{:S(2)}) copy-start(bf16[1,1024,1024]{2,1,0:T(8,128)(2,1)} %param.15) | copy-start | bytes 6291460
Sparse Core Ops, SparseCore 0:
  117.7 27.3 all-gather.3
  277.1 27.2 all-gather.7
  306.7 30.8 all-gather.5

commit v3 on v1

--- a/solution.py
+++ b/solution.py
@@ -41,10 +41,14 @@
     gate_mat = w_gate[0]
     up_mat = w_up[0]
     down_mat = w_down[0]
+    ff = gate_mat.shape[1]
     ranks = slot_ranks(expert_ids.reshape(1, tok_rows, 2), experts).reshape(-1)
     slot_rows = expert_ids.reshape(-1) * capacity + ranks
-    spread = jnp.repeat(tokens, 2, axis=0)
-    outgoing = jnp.zeros((rows_all, quarter), jnp.bfloat16).at[slot_rows].set(spread)
+    select = (slot_rows[:, None] == jnp.arange(rows_all, dtype=slot_rows.dtype)[None, :]).astype(
+        jnp.bfloat16
+    )
+    per_token = jnp.sum(select.reshape(tok_rows, 2, rows_all), axis=1)
+    outgoing = contract(per_token, tokens, 0, 0).astype(jnp.bfloat16)
     arrived = lax.all_to_all(
         outgoing.reshape(experts, capacity, quarter),
         "expert",
@@ -52,12 +56,13 @@
         concat_axis=0,
         tiled=True,
     ).reshape(rows_all, quarter)
-    gate_pre, up_pre = lax.psum_scatter(
-        (contract(arrived, gate_mat, 1, 0), contract(arrived, up_mat, 1, 0)),
+    both = lax.psum_scatter(
+        jnp.concatenate([contract(arrived, gate_mat, 1, 0), contract(arrived, up_mat, 1, 0)], axis=1),
         "dp",
         scatter_dimension=0,
         tiled=True,
     )
+    gate_pre, up_pre = both[:, :ff], both[:, ff:]
     sigmoid_gate, hidden_part = activate(gate_pre, up_pre)
     hidden = lax.all_gather(hidden_part, "dp", axis=0, tiled=True)
     out_slots = (
@@ -66,7 +71,7 @@
     returned = lax.all_to_all(out_slots, "expert", split_axis=0, concat_axis=0, tiled=True).reshape(
         rows_all, quarter
     )
-    picked = returned[slot_rows].reshape(tok_rows, 2, quarter).astype(jnp.float32)
+    picked = contract(select, returned, 1, 0).reshape(tok_rows, 2, quarter)
     combined = jnp.sum(gate_weights[:, :, None] * picked, axis=1)
     mixed = combined.astype(jnp.bfloat16)
     row_grad = level_weights[:, None] * (combined - targets.astype(jnp.float32))
@@ -75,7 +80,7 @@
         .astype(jnp.bfloat16)
         .reshape(2 * tok_rows, quarter)
     )
-    grad_out = jnp.zeros((rows_all, quarter), jnp.bfloat16).at[slot_rows].set(slot_grad)
+    grad_out = contract(select, slot_grad, 0, 0).astype(jnp.bfloat16)
     grad_slots = lax.all_to_all(
         grad_out.reshape(experts, capacity, quarter),
         "expert",
@@ -87,8 +92,13 @@
     hidden_grad = lax.psum_scatter(
         contract(grad_slots, down_mat, 1, 1), "dp", scatter_dimension=0, tiled=True
     )
-    gate_part, up_part = derivatives(hidden_grad, gate_pre, up_pre, sigmoid_gate)
-    gate_delta, up_delta = lax.all_gather((gate_part, up_part), "dp", axis=0, tiled=True)
+    deltas = lax.all_gather(
+        jnp.concatenate(derivatives(hidden_grad, gate_pre, up_pre, sigmoid_gate), axis=1),
+        "dp",
+        axis=0,
+        tiled=True,
+    )
+    gate_delta, up_delta = deltas[:, :ff], deltas[:, ff:]
     input_slots = (contract(gate_delta, gate_mat, 1, 1) + contract(up_delta, up_mat, 1, 1)).astype(
         jnp.bfloat16
     )
@@ -101,9 +111,7 @@
         concat_axis=0,
         tiled=True,
     ).reshape(rows_all, quarter)
-    token_grad = jnp.sum(
-        input_back[slot_rows].reshape(tok_rows, 2, quarter).astype(jnp.float32), axis=1
-    ).astype(jnp.bfloat16)
+    token_grad = contract(per_token, input_back, 1, 0).astype(jnp.bfloat16)
     return (mixed, token_grad, gate_grad[None], up_grad[None], down_grad[None])
 
 

time: 473 us -> 418 us (0.88); the launches traced: 464 us -> 418 us
  local copies, waits for them, and re-layouts: 30.8 us -> 9.17 us
  waiting for transfers between devices: 260 us -> 247 us
  other arithmetic: 22.8 us -> 12.8 us
    gather x2 -> x0, local copies, waits for them, and re-layouts: 9.33 us -> none  [the longest x1 4.74 us: shards(): input_back[slot_rows].reshape(tok_rows, 2, quarter).astype(jnp.float32)]
    reduce_scatter x2 -> x1, waiting for transfers between devices: 88.6 us -> 79.3 us  [shards(): lax.psum_scatter(jnp.concatenate([contract(arrived, gate_mat, 1, 0), cont...]
    reduce_sum x2 -> x1, other arithmetic: 8.89 us -> 0.25 us  [shards(): per_token = jnp.sum(select.reshape(tok_rows, 2, rows_all), axis=1)]
    all_gather x2 -> x1, waiting for transfers between devices: 56.4 us -> 50 us  [shards(): lax.all_gather(jnp.concatenate(derivatives(hidden_grad, gate_pre, up_pre,...]
    scatter x1 -> x0, other arithmetic: 5.22 us -> none  [shards(): jnp.zeros((rows_all, quarter), jnp.bfloat16).at[slot_rows].set(slot_grad)]
    concatenate x0 -> x2, other arithmetic: none -> 5.1 us  [the longest x1 4.07 us: shards(): jnp.concatenate([contract(arrived, gate_mat, 1, 0), contract(arrived, up_...]
    scatter x1 -> x0, local copies, waits for them, and re-layouts: 4.79 us -> none  [shards(): jnp.zeros((rows_all, quarter), jnp.bfloat16).at[slot_rows].set(spread)]
    dot_general x9 -> x13, matrix products: 49.4 us -> 47.1 us  [contract(): lax.dot_general(left, right, (((left_dim,), (right_dim,)), ((), ())), pre...]
  transfers between devices with their start and end apart: 8 -> 6, of which waited for: 8 -> 6; matrix products, arithmetic and copies ran while one was open for 6% -> 4% of each run, Pallas kernels for 0% -> 0%
where the time goes in v3:
time: 418 us
  waiting for transfers between devices  247 us (59%)
  blocking collectives  68.4 us (16%)
  matrix products  47.1 us (11%)
  starting transfers between devices  18.7 us (4%)
  between operations  14 us (3%)
  other arithmetic  12.8 us (3%)
  local copies, waits for them, and re-layouts  9.17 us (2%)
    reduce_scatter x1, waiting for transfers between devices, shards(): lax.psum_scatter(jnp.concatenate([contract(arrived, gate_mat, 1, 0), cont...  79.3 us
    all_gather x1, waiting for transfers between devices, shards(): lax.all_gather(jnp.concatenate(derivatives(hidden_grad, gate_pre, up_pre,...  50 us
    dot_general x13, matrix products, contract(): lax.dot_general(left, right, (((left_dim,), (right_dim,)), ((), ())), pre...  47.1 us
    reduce_scatter x1, waiting for transfers between devices, shards(): lax.psum_scatter(contract(grad_slots, down_mat, 1, 1), 'dp', scatter_dime...  44.1 us
    all_to_all x1, blocking collectives, shards(): lax.all_to_all(outgoing.reshape(experts, capacity, quarter), 'expert', sp...  36.7 us
    all_gather x1, waiting for transfers between devices, shards(): hidden = lax.all_gather(hidden_part, 'dp', axis=0, tiled=True)  32.6 us
    all_to_all x1, blocking collectives, shards(): lax.all_to_all(grad_out.reshape(experts, capacity, quarter), 'expert', sp...  31.8 us
    all_to_all x1, waiting for transfers between devices, shards(): lax.all_to_all(out_slots, 'expert', split_axis=0, concat_axis=0, tiled=True)  27.9 us
  transfers between devices with their start and end apart: 6, of which 6 were waited for; matrix products, arithmetic and copies ran while one was open for 4% of the time, Pallas kernels for 0%

profile of v3, /device:TPU:1, one launch (start us, length us, event | category | flops | bytes accessed | tf_op | source)
XLA Modules:
  0.0 417.7 jit_solution(13039128333032118261)
XLA Ops:
  7.2 1.0 copy.34
  8.5 1.2 reduce-window.6
  12.2 36.7 %all_to_all.20 = bf16[32,32,1024]{2,1,0:T(8,128)(2,1)S(1)} all-to-all(bf16[32,32,1024]{2,1,0:T(8,128)(2,1)S(1)} %bitcast.67), channel_id=1, replica_groups=mesh['dp'=4,'expert'=32] {'expert'}, dimensions={0} | all-to-all | bytes 4194304 | tf_op jit(solution)/shard_map/all_to_all | solution.py:52
  48.9 2.4 fusion.6
  51.3 2.4 fusion.10
  53.7 4.1 pad_maximum_fusion
  57.8 79.3 %reduce-scatter.3.cloned.1.call-done = f32[256,2048]{0,1:T(8,128)} async-done(((f32[1024,2048]{0,1:T(8,128)}), f32[256,2048]{0,1:T(8,128)}) %reduce-scatter.3.cloned.1.call-update) | async-done | bytes 2097168 | tf_op jit(solution)/shard_map/reduce_scatter | solution.py:59
  137.2 2.6 multiply_convert_fusion.4
  139.8 32.6 %all-gather.3.cloned.1.call-done = bf16[1024,1024]{0,1:T(8,128)(2,1)} async-done(((bf16[256,1024]{0,1:T(8,128)(2,1)}), bf16[1024,1024]{0,1:T(8,128)(2,1)}) %all-gather.3.cloned.1.call-update) | async-done | bytes 2097168 | tf_op jit(solution)/shard_map/all_gather | solution.py:67
  172.4 5.3 %fusion.18 = bf16[1024,1024]{1,0:T(8,128)(2,1)} fusion(bf16[1024,1024]{0,1:T(8,128)(2,1)} %all-gather.3.cloned.1.call-done, bf16[1,1024,1024]{2,1,0:T(8,128)(2,1)S(1)} %copy-done), kind=kOutput, calls=%fused_computation.27 | convolution fusion | flops 2148532224 | bytes 6291456 | tf_op jit(solution)/shard_map/dot_general | solution.py:17
  177.7 9.1 %all-to-all-start.1 = ((bf16[32,32,1024]{2,1,0:T(8,128)(2,1)}), bf16[32,32,1024]{2,1,0:T(8,128)(2,1)}, u32[]{:S(2)}, u32[]{:S(2)}) async-start(bf16[32,32,1024]{2,1,0:T(8,128)(2,1)} %bitcast.74), calls=%async_computation.2 | async-start | bytes 4194304 | tf_op jit(solution)/shard_map/all_to_all | solution.py:71
  187.4 27.9 %all-to-all-done.1 = bf16[32,32,1024]{2,1,0:T(8,128)(2,1)} async-done(((bf16[32,32,1024]{2,1,0:T(8,128)(2,1)}), bf16[32,32,1024]{2,1,0:T(8,128)(2,1)}, u32[]{:S(2)}, u32[]{:S(2)}) %all-to-all-start.1) | async-done | bytes 2097184 | tf_op jit(solution)/shard_map/all_to_all | solution.py:71
  215.2 3.1 multiply_reduce_fusion
  218.3 1.0 subtract_multiply_fusion
  219.3 2.0 mul.89
  221.4 3.6 mul.90
  225.0 3.0 fusion.17
  228.0 31.8 %all_to_all.21 = bf16[32,32,1024]{2,1,0:T(8,128)(2,1)S(1)} all-to-all(bf16[32,32,1024]{2,1,0:T(8,128)(2,1)S(1)} %bitcast.76), channel_id=1, replica_groups=mesh['dp'=4,'expert'=32] {'expert'}, dimensions={0} | all-to-all | bytes 4194304 | tf_op jit(solution)/shard_map/all_to_all | solution.py:84
  259.8 1.3 copy-done.5
  261.1 4.4 %fusion = f32[1024,1024]{0,1:T(8,128)} fusion(bf16[1024,1024]{1,0:T(8,128)(2,1)S(1)} %bitcast.72, bf16[1,1024,1024]{2,1,0:T(8,128)(2,1)S(1)} %copy-done), kind=kOutput, calls=%fused_computation.5 | convolution fusion | flops 2147483648 | bytes 8388608 | tf_op jit(solution)/shard_map/dot_general | solution.py:17
  265.8 44.1 %reduce-scatter.5.cloned.1.call-done = f32[256,1024]{0,1:T(8,128)} async-done(((f32[1024,1024]{0,1:T(8,128)}), f32[256,1024]{0,1:T(8,128)}) %reduce-scatter.5.cloned.1.call-update) | async-done | bytes 1048592 | tf_op jit(solution)/shard_map/reduce_scatter | solution.py:92
  309.9 1.7 multiply_convert_fusion.3
  311.6 1.0 pad_maximum_fusion.1
  312.6 50.0 %all-gather.5.cloned.1.call-done = bf16[1024,2048]{0,1:T(8,128)(2,1)} async-done(((bf16[256,2048]{0,1:T(8,128)(2,1)}), bf16[1024,2048]{0,1:T(8,128)(2,1)}) %all-gather.5.cloned.1.call-update) | async-done | bytes 4194320 | tf_op jit(solution)/shard_map/all_gather | solution.py:95
  362.6 4.1 fusion.4
  366.8 3.8 add_convert_fusion
  370.6 9.1 %all-to-all-start.3 = ((bf16[32,32,1024]{2,1,0:T(8,128)(2,1)}), bf16[32,32,1024]{2,1,0:T(8,128)(2,1)}, u32[]{:S(2)}, u32[]{:S(2)}) async-start(bf16[32,32,1024]{2,1,0:T(8,128)(2,1)} %bitcast.75), calls=%async_computation.5 | async-start | bytes 4194304 | tf_op jit(solution)/shard_map/all_to_all | solution.py:107
  379.7 6.1 %convolution_bitcast_fusion = f32[1,1024,1024]{2,1,0:T(8,128)} fusion(bf16[1024,1024]{0,1:T(8,128)(2,1)} %all-gather.3.cloned.1.call-done, bf16[1024,1024]{1,0:T(8,128)(2,1)S(1)} %bitcast.73), kind=kOutput, calls=%fused_computation.2 | convolution fusion | flops 2147483648 | bytes 8388608 | tf_op jit(solution)/shard_map/dot_general | solution.py:17
  385.8 4.4 %convolution_bitcast_fusion.2 = f32[1,1024,1024]{2,1,0:T(8,128)} fusion(bf16[1024,1024]{1,0:T(8,128)(2,1)S(1)} %bitcast.70, bf16[1024,2048]{0,1:T(8,128)(2,1)S(1)} %copy-done.12), kind=kOutput, calls=%fused_computation.4 | convolution fusion | flops 2147483648 | bytes 8388608 | tf_op jit(solution)/shard_map/dot_general | solution.py:17
  390.2 4.4 %convolution_bitcast_fusion.1 = f32[1,1024,1024]{2,1,0:T(8,128)} fusion(bf16[1024,1024]{1,0:T(8,128)(2,1)S(1)} %bitcast.71, bf16[1024,2048]{0,1:T(8,128)(2,1)S(1)} %copy-done.12), kind=kOutput, calls=%fused_computation.3 | convolution fusion | flops 2147483648 | bytes 8388608 | tf_op jit(solution)/shard_map/dot_general | solution.py:17
  394.6 13.4 %all-to-all-done.3 = bf16[32,32,1024]{2,1,0:T(8,128)(2,1)} async-done(((bf16[32,32,1024]{2,1,0:T(8,128)(2,1)}), bf16[32,32,1024]{2,1,0:T(8,128)(2,1)}, u32[]{:S(2)}, u32[]{:S(2)}) %all-to-all-start.3) | async-done | bytes 2097184 | tf_op jit(solution)/shard_map/all_to_all | solution.py:107
  408.1 3.1 convolution_convert_fusion.1
  (59 shorter events, 3.7 us)
Async XLA Ops:
  7.2 165.3 %copy-start = (bf16[1,1024,1024]{2,1,0:T(8,128)(2,1)S(1)}, bf16[1,1024,1024]{2,1,0:T(8,128)(2,1)}, u32[]{:S(2)}) copy-start(bf16[1,1024,1024]{2,1,0:T(8,128)(2,1)} %param.15) | copy-start | bytes 6291460
  7.2 4.3 %copy-start.7 = (bf16[256,1024]{1,0:T(8,128)(2,1)S(1)}, bf16[256,1024]{1,0:T(8,128)(2,1)}, u32[]{:S(2)}) copy-start(bf16[256,1024]{1,0:T(8,128)(2,1)} %param.8) | copy-start | bytes 1572868
  7.2 130.0 %reduce-scatter.3.cloned.1.call-start = ((), (), s32[]{:S(2)}) async-start(), calls=%async_computation.6 | async-start | bytes 10485760 | tf_op jit(solution)/shard_map/reduce_scatter | solution.py:59
  12.2 36.7 %copy-start.13 = (bf16[1,1024,1024]{2,1,0:T(8,128)(2,1)S(1)}, bf16[1,1024,1024]{2,1,0:T(8,128)(2,1)}, u32[]{:S(2)}) copy-start(bf16[1,1024,1024]{2,1,0:T(8,128)(2,1)} %param.14) | copy-start | bytes 6291460
  48.9 2.4 copy-start.3
  48.9 2.4 copy-start.15
  57.8 114.7 %all-gather.3.cloned.1.call-start = ((), (), s32[]{:S(2)}) async-start(), calls=%async_computation.7 | async-start | bytes 2621440 | tf_op jit(solution)/shard_map/all_gather | solution.py:67
  177.7 9.3 %copy-start.9 = (f32[256,2]{0,1:T(2,128)S(1)}, f32[256,2]{0,1:T(2,128)}, u32[]{:S(2)}) copy-start(f32[256,2]{0,1:T(2,128)} %param.11) | copy-start | bytes 6148
  177.7 37.5 %all-to-all-start.1 = ((bf16[32,32,1024]{2,1,0:T(8,128)(2,1)}), bf16[32,32,1024]{2,1,0:T(8,128)(2,1)}, u32[]{:S(2)}, u32[]{:S(2)}) async-start(bf16[32,32,1024]{2,1,0:T(8,128)(2,1)} %bitcast.74), calls=%async_computation.2 | async-start | bytes 4194304 | tf_op jit(solution)/shard_map/all_to_all | solution.py:71
  186.8 123.0 %reduce-scatter.5.cloned.1.call-start = ((), (), s32[]{:S(2)}) async-start(), calls=%async_computation.8 | async-start | bytes 5242880 | tf_op jit(solution)/shard_map/reduce_scatter | solution.py:92
  215.2 3.1 copy-start.8
  215.2 3.1 copy-start.10
  259.8 1.3 copy-start.5
  265.5 44.4 %copy-start.2 = (f32[256,2048]{0,1:T(8,128)S(1)}, f32[256,2048]{0,1:T(8,128)}, u32[]{:S(2)}) copy-start(f32[256,2048]{0,1:T(8,128)} %reduce-scatter.3.cloned.1.call-done) | copy-start | bytes 6291460
  265.5 97.1 %all-gather.5.cloned.1.call-start = ((), (), s32[]{:S(2)}) async-start(), calls=%async_computation.9 | async-start | bytes 5242880 | tf_op jit(solution)/shard_map/all_gather | solution.py:95
  311.5 51.1 %copy-start.14 = (bf16[1,1024,1024]{2,1,0:T(8,128)(2,1)S(1)}, bf16[1,1024,1024]{2,1,0:T(8,128)(2,1)}, u32[]{:S(2)}) copy-start(bf16[1,1024,1024]{2,1,0:T(8,128)(2,1)} %param.14) | copy-start | bytes 6291460
  362.6 4.1 copy-start.11
  362.6 4.1 copy-start.16
  370.6 9.1 %copy-start.6 = (bf16[32,32,1024]{2,1,0:T(8,128)(2,1)S(1)}, bf16[32,32,1024]{2,1,0:T(8,128)(2,1)}, u32[]{:S(2)}) copy-start(bf16[32,32,1024]{2,1,0:T(8,128)(2,1)} %copy-done.5) | copy-start | bytes 6291460
  370.6 37.5 %all-to-all-start.3 = ((bf16[32,32,1024]{2,1,0:T(8,128)(2,1)}), bf16[32,32,1024]{2,1,0:T(8,128)(2,1)}, u32[]{:S(2)}, u32[]{:S(2)}) async-start(bf16[32,32,1024]{2,1,0:T(8,128)(2,1)} %bitcast.75), calls=%async_computation.5 | async-start | bytes 4194304 | tf_op jit(solution)/shard_map/all_to_all | solution.py:107
  379.7 6.1 %copy-start.4 = (bf16[32,32,1024]{2,1,0:T(8,128)(2,1)S(1)}, bf16[32,32,1024]{2,1,0:T(8,128)(2,1)}, u32[]{:S(2)}) copy-start(bf16[32,32,1024]{2,1,0:T(8,128)(2,1)} %copy-done.3) | copy-start | bytes 6291460
  379.7 6.1 %copy-start.12 = (bf16[1024,2048]{0,1:T(8,128)(2,1)S(1)}, bf16[1024,2048]{0,1:T(8,128)(2,1)}, u32[]{:S(2)}) copy-start(bf16[1024,2048]{0,1:T(8,128)(2,1)} %all-gather.5.cloned.1.call-done) | copy-start | bytes 12582916
  390.2 20.9 %copy-start.1 = (bf16[1,1024,1024]{2,1,0:T(8,128)(2,1)S(1)}, bf16[1,1024,1024]{2,1,0:T(8,128)(2,1)}, u32[]{:S(2)}) copy-start(bf16[1,1024,1024]{2,1,0:T(8,128)(2,1)} %param.15) | copy-start | bytes 6291460
Sparse Core Ops, SparseCore 0:
  57.9 79.2 reduce-scatter.2
  139.9 32.4 all-gather.2
  265.6 44.1 reduce-scatter.4
  312.7 49.8 all-gather.4

commit v4 on v3

--- a/solution.py
+++ b/solution.py
@@ -57,7 +57,7 @@
         tiled=True,
     ).reshape(rows_all, quarter)
     both = lax.psum_scatter(
-        jnp.concatenate([contract(arrived, gate_mat, 1, 0), contract(arrived, up_mat, 1, 0)], axis=1),
+        contract(arrived, jnp.concatenate([gate_mat, up_mat], axis=1), 1, 0),
         "dp",
         scatter_dimension=0,
         tiled=True,
@@ -71,16 +71,17 @@
     returned = lax.all_to_all(out_slots, "expert", split_axis=0, concat_axis=0, tiled=True).reshape(
         rows_all, quarter
     )
-    picked = contract(select, returned, 1, 0).reshape(tok_rows, 2, quarter)
-    combined = jnp.sum(gate_weights[:, :, None] * picked, axis=1)
+    pair = select.reshape(tok_rows, 2, rows_all)
+    first, second = pair[:, 0], pair[:, 1]
+    combined = gate_weights[:, 0:1] * contract(first, returned, 1, 0) + gate_weights[
+        :, 1:2
+    ] * contract(second, returned, 1, 0)
     mixed = combined.astype(jnp.bfloat16)
     row_grad = level_weights[:, None] * (combined - targets.astype(jnp.float32))
-    slot_grad = (
-        (gate_weights[:, :, None] * row_grad[:, None, :])
-        .astype(jnp.bfloat16)
-        .reshape(2 * tok_rows, quarter)
-    )
-    grad_out = contract(select, slot_grad, 0, 0).astype(jnp.bfloat16)
+    grad_out = (
+        contract(first, (gate_weights[:, 0:1] * row_grad).astype(jnp.bfloat16), 0, 0)
+        + contract(second, (gate_weights[:, 1:2] * row_grad).astype(jnp.bfloat16), 0, 0)
+    ).astype(jnp.bfloat16)
     grad_slots = lax.all_to_all(
         grad_out.reshape(experts, capacity, quarter),
         "expert",

time: 418 us -> 405 us (0.969)
  local copies, waits for them, and re-layouts: 9.17 us -> 4.53 us
  other arithmetic: 12.8 us -> 8.26 us
    mul x3 -> x0, local copies, waits for them, and re-layouts: 5.83 us -> none  [the longest x2 5.68 us: shards(): gate_weights[:, :, None] * row_grad[:, None, :]]
    dot_general x13 -> x14, matrix products: 47.1 us -> 50.8 us  [contract(): lax.dot_general(left, right, (((left_dim,), (right_dim,)), ((), ())), pre...]
where the time goes in v4:
time: 405 us
  waiting for transfers between devices  243 us (60%)
  blocking collectives  68.5 us (17%)
  matrix products  50.8 us (13%)
  starting transfers between devices  15.9 us (4%)
  between operations  14 us (3%)
  other arithmetic  8.26 us (2%)
  local copies, waits for them, and re-layouts  4.53 us (1%)
    reduce_scatter x1, waiting for transfers between devices, shards(): lax.psum_scatter(contract(arrived, jnp.concatenate([gate_mat, up_mat], ax...  79.3 us
    dot_general x14, matrix products, contract(): lax.dot_general(left, right, (((left_dim,), (right_dim,)), ((), ())), pre...  50.8 us
    all_gather x1, waiting for transfers between devices, shards(): lax.all_gather(jnp.concatenate(derivatives(hidden_grad, gate_pre, up_pre,...  48 us
    reduce_scatter x1, waiting for transfers between devices, shards(): lax.psum_scatter(contract(grad_slots, down_mat, 1, 1), 'dp', scatter_dime...  43.4 us
    all_to_all x1, blocking collectives, shards(): lax.all_to_all(outgoing.reshape(experts, capacity, quarter), 'expert', sp...  36.8 us
    all_to_all x1, blocking collectives, shards(): lax.all_to_all(grad_out.reshape(experts, capacity, quarter), 'expert', sp...  31.8 us
    all_gather x1, waiting for transfers between devices, shards(): hidden = lax.all_gather(hidden_part, 'dp', axis=0, tiled=True)  30.6 us
    all_to_all x1, waiting for transfers between devices, shards(): lax.all_to_all(out_slots, 'expert', split_axis=0, concat_axis=0, tiled=True)  28 us
  transfers between devices with their start and end apart: 6, of which 6 were waited for; matrix products, arithmetic and copies ran while one was open for 4% of the time, Pallas kernels for 0%

profile of v4, /device:TPU:1, one launch (start us, length us, event | category | flops | bytes accessed | tf_op | source)
XLA Modules:
  0.0 404.8 jit_solution(6384836964172534342)
XLA Ops:
  7.2 1.0 copy.21
  8.5 1.2 reduce-window.6
  10.5 0.7 multiply_add_fusion
  11.5 0.7 convolution_convert_fusion
  12.2 36.8 %all_to_all.20 = bf16[32,32,1024]{2,1,0:T(8,128)(2,1)S(1)} all-to-all(bf16[32,32,1024]{2,1,0:T(8,128)(2,1)S(1)} %bitcast.67), channel_id=1, replica_groups=mesh['dp'=4,'expert'=32] {'expert'}, dimensions={0} | all-to-all | bytes 4194304 | tf_op jit(solution)/shard_map/all_to_all | solution.py:52
  49.0 1.3 copy-done.4
  50.4 6.8 %fusion = f32[1024,2048]{1,0:T(8,128)} fusion(bf16[1024,1024]{1,0:T(8,128)(2,1)S(1)} %bitcast.68, bf16[1024,1024]{1,0:T(8,128)(2,1)S(1)} %bitcast.84, bf16[1024,1024]{1,0:T(8,128)(2,1)S(1)} %bitcast.83), kind=kOutput, calls=%fused_computation | convolution fusion | flops 4303355904 | bytes 14680064 | tf_op jit(solution)/shard_map/dot_general | solution.py:17
  57.3 79.3 %reduce-scatter.3.cloned.1.call-done = f32[256,2048]{1,0:T(8,128)} async-done(((f32[1024,2048]{1,0:T(8,128)}), f32[256,2048]{1,0:T(8,128)}) %reduce-scatter.3.cloned.1.call-update) | async-done | bytes 2097168 | tf_op jit(solution)/shard_map/reduce_scatter | solution.py:59
  136.6 2.6 multiply_convert_fusion.4
  139.3 30.6 %all-gather.3.cloned.1.call-done = bf16[1024,1024]{1,0:T(8,128)(2,1)} async-done(((bf16[256,1024]{1,0:T(8,128)(2,1)}), bf16[1024,1024]{1,0:T(8,128)(2,1)}) %all-gather.3.cloned.1.call-update) | async-done | bytes 2097168 | tf_op jit(solution)/shard_map/all_gather | solution.py:67
  169.9 5.2 %fusion.8 = bf16[1024,1024]{1,0:T(8,128)(2,1)} fusion(bf16[1024,1024]{1,0:T(8,128)(2,1)} %all-gather.3.cloned.1.call-done, bf16[1,1024,1024]{2,1,0:T(8,128)(2,1)S(1)} %copy-done), kind=kOutput, calls=%fused_computation.14 | convolution fusion | flops 2148532224 | bytes 6291456 | tf_op jit(solution)/shard_map/dot_general | solution.py:17
  175.1 7.9 %all-to-all-start.1 = ((bf16[32,32,1024]{2,1,0:T(8,128)(2,1)}), bf16[32,32,1024]{2,1,0:T(8,128)(2,1)}, u32[]{:S(2)}, u32[]{:S(2)}) async-start(bf16[32,32,1024]{2,1,0:T(8,128)(2,1)} %bitcast.74), calls=%async_computation.2 | async-start | bytes 4194304 | tf_op jit(solution)/shard_map/all_to_all | solution.py:71
  183.5 28.0 %all-to-all-done.1 = bf16[32,32,1024]{2,1,0:T(8,128)(2,1)} async-done(((bf16[32,32,1024]{2,1,0:T(8,128)(2,1)}), bf16[32,32,1024]{2,1,0:T(8,128)(2,1)}, u32[]{:S(2)}, u32[]{:S(2)}) %all-to-all-start.1) | async-done | bytes 2097184 | tf_op jit(solution)/shard_map/all_to_all | solution.py:71
  211.4 2.4 convolution_multiply_fusion.1
  213.8 3.3 fusion.27
  217.1 0.9 fusion.17
  218.0 0.9 add_convert_fusion.1
  219.0 31.8 %all_to_all.21 = bf16[32,32,1024]{2,1,0:T(8,128)(2,1)S(1)} all-to-all(bf16[32,32,1024]{2,1,0:T(8,128)(2,1)S(1)} %bitcast.66), channel_id=1, replica_groups=mesh['dp'=4,'expert'=32] {'expert'}, dimensions={0} | all-to-all | bytes 4194304 | tf_op jit(solution)/shard_map/all_to_all | solution.py:85
  250.8 1.3 copy-done.6
  252.1 4.4 %fusion.4 = f32[1024,1024]{1,0:T(8,128)} fusion(bf16[1024,1024]{1,0:T(8,128)(2,1)S(1)} %bitcast.71, bf16[1,1024,1024]{2,1,0:T(8,128)(2,1)S(1)} %copy-done), kind=kOutput, calls=%fused_computation.9 | convolution fusion | flops 2147483648 | bytes 8388608 | tf_op jit(solution)/shard_map/dot_general | solution.py:17
  256.6 43.4 %reduce-scatter.5.cloned.1.call-done = f32[256,1024]{1,0:T(8,128)} async-done(((f32[1024,1024]{1,0:T(8,128)}), f32[256,1024]{1,0:T(8,128)}) %reduce-scatter.5.cloned.1.call-update) | async-done | bytes 1048592 | tf_op jit(solution)/shard_map/reduce_scatter | solution.py:93
  300.0 1.8 multiply_convert_fusion.1
  301.8 1.1 pad_maximum_fusion
  302.9 48.0 %all-gather.5.cloned.1.call-done = bf16[1024,2048]{1,0:T(8,128)(2,1)} async-done(((bf16[256,2048]{1,0:T(8,128)(2,1)}), bf16[1024,2048]{1,0:T(8,128)(2,1)}) %all-gather.5.cloned.1.call-update) | async-done | bytes 4194320 | tf_op jit(solution)/shard_map/all_gather | solution.py:96
  351.0 4.1 %fusion.14 = f32[1024,1024]{1,0:T(8,128)S(1)} fusion(bf16[1024,2048]{1,0:T(8,128)(2,1)} %all-gather.5.cloned.1.call-done, bf16[1,1024,1024]{2,1,0:T(8,128)(2,1)S(1)} %copy-done.14), kind=kOutput, calls=%fused_computation.19 | convolution fusion | flops 2147483648 | bytes 8388608 | tf_op jit(solution)/shard_map/dot_general | solution.py:17
  355.1 3.8 add_convert_fusion
  358.9 7.9 %all-to-all-start.3 = ((bf16[32,32,1024]{2,1,0:T(8,128)(2,1)}), bf16[32,32,1024]{2,1,0:T(8,128)(2,1)}, u32[]{:S(2)}, u32[]{:S(2)}) async-start(bf16[32,32,1024]{2,1,0:T(8,128)(2,1)} %bitcast.73), calls=%async_computation.5 | async-start | bytes 4194304 | tf_op jit(solution)/shard_map/all_to_all | solution.py:108
  366.8 6.1 %convolution_bitcast_fusion = f32[1,1024,1024]{2,1,0:T(8,128)} fusion(bf16[1024,1024]{1,0:T(8,128)(2,1)} %all-gather.3.cloned.1.call-done, bf16[1024,1024]{1,0:T(8,128)(2,1)S(1)} %bitcast.72), kind=kOutput, calls=%fused_computation.6 | convolution fusion | flops 2147483648 | bytes 8388608 | tf_op jit(solution)/shard_map/dot_general | solution.py:17
  372.9 4.4 %convolution_bitcast_fusion.2 = f32[1,1024,1024]{2,1,0:T(8,128)} fusion(bf16[1024,1024]{1,0:T(8,128)(2,1)S(1)} %bitcast.69, bf16[1024,2048]{1,0:T(8,128)(2,1)S(1)} %copy-done.12), kind=kOutput, calls=%fused_computation.8 | convolution fusion | flops 2147483648 | bytes 8388608 | tf_op jit(solution)/shard_map/dot_general | solution.py:17
  377.4 4.4 %convolution_bitcast_fusion.1 = f32[1,1024,1024]{2,1,0:T(8,128)} fusion(bf16[1024,1024]{1,0:T(8,128)(2,1)S(1)} %bitcast.70, bf16[1024,2048]{1,0:T(8,128)(2,1)S(1)} %copy-done.12), kind=kOutput, calls=%fused_computation.7 | convolution fusion | flops 2147483648 | bytes 8388608 | tf_op jit(solution)/shard_map/dot_general | solution.py:17
  381.8 13.3 %all-to-all-done.3 = bf16[32,32,1024]{2,1,0:T(8,128)(2,1)} async-done(((bf16[32,32,1024]{2,1,0:T(8,128)(2,1)}), bf16[32,32,1024]{2,1,0:T(8,128)(2,1)}, u32[]{:S(2)}, u32[]{:S(2)}) %all-to-all-start.3) | async-done | bytes 2097184 | tf_op jit(solution)/shard_map/all_to_all | solution.py:108
  395.1 3.1 convolution_convert_fusion.1
  (55 shorter events, 2.0 us)
Async XLA Ops:
  7.2 162.7 %copy-start = (bf16[1,1024,1024]{2,1,0:T(8,128)(2,1)S(1)}, bf16[1,1024,1024]{2,1,0:T(8,128)(2,1)}, u32[]{:S(2)}) copy-start(bf16[1,1024,1024]{2,1,0:T(8,128)(2,1)} %param.15) | copy-start | bytes 6291460
  7.2 4.3 %copy-start.8 = (bf16[256,1024]{1,0:T(8,128)(2,1)S(1)}, bf16[256,1024]{1,0:T(8,128)(2,1)}, u32[]{:S(2)}) copy-start(bf16[256,1024]{1,0:T(8,128)(2,1)} %param.8) | copy-start | bytes 1572868
  7.2 129.4 %reduce-scatter.3.cloned.1.call-start = ((), (), s32[]{:S(2)}) async-start(), calls=%async_computation.6 | async-start | bytes 10485760 | tf_op jit(solution)/shard_map/reduce_scatter | solution.py:59
  12.2 38.1 %copy-start.13 = (bf16[1,1024,1024]{2,1,0:T(8,128)(2,1)S(1)}, bf16[1,1024,1024]{2,1,0:T(8,128)(2,1)}, u32[]{:S(2)}) copy-start(bf16[1,1024,1024]{2,1,0:T(8,128)(2,1)} %param.13) | copy-start | bytes 6291460
  12.2 38.1 %copy-start.15 = (bf16[1,1024,1024]{2,1,0:T(8,128)(2,1)S(1)}, bf16[1,1024,1024]{2,1,0:T(8,128)(2,1)}, u32[]{:S(2)}) copy-start(bf16[1,1024,1024]{2,1,0:T(8,128)(2,1)} %param.14) | copy-start | bytes 6291460
  49.0 1.3 copy-start.4
  57.2 112.7 %all-gather.3.cloned.1.call-start = ((), (), s32[]{:S(2)}) async-start(), calls=%async_computation.7 | async-start | bytes 2621440 | tf_op jit(solution)/shard_map/all_gather | solution.py:67
  175.1 7.9 %copy-start.10 = (f32[256,2]{0,1:T(2,128)S(1)}, f32[256,2]{0,1:T(2,128)}, u32[]{:S(2)}) copy-start(f32[256,2]{0,1:T(2,128)} %param.11) | copy-start | bytes 6148
  175.1 36.3 %all-to-all-start.1 = ((bf16[32,32,1024]{2,1,0:T(8,128)(2,1)}), bf16[32,32,1024]{2,1,0:T(8,128)(2,1)}, u32[]{:S(2)}, u32[]{:S(2)}) async-start(bf16[32,32,1024]{2,1,0:T(8,128)(2,1)} %bitcast.74), calls=%async_computation.2 | async-start | bytes 4194304 | tf_op jit(solution)/shard_map/all_to_all | solution.py:71
  183.0 116.9 %reduce-scatter.5.cloned.1.call-start = ((), (), s32[]{:S(2)}) async-start(), calls=%async_computation.8 | async-start | bytes 5242880 | tf_op jit(solution)/shard_map/reduce_scatter | solution.py:93
  213.8 3.3 copy-start.3
  213.8 3.3 copy-start.9
  250.8 1.3 copy-start.6
  256.5 43.4 %copy-start.2 = (f32[256,2048]{1,0:T(8,128)S(1)}, f32[256,2048]{1,0:T(8,128)}, u32[]{:S(2)}) copy-start(f32[256,2048]{1,0:T(8,128)} %reduce-scatter.3.cloned.1.call-done) | copy-start | bytes 6291460
  256.5 94.4 %all-gather.5.cloned.1.call-start = ((), (), s32[]{:S(2)}) async-start(), calls=%async_computation.9 | async-start | bytes 5242880 | tf_op jit(solution)/shard_map/all_gather | solution.py:96
  301.8 49.1 %copy-start.14 = (bf16[1,1024,1024]{2,1,0:T(8,128)(2,1)S(1)}, bf16[1,1024,1024]{2,1,0:T(8,128)(2,1)}, u32[]{:S(2)}) copy-start(bf16[1,1024,1024]{2,1,0:T(8,128)(2,1)} %param.13) | copy-start | bytes 6291460
  351.0 4.1 %copy-start.11 = (bf16[1024,2048]{1,0:T(8,128)(2,1)S(1)}, bf16[1024,2048]{1,0:T(8,128)(2,1)}, u32[]{:S(2)}) copy-start(bf16[1024,2048]{1,0:T(8,128)(2,1)} %all-gather.5.cloned.1.call-done) | copy-start | bytes 12582916
  351.0 4.1 %copy-start.16 = (bf16[1,1024,1024]{2,1,0:T(8,128)(2,1)S(1)}, bf16[1,1024,1024]{2,1,0:T(8,128)(2,1)}, u32[]{:S(2)}) copy-start(bf16[1,1024,1024]{2,1,0:T(8,128)(2,1)} %param.14) | copy-start | bytes 6291460
  358.9 7.9 %copy-start.7 = (bf16[32,32,1024]{2,1,0:T(8,128)(2,1)S(1)}, bf16[32,32,1024]{2,1,0:T(8,128)(2,1)}, u32[]{:S(2)}) copy-start(bf16[32,32,1024]{2,1,0:T(8,128)(2,1)} %copy-done.6) | copy-start | bytes 6291460
  358.9 36.3 %all-to-all-start.3 = ((bf16[32,32,1024]{2,1,0:T(8,128)(2,1)}), bf16[32,32,1024]{2,1,0:T(8,128)(2,1)}, u32[]{:S(2)}, u32[]{:S(2)}) async-start(bf16[32,32,1024]{2,1,0:T(8,128)(2,1)} %bitcast.73), calls=%async_computation.5 | async-start | bytes 4194304 | tf_op jit(solution)/shard_map/all_to_all | solution.py:108
  366.8 6.2 %copy-start.5 = (bf16[32,32,1024]{2,1,0:T(8,128)(2,1)S(1)}, bf16[32,32,1024]{2,1,0:T(8,128)(2,1)}, u32[]{:S(2)}) copy-start(bf16[32,32,1024]{2,1,0:T(8,128)(2,1)} %copy-done.4) | copy-start | bytes 6291460
  366.8 6.2 %copy-start.12 = (bf16[1024,2048]{1,0:T(8,128)(2,1)S(1)}, bf16[1024,2048]{1,0:T(8,128)(2,1)}, u32[]{:S(2)}) copy-start(bf16[1024,2048]{1,0:T(8,128)(2,1)} %all-gather.5.cloned.1.call-done) | copy-start | bytes 12582916
  377.4 20.9 %copy-start.1 = (bf16[1,1024,1024]{2,1,0:T(8,128)(2,1)S(1)}, bf16[1,1024,1024]{2,1,0:T(8,128)(2,1)}, u32[]{:S(2)}) copy-start(bf16[1,1024,1024]{2,1,0:T(8,128)(2,1)} %param.15) | copy-start | bytes 6291460
Sparse Core Ops, SparseCore 0:
  57.3 79.2 reduce-scatter.2
  139.4 30.4 all-gather.2
  256.7 43.2 reduce-scatter.4
  303.0 47.8 all-gather.4

commit v5 on v4

--- a/solution.py
+++ b/solution.py
@@ -42,6 +42,7 @@
     up_mat = w_up[0]
     down_mat = w_down[0]
     ff = gate_mat.shape[1]
+    joined = jnp.concatenate([gate_mat, up_mat], axis=1)
     ranks = slot_ranks(expert_ids.reshape(1, tok_rows, 2), experts).reshape(-1)
     slot_rows = expert_ids.reshape(-1) * capacity + ranks
     select = (slot_rows[:, None] == jnp.arange(rows_all, dtype=slot_rows.dtype)[None, :]).astype(
@@ -57,7 +58,7 @@
         tiled=True,
     ).reshape(rows_all, quarter)
     both = lax.psum_scatter(
-        contract(arrived, jnp.concatenate([gate_mat, up_mat], axis=1), 1, 0),
+        contract(arrived, joined, 1, 0),
         "dp",
         scatter_dimension=0,
         tiled=True,
@@ -100,9 +101,7 @@
         tiled=True,
     )
     gate_delta, up_delta = deltas[:, :ff], deltas[:, ff:]
-    input_slots = (contract(gate_delta, gate_mat, 1, 1) + contract(up_delta, up_mat, 1, 1)).astype(
-        jnp.bfloat16
-    )
+    input_slots = contract(deltas, joined, 1, 1).astype(jnp.bfloat16)
     gate_grad = contract(arrived, gate_delta, 0, 0)
     up_grad = contract(arrived, up_delta, 0, 0)
     input_back = lax.all_to_all(

time: 405 us -> 406 us (level)
    dot_general x14 -> x13, matrix products: 50.8 us -> 51.7 us  [contract(): lax.dot_general(left, right, (((left_dim,), (right_dim,)), ((), ())), pre...]
where the time goes in v5:
time: 406 us
  waiting for transfers between devices  243 us (60%)
  blocking collectives  68.5 us (17%)
  matrix products  51.7 us (13%)
  starting transfers between devices  15.9 us (4%)
  between operations  14 us (3%)
  other arithmetic  8.25 us (2%)
  local copies, waits for them, and re-layouts  4.53 us (1%)
    reduce_scatter x1, waiting for transfers between devices, shards(): lax.psum_scatter(contract(arrived, joined, 1, 0), 'dp', scatter_dimension...  79.3 us
    dot_general x13, matrix products, contract(): lax.dot_general(left, right, (((left_dim,), (right_dim,)), ((), ())), pre...  51.7 us
    all_gather x1, waiting for transfers between devices, shards(): lax.all_gather(jnp.concatenate(derivatives(hidden_grad, gate_pre, up_pre,...  48 us
    reduce_scatter x1, waiting for transfers between devices, shards(): lax.psum_scatter(contract(grad_slots, down_mat, 1, 1), 'dp', scatter_dime...  43.4 us
    all_to_all x1, blocking collectives, shards(): lax.all_to_all(outgoing.reshape(experts, capacity, quarter), 'expert', sp...  36.8 us
    all_to_all x1, blocking collectives, shards(): lax.all_to_all(grad_out.reshape(experts, capacity, quarter), 'expert', sp...  31.8 us
    all_gather x1, waiting for transfers between devices, shards(): hidden = lax.all_gather(hidden_part, 'dp', axis=0, tiled=True)  30.6 us
    all_to_all x1, waiting for transfers between devices, shards(): lax.all_to_all(out_slots, 'expert', split_axis=0, concat_axis=0, tiled=True)  28 us
  transfers between devices with their start and end apart: 6, of which 6 were waited for; matrix products, arithmetic and copies ran while one was open for 4% of the time, Pallas kernels for 0%

profile of v5, /device:TPU:1, one launch (start us, length us, event | category | flops | bytes accessed | tf_op | source)
XLA Modules:
  0.0 405.6 jit_solution(11677237460309613332)
XLA Ops:
  7.2 1.0 copy.21
  8.5 1.2 reduce-window.6
  10.5 0.7 multiply_add_fusion
  11.5 0.7 convolution_convert_fusion
  12.2 36.8 %all_to_all.20 = bf16[32,32,1024]{2,1,0:T(8,128)(2,1)S(1)} all-to-all(bf16[32,32,1024]{2,1,0:T(8,128)(2,1)S(1)} %bitcast.64), channel_id=1, replica_groups=mesh['dp'=4,'expert'=32] {'expert'}, dimensions={0} | all-to-all | bytes 4194304 | tf_op jit(solution)/shard_map/all_to_all | solution.py:53
  49.0 1.3 copy-done.4
  50.4 6.8 %fusion.1 = f32[1024,2048]{1,0:T(8,128)} fusion(bf16[1024,1024]{1,0:T(8,128)(2,1)S(1)} %bitcast.65, bf16[1024,1024]{1,0:T(8,128)(2,1)S(1)} %bitcast.80, bf16[1024,1024]{1,0:T(8,128)(2,1)S(1)} %bitcast.83), kind=kOutput, calls=%fused_computation.3 | convolution fusion | flops 4303355904 | bytes 14680064 | tf_op jit(solution)/shard_map/dot_general | solution.py:17
  57.3 79.3 %reduce-scatter.3.cloned.1.call-done = f32[256,2048]{1,0:T(8,128)} async-done(((f32[1024,2048]{1,0:T(8,128)}), f32[256,2048]{1,0:T(8,128)}) %reduce-scatter.3.cloned.1.call-update) | async-done | bytes 2097168 | tf_op jit(solution)/shard_map/reduce_scatter | solution.py:60
  136.6 2.6 multiply_convert_fusion.4
  139.3 30.6 %all-gather.3.cloned.1.call-done = bf16[1024,1024]{1,0:T(8,128)(2,1)} async-done(((bf16[256,1024]{1,0:T(8,128)(2,1)}), bf16[1024,1024]{1,0:T(8,128)(2,1)}) %all-gather.3.cloned.1.call-update) | async-done | bytes 2097168 | tf_op jit(solution)/shard_map/all_gather | solution.py:68
  169.9 5.2 %fusion.8 = bf16[1024,1024]{1,0:T(8,128)(2,1)} fusion(bf16[1024,1024]{1,0:T(8,128)(2,1)} %all-gather.3.cloned.1.call-done, bf16[1,1024,1024]{2,1,0:T(8,128)(2,1)S(1)} %copy-done), kind=kOutput, calls=%fused_computation.14 | convolution fusion | flops 2148532224 | bytes 6291456 | tf_op jit(solution)/shard_map/dot_general | solution.py:17
  175.1 7.9 %all-to-all-start.1 = ((bf16[32,32,1024]{2,1,0:T(8,128)(2,1)}), bf16[32,32,1024]{2,1,0:T(8,128)(2,1)}, u32[]{:S(2)}, u32[]{:S(2)}) async-start(bf16[32,32,1024]{2,1,0:T(8,128)(2,1)} %bitcast.70), calls=%async_computation.2 | async-start | bytes 4194304 | tf_op jit(solution)/shard_map/all_to_all | solution.py:72
  183.1 0.4 iota_compare_fusion
  183.5 28.0 %all-to-all-done.1 = bf16[32,32,1024]{2,1,0:T(8,128)(2,1)} async-done(((bf16[32,32,1024]{2,1,0:T(8,128)(2,1)}), bf16[32,32,1024]{2,1,0:T(8,128)(2,1)}, u32[]{:S(2)}, u32[]{:S(2)}) %all-to-all-start.1) | async-done | bytes 2097184 | tf_op jit(solution)/shard_map/all_to_all | solution.py:72
  211.4 2.4 convolution_multiply_fusion.1
  213.8 3.3 fusion.22
  217.1 0.9 fusion.13
  218.1 0.9 add_convert_fusion
  219.0 31.8 %all_to_all.21 = bf16[32,32,1024]{2,1,0:T(8,128)(2,1)S(1)} all-to-all(bf16[32,32,1024]{2,1,0:T(8,128)(2,1)S(1)} %bitcast.63), channel_id=1, replica_groups=mesh['dp'=4,'expert'=32] {'expert'}, dimensions={0} | all-to-all | bytes 4194304 | tf_op jit(solution)/shard_map/all_to_all | solution.py:86
  250.8 1.3 copy-done.6
  252.1 4.4 %fusion.4 = f32[1024,1024]{1,0:T(8,128)} fusion(bf16[1024,1024]{1,0:T(8,128)(2,1)S(1)} %bitcast.68, bf16[1,1024,1024]{2,1,0:T(8,128)(2,1)S(1)} %copy-done), kind=kOutput, calls=%fused_computation.9 | convolution fusion | flops 2147483648 | bytes 8388608 | tf_op jit(solution)/shard_map/dot_general | solution.py:17
  256.6 43.4 %reduce-scatter.5.cloned.1.call-done = f32[256,1024]{1,0:T(8,128)} async-done(((f32[1024,1024]{1,0:T(8,128)}), f32[256,1024]{1,0:T(8,128)}) %reduce-scatter.5.cloned.1.call-update) | async-done | bytes 1048592 | tf_op jit(solution)/shard_map/reduce_scatter | solution.py:94
  300.0 1.8 multiply_convert_fusion.1
  301.8 1.1 pad_maximum_fusion.5
  302.9 48.0 %all-gather.5.cloned.1.call-done = bf16[1024,2048]{1,0:T(8,128)(2,1)} async-done(((bf16[256,2048]{1,0:T(8,128)(2,1)}), bf16[1024,2048]{1,0:T(8,128)(2,1)}) %all-gather.5.cloned.1.call-update) | async-done | bytes 4194320 | tf_op jit(solution)/shard_map/all_gather | solution.py:97
  351.0 8.8 %fusion.11 = bf16[1024,1024]{1,0:T(8,128)(2,1)} fusion(bf16[1024,2048]{1,0:T(8,128)(2,1)} %all-gather.5.cloned.1.call-done, bf16[1024,1024]{1,0:T(8,128)(2,1)S(1)} %bitcast.81, bf16[1024,1024]{1,0:T(8,128)(2,1)} %bitcast.82), kind=kOutput, calls=%fused_computation.15 | convolution fusion | flops 4304404480 | bytes 10485760 | tf_op jit(solution)/shard_map/dot_general | solution.py:17
  359.7 7.9 %all-to-all-start.3 = ((bf16[32,32,1024]{2,1,0:T(8,128)(2,1)}), bf16[32,32,1024]{2,1,0:T(8,128)(2,1)}, u32[]{:S(2)}, u32[]{:S(2)}) async-start(bf16[32,32,1024]{2,1,0:T(8,128)(2,1)} %bitcast.71), calls=%async_computation.5 | async-start | bytes 4194304 | tf_op jit(solution)/shard_map/all_to_all | solution.py:107
  367.6 6.1 %convolution_bitcast_fusion = f32[1,1024,1024]{2,1,0:T(8,128)} fusion(bf16[1024,1024]{1,0:T(8,128)(2,1)} %all-gather.3.cloned.1.call-done, bf16[1024,1024]{1,0:T(8,128)(2,1)S(1)} %bitcast.69), kind=kOutput, calls=%fused_computation.4 | convolution fusion | flops 2147483648 | bytes 8388608 | tf_op jit(solution)/shard_map/dot_general | solution.py:17
  373.8 4.4 %convolution_bitcast_fusion.1 = f32[1,1024,1024]{2,1,0:T(8,128)} fusion(bf16[1024,1024]{1,0:T(8,128)(2,1)S(1)} %bitcast.66, bf16[1024,2048]{1,0:T(8,128)(2,1)S(1)} %copy-done.11), kind=kOutput, calls=%fused_computation.5 | convolution fusion | flops 2147483648 | bytes 8388608 | tf_op jit(solution)/shard_map/dot_general | solution.py:17
  378.2 4.4 %convolution_bitcast_fusion.2 = f32[1,1024,1024]{2,1,0:T(8,128)} fusion(bf16[1024,1024]{1,0:T(8,128)(2,1)S(1)} %bitcast.67, bf16[1024,2048]{1,0:T(8,128)(2,1)S(1)} %copy-done.11), kind=kOutput, calls=%fused_computation.6 | convolution fusion | flops 2147483648 | bytes 8388608 | tf_op jit(solution)/shard_map/dot_general | solution.py:17
  382.7 13.3 %all-to-all-done.3 = bf16[32,32,1024]{2,1,0:T(8,128)(2,1)} async-done(((bf16[32,32,1024]{2,1,0:T(8,128)(2,1)}), bf16[32,32,1024]{2,1,0:T(8,128)(2,1)}, u32[]{:S(2)}, u32[]{:S(2)}) %all-to-all-start.3) | async-done | bytes 2097184 | tf_op jit(solution)/shard_map/all_to_all | solution.py:107
  396.0 3.1 convolution_convert_fusion.1
  (50 shorter events, 1.6 us)
Async XLA Ops:
  7.2 162.7 %copy-start = (bf16[1,1024,1024]{2,1,0:T(8,128)(2,1)S(1)}, bf16[1,1024,1024]{2,1,0:T(8,128)(2,1)}, u32[]{:S(2)}) copy-start(bf16[1,1024,1024]{2,1,0:T(8,128)(2,1)} %param.15) | copy-start | bytes 6291460
  7.2 4.3 %copy-start.8 = (bf16[256,1024]{1,0:T(8,128)(2,1)S(1)}, bf16[256,1024]{1,0:T(8,128)(2,1)}, u32[]{:S(2)}) copy-start(bf16[256,1024]{1,0:T(8,128)(2,1)} %param.8) | copy-start | bytes 1572868
  7.2 129.4 %reduce-scatter.3.cloned.1.call-start = ((), (), s32[]{:S(2)}) async-start(), calls=%async_computation.6 | async-start | bytes 10485760 | tf_op jit(solution)/shard_map/reduce_scatter | solution.py:60
  12.2 38.1 %copy-start.12 = (bf16[1,1024,1024]{2,1,0:T(8,128)(2,1)S(1)}, bf16[1,1024,1024]{2,1,0:T(8,128)(2,1)}, u32[]{:S(2)}) copy-start(bf16[1,1024,1024]{2,1,0:T(8,128)(2,1)} %param.14) | copy-start | bytes 6291460
  12.2 38.1 %copy-start.14 = (bf16[1,1024,1024]{2,1,0:T(8,128)(2,1)S(1)}, bf16[1,1024,1024]{2,1,0:T(8,128)(2,1)}, u32[]{:S(2)}) copy-start(bf16[1,1024,1024]{2,1,0:T(8,128)(2,1)} %param.13) | copy-start | bytes 6291460
  49.0 1.3 copy-start.4
  57.2 112.7 %all-gather.3.cloned.1.call-start = ((), (), s32[]{:S(2)}) async-start(), calls=%async_computation.7 | async-start | bytes 2621440 | tf_op jit(solution)/shard_map/all_gather | solution.py:68
  175.1 7.9 %copy-start.10 = (f32[256,2]{0,1:T(2,128)S(1)}, f32[256,2]{0,1:T(2,128)}, u32[]{:S(2)}) copy-start(f32[256,2]{0,1:T(2,128)} %param.11) | copy-start | bytes 6148
  175.1 36.3 %all-to-all-start.1 = ((bf16[32,32,1024]{2,1,0:T(8,128)(2,1)}), bf16[32,32,1024]{2,1,0:T(8,128)(2,1)}, u32[]{:S(2)}, u32[]{:S(2)}) async-start(bf16[32,32,1024]{2,1,0:T(8,128)(2,1)} %bitcast.70), calls=%async_computation.2 | async-start | bytes 4194304 | tf_op jit(solution)/shard_map/all_to_all | solution.py:72
  183.0 116.9 %reduce-scatter.5.cloned.1.call-start = ((), (), s32[]{:S(2)}) async-start(), calls=%async_computation.8 | async-start | bytes 5242880 | tf_op jit(solution)/shard_map/reduce_scatter | solution.py:94
  213.8 3.3 copy-start.3
  213.8 3.3 copy-start.9
  250.8 1.3 copy-start.6
  256.5 43.4 %copy-start.2 = (f32[256,2048]{1,0:T(8,128)S(1)}, f32[256,2048]{1,0:T(8,128)}, u32[]{:S(2)}) copy-start(f32[256,2048]{1,0:T(8,128)} %reduce-scatter.3.cloned.1.call-done) | copy-start | bytes 6291460
  256.6 94.4 %all-gather.5.cloned.1.call-start = ((), (), s32[]{:S(2)}) async-start(), calls=%async_computation.9 | async-start | bytes 5242880 | tf_op jit(solution)/shard_map/all_gather | solution.py:97
  301.8 49.1 %copy-start.13 = (bf16[1,1024,1024]{2,1,0:T(8,128)(2,1)S(1)}, bf16[1,1024,1024]{2,1,0:T(8,128)(2,1)}, u32[]{:S(2)}) copy-start(bf16[1,1024,1024]{2,1,0:T(8,128)(2,1)} %param.14) | copy-start | bytes 6291460
  359.7 7.9 %copy-start.7 = (bf16[32,32,1024]{2,1,0:T(8,128)(2,1)S(1)}, bf16[32,32,1024]{2,1,0:T(8,128)(2,1)}, u32[]{:S(2)}) copy-start(bf16[32,32,1024]{2,1,0:T(8,128)(2,1)} %copy-done.6) | copy-start | bytes 6291460
  359.7 36.3 %all-to-all-start.3 = ((bf16[32,32,1024]{2,1,0:T(8,128)(2,1)}), bf16[32,32,1024]{2,1,0:T(8,128)(2,1)}, u32[]{:S(2)}, u32[]{:S(2)}) async-start(bf16[32,32,1024]{2,1,0:T(8,128)(2,1)} %bitcast.71), calls=%async_computation.5 | async-start | bytes 4194304 | tf_op jit(solution)/shard_map/all_to_all | solution.py:107
  367.6 6.2 %copy-start.5 = (bf16[32,32,1024]{2,1,0:T(8,128)(2,1)S(1)}, bf16[32,32,1024]{2,1,0:T(8,128)(2,1)}, u32[]{:S(2)}) copy-start(bf16[32,32,1024]{2,1,0:T(8,128)(2,1)} %copy-done.4) | copy-start | bytes 6291460
  367.6 6.2 %copy-start.11 = (bf16[1024,2048]{1,0:T(8,128)(2,1)S(1)}, bf16[1024,2048]{1,0:T(8,128)(2,1)}, u32[]{:S(2)}) copy-start(bf16[1024,2048]{1,0:T(8,128)(2,1)} %all-gather.5.cloned.1.call-done) | copy-start | bytes 12582916
  378.2 20.9 %copy-start.1 = (bf16[1,1024,1024]{2,1,0:T(8,128)(2,1)S(1)}, bf16[1,1024,1024]{2,1,0:T(8,128)(2,1)}, u32[]{:S(2)}) copy-start(bf16[1,1024,1024]{2,1,0:T(8,128)(2,1)} %param.15) | copy-start | bytes 6291460
Sparse Core Ops, SparseCore 0:
  57.3 79.2 reduce-scatter.2
  139.4 30.4 all-gather.2
  256.7 43.2 reduce-scatter.4
  303.0 47.8 all-gather.4

commit v6 on v4

--- a/solution.py
+++ b/solution.py
@@ -2,15 +2,6 @@
 import jax.numpy as jnp
 from jax import lax
 from jax.sharding import PartitionSpec as P
-
-
-def slot_ranks(routing, experts):
-    listed = routing.reshape(routing.shape[0], -1)
-    onehot = (listed[:, :, None] == jnp.arange(experts, dtype=jnp.int32)[None, None, :]).astype(
-        jnp.int32
-    )
-    earlier = jnp.cumsum(onehot, axis=1) - onehot
-    return jnp.sum(earlier * onehot, axis=2)
 
 
 def contract(left, right, left_dim, right_dim):
@@ -42,12 +33,17 @@
     up_mat = w_up[0]
     down_mat = w_down[0]
     ff = gate_mat.shape[1]
-    ranks = slot_ranks(expert_ids.reshape(1, tok_rows, 2), experts).reshape(-1)
-    slot_rows = expert_ids.reshape(-1) * capacity + ranks
+    listed = expert_ids.reshape(-1)
+    order = jnp.arange(2 * tok_rows, dtype=jnp.int32)
+    onehot = (listed[:, None] == jnp.arange(experts, dtype=jnp.int32)[None, :]).astype(jnp.bfloat16)
+    before = (order[None, :] < order[:, None]).astype(jnp.bfloat16)
+    counts = contract(before, onehot, 1, 0)
+    ranks = jnp.sum(counts * onehot.astype(jnp.float32), axis=1).astype(jnp.int32)
+    slot_rows = (listed * capacity + ranks).reshape(tok_rows, 2).T.reshape(-1)
     select = (slot_rows[:, None] == jnp.arange(rows_all, dtype=slot_rows.dtype)[None, :]).astype(
         jnp.bfloat16
     )
-    per_token = jnp.sum(select.reshape(tok_rows, 2, rows_all), axis=1)
+    per_token = select[:tok_rows] + select[tok_rows:]
     outgoing = contract(per_token, tokens, 0, 0).astype(jnp.bfloat16)
     arrived = lax.all_to_all(
         outgoing.reshape(experts, capacity, quarter),
@@ -71,17 +67,16 @@
     returned = lax.all_to_all(out_slots, "expert", split_axis=0, concat_axis=0, tiled=True).reshape(
         rows_all, quarter
     )
-    pair = select.reshape(tok_rows, 2, rows_all)
-    first, second = pair[:, 0], pair[:, 1]
-    combined = gate_weights[:, 0:1] * contract(first, returned, 1, 0) + gate_weights[
-        :, 1:2
-    ] * contract(second, returned, 1, 0)
+    picked = contract(select, returned, 1, 0)
+    combined = (
+        gate_weights[:, 0:1] * picked[:tok_rows] + gate_weights[:, 1:2] * picked[tok_rows:]
+    )
     mixed = combined.astype(jnp.bfloat16)
     row_grad = level_weights[:, None] * (combined - targets.astype(jnp.float32))
-    grad_out = (
-        contract(first, (gate_weights[:, 0:1] * row_grad).astype(jnp.bfloat16), 0, 0)
-        + contract(second, (gate_weights[:, 1:2] * row_grad).astype(jnp.bfloat16), 0, 0)
+    slot_grad = jnp.concatenate(
+        [gate_weights[:, 0:1] * row_grad, gate_weights[:, 1:2] * row_grad], axis=0
     ).astype(jnp.bfloat16)
+    grad_out = contract(select, slot_grad, 0, 0).astype(jnp.bfloat16)
     grad_slots = lax.all_to_all(
         grad_out.reshape(experts, capacity, quarter),
         "expert",

time: 405 us -> 403 us (level)
    dot_general x14 -> x13, matrix products: 50.8 us -> 49 us  [contract(): lax.dot_general(left, right, (((left_dim,), (right_dim,)), ((), ())), pre...]
where the time goes in v6:
time: 403 us; the launch traced here: 402 us
  waiting for transfers between devices  243 us (60%)
  blocking collectives  68.5 us (17%)
  matrix products  49 us (12%)
  starting transfers between devices  15.9 us (4%)
  between operations  14 us (3%)
  other arithmetic  7.9 us (2%)
    reduce_scatter x1, waiting for transfers between devices, shards(): lax.psum_scatter(contract(arrived, jnp.concatenate([gate_mat, up_mat], ax...  79.3 us
    dot_general x13, matrix products, contract(): lax.dot_general(left, right, (((left_dim,), (right_dim,)), ((), ())), pre...  49 us
    all_gather x1, waiting for transfers between devices, shards(): lax.all_gather(jnp.concatenate(derivatives(hidden_grad, gate_pre, up_pre,...  48 us
    reduce_scatter x1, waiting for transfers between devices, shards(): lax.psum_scatter(contract(grad_slots, down_mat, 1, 1), 'dp', scatter_dime...  43.4 us
    all_to_all x1, blocking collectives, shards(): lax.all_to_all(outgoing.reshape(experts, capacity, quarter), 'expert', sp...  36.8 us
    all_to_all x1, blocking collectives, shards(): lax.all_to_all(grad_out.reshape(experts, capacity, quarter), 'expert', sp...  31.8 us
    all_gather x1, waiting for transfers between devices, shards(): hidden = lax.all_gather(hidden_part, 'dp', axis=0, tiled=True)  30.6 us
    all_to_all x1, waiting for transfers between devices, shards(): lax.all_to_all(out_slots, 'expert', split_axis=0, concat_axis=0, tiled=True)  28.3 us
  transfers between devices with their start and end apart: 6, of which 6 were waited for; matrix products, arithmetic and copies ran while one was open for 4% of the time, Pallas kernels for 0%

profile of v6, /device:TPU:1, one launch (start us, length us, event | category | flops | bytes accessed | tf_op | source)
XLA Modules:
  0.0 402.4 jit_solution(17099181290560538631)
XLA Ops:
  7.2 0.9 copy.20
  8.3 0.3 fusion.20
  8.8 0.7 add_bitcast_fusion
  9.8 1.8 convolution_convert_fusion
  11.6 36.8 %all_to_all.20 = bf16[32,32,1024]{2,1,0:T(8,128)(2,1)S(1)} all-to-all(bf16[32,32,1024]{2,1,0:T(8,128)(2,1)S(1)} %bitcast.43), channel_id=1, replica_groups=mesh['dp'=4,'expert'=32] {'expert'}, dimensions={0} | all-to-all | bytes 4194304 | tf_op jit(solution)/shard_map/all_to_all | solution.py:48
  48.4 1.3 copy-done.3
  49.7 6.9 %fusion = f32[1024,2048]{1,0:T(8,128)} fusion(bf16[1024,1024]{1,0:T(8,128)(2,1)S(1)} %bitcast.44, bf16[1024,1024]{1,0:T(8,128)(2,1)S(1)} %bitcast.59, bf16[1024,1024]{1,0:T(8,128)(2,1)S(1)} %bitcast.58), kind=kOutput, calls=%fused_computation | convolution fusion | flops 4303355904 | bytes 14680064 | tf_op jit(solution)/shard_map/dot_general | solution.py:8
  56.7 79.3 %reduce-scatter.3.cloned.1.call-done = f32[256,2048]{1,0:T(8,128)} async-done(((f32[1024,2048]{1,0:T(8,128)}), f32[256,2048]{1,0:T(8,128)}) %reduce-scatter.3.cloned.1.call-update) | async-done | bytes 2097168 | tf_op jit(solution)/shard_map/reduce_scatter | solution.py:55
  136.0 2.6 multiply_convert_fusion.4
  138.7 30.6 %all-gather.3.cloned.1.call-done = bf16[1024,1024]{1,0:T(8,128)(2,1)} async-done(((bf16[256,1024]{1,0:T(8,128)(2,1)}), bf16[1024,1024]{1,0:T(8,128)(2,1)}) %all-gather.3.cloned.1.call-update) | async-done | bytes 2097168 | tf_op jit(solution)/shard_map/all_gather | solution.py:63
  169.3 5.2 %fusion.12 = bf16[1024,1024]{1,0:T(8,128)(2,1)} fusion(bf16[1024,1024]{1,0:T(8,128)(2,1)} %all-gather.3.cloned.1.call-done, bf16[1,1024,1024]{2,1,0:T(8,128)(2,1)S(1)} %copy-done), kind=kOutput, calls=%fused_computation.17 | convolution fusion | flops 2148532224 | bytes 6291456 | tf_op jit(solution)/shard_map/dot_general | solution.py:8
  174.6 7.9 %all-to-all-start.1 = ((bf16[32,32,1024]{2,1,0:T(8,128)(2,1)}), bf16[32,32,1024]{2,1,0:T(8,128)(2,1)}, u32[]{:S(2)}, u32[]{:S(2)}) async-start(bf16[32,32,1024]{2,1,0:T(8,128)(2,1)} %bitcast.50), calls=%async_computation.2 | async-start | bytes 4194304 | tf_op jit(solution)/shard_map/all_to_all | solution.py:67
  182.5 28.3 %all-to-all-done.1 = bf16[32,32,1024]{2,1,0:T(8,128)(2,1)} async-done(((bf16[32,32,1024]{2,1,0:T(8,128)(2,1)}), bf16[32,32,1024]{2,1,0:T(8,128)(2,1)}, u32[]{:S(2)}, u32[]{:S(2)}) %all-to-all-start.1) | async-done | bytes 2097184 | tf_op jit(solution)/shard_map/all_to_all | solution.py:67
  210.9 2.9 fusion.9
  213.8 0.3 multiply_convert_fusion.3
  214.2 1.1 multiply_convert_fusion.2
  215.2 1.4 fusion.11
  216.6 31.8 %all_to_all.21 = bf16[32,32,1024]{2,1,0:T(8,128)(2,1)S(1)} all-to-all(bf16[32,32,1024]{2,1,0:T(8,128)(2,1)S(1)} %bitcast.51), channel_id=1, replica_groups=mesh['dp'=4,'expert'=32] {'expert'}, dimensions={0} | all-to-all | bytes 4194304 | tf_op jit(solution)/shard_map/all_to_all | solution.py:80
  248.4 1.3 copy-done.5
  249.7 4.4 %fusion.4 = f32[1024,1024]{1,0:T(8,128)} fusion(bf16[1024,1024]{1,0:T(8,128)(2,1)S(1)} %bitcast.47, bf16[1,1024,1024]{2,1,0:T(8,128)(2,1)S(1)} %copy-done), kind=kOutput, calls=%fused_computation.8 | convolution fusion | flops 2147483648 | bytes 8388608 | tf_op jit(solution)/shard_map/dot_general | solution.py:8
  254.2 43.4 %reduce-scatter.5.cloned.1.call-done = f32[256,1024]{1,0:T(8,128)} async-done(((f32[1024,1024]{1,0:T(8,128)}), f32[256,1024]{1,0:T(8,128)}) %reduce-scatter.5.cloned.1.call-update) | async-done | bytes 1048592 | tf_op jit(solution)/shard_map/reduce_scatter | solution.py:88
  297.6 1.8 multiply_convert_fusion.1
  299.5 1.1 pad_maximum_fusion
  300.5 48.0 %all-gather.5.cloned.1.call-done = bf16[1024,2048]{1,0:T(8,128)(2,1)} async-done(((bf16[256,2048]{1,0:T(8,128)(2,1)}), bf16[1024,2048]{1,0:T(8,128)(2,1)}) %all-gather.5.cloned.1.call-update) | async-done | bytes 4194320 | tf_op jit(solution)/shard_map/all_gather | solution.py:91
  348.6 4.1 %fusion.18 = f32[1024,1024]{1,0:T(8,128)S(1)} fusion(bf16[1024,2048]{1,0:T(8,128)(2,1)} %all-gather.5.cloned.1.call-done, bf16[1,1024,1024]{2,1,0:T(8,128)(2,1)S(1)} %copy-done.13), kind=kOutput, calls=%fused_computation.22 | convolution fusion | flops 2147483648 | bytes 8388608 | tf_op jit(solution)/shard_map/dot_general | solution.py:8
  352.7 3.8 add_convert_fusion
  356.5 7.9 %all-to-all-start.3 = ((bf16[32,32,1024]{2,1,0:T(8,128)(2,1)}), bf16[32,32,1024]{2,1,0:T(8,128)(2,1)}, u32[]{:S(2)}, u32[]{:S(2)}) async-start(bf16[32,32,1024]{2,1,0:T(8,128)(2,1)} %bitcast.49), calls=%async_computation.5 | async-start | bytes 4194304 | tf_op jit(solution)/shard_map/all_to_all | solution.py:103
  364.4 6.1 %convolution_bitcast_fusion = f32[1,1024,1024]{2,1,0:T(8,128)} fusion(bf16[1024,1024]{1,0:T(8,128)(2,1)} %all-gather.3.cloned.1.call-done, bf16[1024,1024]{1,0:T(8,128)(2,1)S(1)} %bitcast.48), kind=kOutput, calls=%fused_computation.5 | convolution fusion | flops 2147483648 | bytes 8388608 | tf_op jit(solution)/shard_map/dot_general | solution.py:8
  370.6 4.4 %convolution_bitcast_fusion.2 = f32[1,1024,1024]{2,1,0:T(8,128)} fusion(bf16[1024,1024]{1,0:T(8,128)(2,1)S(1)} %bitcast.45, bf16[1024,2048]{1,0:T(8,128)(2,1)S(1)} %copy-done.11), kind=kOutput, calls=%fused_computation.7 | convolution fusion | flops 2147483648 | bytes 8388608 | tf_op jit(solution)/shard_map/dot_general | solution.py:8
  375.0 4.4 %convolution_bitcast_fusion.1 = f32[1,1024,1024]{2,1,0:T(8,128)} fusion(bf16[1024,1024]{1,0:T(8,128)(2,1)S(1)} %bitcast.46, bf16[1024,2048]{1,0:T(8,128)(2,1)S(1)} %copy-done.11), kind=kOutput, calls=%fused_computation.6 | convolution fusion | flops 2147483648 | bytes 8388608 | tf_op jit(solution)/shard_map/dot_general | solution.py:8
  379.5 13.3 %all-to-all-done.3 = bf16[32,32,1024]{2,1,0:T(8,128)(2,1)} async-done(((bf16[32,32,1024]{2,1,0:T(8,128)(2,1)}), bf16[32,32,1024]{2,1,0:T(8,128)(2,1)}, u32[]{:S(2)}, u32[]{:S(2)}) %all-to-all-start.3) | async-done | bytes 2097184 | tf_op jit(solution)/shard_map/all_to_all | solution.py:103
  392.8 3.1 convolution_convert_fusion.1
  (45 shorter events, 0.9 us)
Async XLA Ops:
  7.2 162.2 %copy-start = (bf16[1,1024,1024]{2,1,0:T(8,128)(2,1)S(1)}, bf16[1,1024,1024]{2,1,0:T(8,128)(2,1)}, u32[]{:S(2)}) copy-start(bf16[1,1024,1024]{2,1,0:T(8,128)(2,1)} %param.15) | copy-start | bytes 6291460
  7.2 128.8 %reduce-scatter.3.cloned.1.call-start = ((), (), s32[]{:S(2)}) async-start(), calls=%async_computation.6 | async-start | bytes 10485760 | tf_op jit(solution)/shard_map/reduce_scatter | solution.py:55
  11.6 38.1 %copy-start.12 = (bf16[1,1024,1024]{2,1,0:T(8,128)(2,1)S(1)}, bf16[1,1024,1024]{2,1,0:T(8,128)(2,1)}, u32[]{:S(2)}) copy-start(bf16[1,1024,1024]{2,1,0:T(8,128)(2,1)} %param.13) | copy-start | bytes 6291460
  11.6 38.1 %copy-start.14 = (bf16[1,1024,1024]{2,1,0:T(8,128)(2,1)S(1)}, bf16[1,1024,1024]{2,1,0:T(8,128)(2,1)}, u32[]{:S(2)}) copy-start(bf16[1,1024,1024]{2,1,0:T(8,128)(2,1)} %param.14) | copy-start | bytes 6291460
  48.4 1.3 copy-start.3
  56.6 112.7 %all-gather.3.cloned.1.call-start = ((), (), s32[]{:S(2)}) async-start(), calls=%async_computation.7 | async-start | bytes 2621440 | tf_op jit(solution)/shard_map/all_gather | solution.py:63
  174.6 7.9 %copy-start.9 = (f32[256,2]{0,1:T(2,128)S(1)}, f32[256,2]{0,1:T(2,128)}, u32[]{:S(2)}) copy-start(f32[256,2]{0,1:T(2,128)} %param.11) | copy-start | bytes 6148
  174.6 36.3 %all-to-all-start.1 = ((bf16[32,32,1024]{2,1,0:T(8,128)(2,1)}), bf16[32,32,1024]{2,1,0:T(8,128)(2,1)}, u32[]{:S(2)}, u32[]{:S(2)}) async-start(bf16[32,32,1024]{2,1,0:T(8,128)(2,1)} %bitcast.50), calls=%async_computation.2 | async-start | bytes 4194304 | tf_op jit(solution)/shard_map/all_to_all | solution.py:67
  182.5 115.1 %reduce-scatter.5.cloned.1.call-start = ((), (), s32[]{:S(2)}) async-start(), calls=%async_computation.8 | async-start | bytes 5242880 | tf_op jit(solution)/shard_map/reduce_scatter | solution.py:88
  210.9 3.0 copy-start.7
  210.9 3.0 copy-start.8
  248.4 1.3 copy-start.5
  254.2 43.4 %copy-start.2 = (f32[256,2048]{1,0:T(8,128)S(1)}, f32[256,2048]{1,0:T(8,128)}, u32[]{:S(2)}) copy-start(f32[256,2048]{1,0:T(8,128)} %reduce-scatter.3.cloned.1.call-done) | copy-start | bytes 6291460
  254.2 94.4 %all-gather.5.cloned.1.call-start = ((), (), s32[]{:S(2)}) async-start(), calls=%async_computation.9 | async-start | bytes 5242880 | tf_op jit(solution)/shard_map/all_gather | solution.py:91
  299.5 49.1 %copy-start.13 = (bf16[1,1024,1024]{2,1,0:T(8,128)(2,1)S(1)}, bf16[1,1024,1024]{2,1,0:T(8,128)(2,1)}, u32[]{:S(2)}) copy-start(bf16[1,1024,1024]{2,1,0:T(8,128)(2,1)} %param.13) | copy-start | bytes 6291460
  348.6 4.1 %copy-start.10 = (bf16[1024,2048]{1,0:T(8,128)(2,1)S(1)}, bf16[1024,2048]{1,0:T(8,128)(2,1)}, u32[]{:S(2)}) copy-start(bf16[1024,2048]{1,0:T(8,128)(2,1)} %all-gather.5.cloned.1.call-done) | copy-start | bytes 12582916
  348.6 4.1 %copy-start.15 = (bf16[1,1024,1024]{2,1,0:T(8,128)(2,1)S(1)}, bf16[1,1024,1024]{2,1,0:T(8,128)(2,1)}, u32[]{:S(2)}) copy-start(bf16[1,1024,1024]{2,1,0:T(8,128)(2,1)} %param.14) | copy-start | bytes 6291460
  356.5 7.9 %copy-start.6 = (bf16[32,32,1024]{2,1,0:T(8,128)(2,1)S(1)}, bf16[32,32,1024]{2,1,0:T(8,128)(2,1)}, u32[]{:S(2)}) copy-start(bf16[32,32,1024]{2,1,0:T(8,128)(2,1)} %copy-done.5) | copy-start | bytes 6291460
  356.5 36.3 %all-to-all-start.3 = ((bf16[32,32,1024]{2,1,0:T(8,128)(2,1)}), bf16[32,32,1024]{2,1,0:T(8,128)(2,1)}, u32[]{:S(2)}, u32[]{:S(2)}) async-start(bf16[32,32,1024]{2,1,0:T(8,128)(2,1)} %bitcast.49), calls=%async_computation.5 | async-start | bytes 4194304 | tf_op jit(solution)/shard_map/all_to_all | solution.py:103
  364.4 6.2 %copy-start.4 = (bf16[32,32,1024]{2,1,0:T(8,128)(2,1)S(1)}, bf16[32,32,1024]{2,1,0:T(8,128)(2,1)}, u32[]{:S(2)}) copy-start(bf16[32,32,1024]{2,1,0:T(8,128)(2,1)} %copy-done.3) | copy-start | bytes 6291460
  364.4 6.2 %copy-start.11 = (bf16[1024,2048]{1,0:T(8,128)(2,1)S(1)}, bf16[1024,2048]{1,0:T(8,128)(2,1)}, u32[]{:S(2)}) copy-start(bf16[1024,2048]{1,0:T(8,128)(2,1)} %all-gather.5.cloned.1.call-done) | copy-start | bytes 12582916
  375.0 20.9 %copy-start.1 = (bf16[1,1024,1024]{2,1,0:T(8,128)(2,1)S(1)}, bf16[1,1024,1024]{2,1,0:T(8,128)(2,1)}, u32[]{:S(2)}) copy-start(bf16[1,1024,1024]{2,1,0:T(8,128)(2,1)} %param.15) | copy-start | bytes 6291460
Sparse Core Ops, SparseCore 0:
  56.7 79.2 reduce-scatter.2
  138.8 30.4 all-gather.2
  254.3 43.2 reduce-scatter.4
  300.7 47.8 all-gather.4

commit v7 on v6

--- a/solution.py
+++ b/solution.py
@@ -88,6 +88,7 @@
     hidden_grad = lax.psum_scatter(
         contract(grad_slots, down_mat, 1, 1), "dp", scatter_dimension=0, tiled=True
     )
+    hidden_grad, down_grad = lax.optimization_barrier((hidden_grad, down_grad))
     deltas = lax.all_gather(
         jnp.concatenate(derivatives(hidden_grad, gate_pre, up_pre, sigmoid_gate), axis=1),
         "dp",

time: 403 us -> 403 us (level)
    reduce_scatter x1, waiting for transfers between devices: 43.4 us -> 36.6 us  [shards(): lax.psum_scatter(contract(grad_slots, down_mat, 1, 1), 'dp', scatter_dime...]
    all_to_all x1, waiting for transfers between devices: 13.3 us -> 17.8 us  [shards(): lax.all_to_all(input_slots.reshape(experts, capacity, quarter), 'expert',...]
where the time goes in v7:
time: 403 us
  waiting for transfers between devices  241 us (60%)
  blocking collectives  68.5 us (17%)
  matrix products  51.3 us (13%)
  starting transfers between devices  15.9 us (4%)
  between operations  14 us (3%)
  other arithmetic  7.9 us (2%)
  local copies, waits for them, and re-layouts  4.09 us (1%)
    reduce_scatter x1, waiting for transfers between devices, shards(): lax.psum_scatter(contract(arrived, jnp.concatenate([gate_mat, up_mat], ax...  79.3 us
    dot_general x13, matrix products, contract(): lax.dot_general(left, right, (((left_dim,), (right_dim,)), ((), ())), pre...  51.3 us
    all_gather x1, waiting for transfers between devices, shards(): lax.all_gather(jnp.concatenate(derivatives(hidden_grad, gate_pre, up_pre,...  48.1 us
    all_to_all x1, blocking collectives, shards(): lax.all_to_all(outgoing.reshape(experts, capacity, quarter), 'expert', sp...  36.8 us
    reduce_scatter x1, waiting for transfers between devices, shards(): lax.psum_scatter(contract(grad_slots, down_mat, 1, 1), 'dp', scatter_dime...  36.6 us
    all_to_all x1, blocking collectives, shards(): lax.all_to_all(grad_out.reshape(experts, capacity, quarter), 'expert', sp...  31.8 us
    all_gather x1, waiting for transfers between devices, shards(): hidden = lax.all_gather(hidden_part, 'dp', axis=0, tiled=True)  30.6 us
    all_to_all x1, waiting for transfers between devices, shards(): lax.all_to_all(out_slots, 'expert', split_axis=0, concat_axis=0, tiled=True)  28.3 us
  transfers between devices with their start and end apart: 6, of which 6 were waited for; matrix products, arithmetic and copies ran while one was open for 4% of the time, Pallas kernels for 0%

profile of v7, /device:TPU:1, one launch (start us, length us, event | category | flops | bytes accessed | tf_op | source)
XLA Modules:
  0.0 402.5 jit_solution(3489858849017022979)
XLA Ops:
  7.2 0.9 copy.20
  8.3 0.3 fusion.20
  8.8 0.7 add_bitcast_fusion
  9.8 1.8 convolution_convert_fusion
  11.6 36.8 %all_to_all.20 = bf16[32,32,1024]{2,1,0:T(8,128)(2,1)S(1)} all-to-all(bf16[32,32,1024]{2,1,0:T(8,128)(2,1)S(1)} %bitcast.42), channel_id=1, replica_groups=mesh['dp'=4,'expert'=32] {'expert'}, dimensions={0} | all-to-all | bytes 4194304 | tf_op jit(solution)/shard_map/all_to_all | solution.py:48
  48.4 1.4 copy-done.3
  49.8 6.9 %fusion = f32[1024,2048]{1,0:T(8,128)} fusion(bf16[1024,1024]{1,0:T(8,128)(2,1)S(1)} %bitcast.43, bf16[1024,1024]{1,0:T(8,128)(2,1)S(1)} %bitcast.58, bf16[1024,1024]{1,0:T(8,128)(2,1)S(1)} %bitcast.57), kind=kOutput, calls=%fused_computation | convolution fusion | flops 4303355904 | bytes 14680064 | tf_op jit(solution)/shard_map/dot_general | solution.py:8
  56.8 79.3 %reduce-scatter.3.cloned.1.call-done = f32[256,2048]{1,0:T(8,128)} async-done(((f32[1024,2048]{1,0:T(8,128)}), f32[256,2048]{1,0:T(8,128)}) %reduce-scatter.3.cloned.1.call-update) | async-done | bytes 2097168 | tf_op jit(solution)/shard_map/reduce_scatter | solution.py:55
  136.1 2.6 multiply_convert_fusion.4
  138.8 30.6 %all-gather.3.cloned.1.call-done = bf16[1024,1024]{1,0:T(8,128)(2,1)} async-done(((bf16[256,1024]{1,0:T(8,128)(2,1)}), bf16[1024,1024]{1,0:T(8,128)(2,1)}) %all-gather.3.cloned.1.call-update) | async-done | bytes 2097168 | tf_op jit(solution)/shard_map/all_gather | solution.py:63
  169.4 5.2 %fusion.12 = bf16[1024,1024]{1,0:T(8,128)(2,1)} fusion(bf16[1024,1024]{1,0:T(8,128)(2,1)} %all-gather.3.cloned.1.call-done, bf16[1,1024,1024]{2,1,0:T(8,128)(2,1)S(1)} %copy-done), kind=kOutput, calls=%fused_computation.16 | convolution fusion | flops 2148532224 | bytes 6291456 | tf_op jit(solution)/shard_map/dot_general | solution.py:8
  174.6 7.9 %all-to-all-start.1 = ((bf16[32,32,1024]{2,1,0:T(8,128)(2,1)}), bf16[32,32,1024]{2,1,0:T(8,128)(2,1)}, u32[]{:S(2)}, u32[]{:S(2)}) async-start(bf16[32,32,1024]{2,1,0:T(8,128)(2,1)} %bitcast.48), calls=%async_computation.2 | async-start | bytes 4194304 | tf_op jit(solution)/shard_map/all_to_all | solution.py:67
  182.6 28.3 %all-to-all-done.1 = bf16[32,32,1024]{2,1,0:T(8,128)(2,1)} async-done(((bf16[32,32,1024]{2,1,0:T(8,128)(2,1)}), bf16[32,32,1024]{2,1,0:T(8,128)(2,1)}, u32[]{:S(2)}, u32[]{:S(2)}) %all-to-all-start.1) | async-done | bytes 2097184 | tf_op jit(solution)/shard_map/all_to_all | solution.py:67
  210.9 2.9 fusion.9
  213.9 0.3 multiply_convert_fusion.3
  214.2 1.1 multiply_convert_fusion.2
  215.3 1.4 fusion.11
  216.7 31.8 %all_to_all.21 = bf16[32,32,1024]{2,1,0:T(8,128)(2,1)S(1)} all-to-all(bf16[32,32,1024]{2,1,0:T(8,128)(2,1)S(1)} %bitcast.50), channel_id=1, replica_groups=mesh['dp'=4,'expert'=32] {'expert'}, dimensions={0} | all-to-all | bytes 4194304 | tf_op jit(solution)/shard_map/all_to_all | solution.py:80
  248.5 1.3 copy-done.6
  249.8 4.4 %fusion.4 = f32[1024,1024]{1,0:T(8,128)} fusion(bf16[1024,1024]{1,0:T(8,128)(2,1)S(1)} %bitcast.46, bf16[1,1024,1024]{2,1,0:T(8,128)(2,1)S(1)} %copy-done), kind=kOutput, calls=%fused_computation.7 | convolution fusion | flops 2147483648 | bytes 8388608 | tf_op jit(solution)/shard_map/dot_general | solution.py:8
  254.3 6.8 %fusion.35 = f32[1024,1024]{1,0:T(8,128)} fusion(bf16[1024,1024]{1,0:T(8,128)(2,1)} %all-gather.3.cloned.1.call-done, bf16[1024,1024]{1,0:T(8,128)(2,1)} %bitcast.47), kind=kOutput, calls=%fused_computation.53 | convolution fusion | flops 2147483648 | bytes 8388608 | tf_op jit(solution)/shard_map/dot_general | solution.py:8
  261.1 36.6 %reduce-scatter.5.cloned.1.call-done = f32[256,1024]{1,0:T(8,128)} async-done(((f32[1024,1024]{1,0:T(8,128)}), f32[256,1024]{1,0:T(8,128)}) %reduce-scatter.5.cloned.1.call-update) | async-done | bytes 1048592 | tf_op jit(solution)/shard_map/reduce_scatter | solution.py:88
  297.7 1.8 multiply_convert_fusion.1
  299.5 1.1 pad_maximum_fusion
  300.6 48.1 %all-gather.5.cloned.1.call-done = bf16[1024,2048]{1,0:T(8,128)(2,1)} async-done(((bf16[256,2048]{1,0:T(8,128)(2,1)}), bf16[1024,2048]{1,0:T(8,128)(2,1)}) %all-gather.5.cloned.1.call-update) | async-done | bytes 4194320 | tf_op jit(solution)/shard_map/all_gather | solution.py:92
  348.7 4.1 %fusion.18 = f32[1024,1024]{1,0:T(8,128)S(1)} fusion(bf16[1024,2048]{1,0:T(8,128)(2,1)} %all-gather.5.cloned.1.call-done, bf16[1,1024,1024]{2,1,0:T(8,128)(2,1)S(1)} %copy-done.13), kind=kOutput, calls=%fused_computation.21 | convolution fusion | flops 2147483648 | bytes 8388608 | tf_op jit(solution)/shard_map/dot_general | solution.py:8
  352.8 3.8 add_convert_fusion
  356.6 7.9 %all-to-all-start.3 = ((bf16[32,32,1024]{2,1,0:T(8,128)(2,1)}), bf16[32,32,1024]{2,1,0:T(8,128)(2,1)}, u32[]{:S(2)}, u32[]{:S(2)}) async-start(bf16[32,32,1024]{2,1,0:T(8,128)(2,1)} %bitcast.49), calls=%async_computation.5 | async-start | bytes 4194304 | tf_op jit(solution)/shard_map/all_to_all | solution.py:104
  364.5 6.1 %convolution_bitcast_fusion.1 = f32[1,1024,1024]{2,1,0:T(8,128)} fusion(bf16[1024,1024]{1,0:T(8,128)(2,1)S(1)} %bitcast.44, bf16[1024,2048]{1,0:T(8,128)(2,1)} %all-gather.5.cloned.1.call-done), kind=kOutput, calls=%fused_computation.6 | convolution fusion | flops 2147483648 | bytes 8388608 | tf_op jit(solution)/shard_map/dot_general | solution.py:8
  370.7 4.4 %convolution_bitcast_fusion = f32[1,1024,1024]{2,1,0:T(8,128)} fusion(bf16[1024,1024]{1,0:T(8,128)(2,1)S(1)} %bitcast.45, bf16[1024,2048]{1,0:T(8,128)(2,1)S(1)} %copy-done.11), kind=kOutput, calls=%fused_computation.5 | convolution fusion | flops 2147483648 | bytes 8388608 | tf_op jit(solution)/shard_map/dot_general | solution.py:8
  375.1 17.8 %all-to-all-done.3 = bf16[32,32,1024]{2,1,0:T(8,128)(2,1)} async-done(((bf16[32,32,1024]{2,1,0:T(8,128)(2,1)}), bf16[32,32,1024]{2,1,0:T(8,128)(2,1)}, u32[]{:S(2)}, u32[]{:S(2)}) %all-to-all-start.3) | async-done | bytes 2097184 | tf_op jit(solution)/shard_map/all_to_all | solution.py:104
  392.9 3.1 convolution_convert_fusion.1
  (45 shorter events, 0.9 us)
Async XLA Ops:
  7.2 162.2 %copy-start = (bf16[1,1024,1024]{2,1,0:T(8,128)(2,1)S(1)}, bf16[1,1024,1024]{2,1,0:T(8,128)(2,1)}, u32[]{:S(2)}) copy-start(bf16[1,1024,1024]{2,1,0:T(8,128)(2,1)} %param.15) | copy-start | bytes 6291460
  7.2 128.9 %reduce-scatter.3.cloned.1.call-start = ((), (), s32[]{:S(2)}) async-start(), calls=%async_computation.6 | async-start | bytes 10485760 | tf_op jit(solution)/shard_map/reduce_scatter | solution.py:55
  11.6 38.2 %copy-start.12 = (bf16[1,1024,1024]{2,1,0:T(8,128)(2,1)S(1)}, bf16[1,1024,1024]{2,1,0:T(8,128)(2,1)}, u32[]{:S(2)}) copy-start(bf16[1,1024,1024]{2,1,0:T(8,128)(2,1)} %param.13) | copy-start | bytes 6291460
  11.6 38.2 %copy-start.14 = (bf16[1,1024,1024]{2,1,0:T(8,128)(2,1)S(1)}, bf16[1,1024,1024]{2,1,0:T(8,128)(2,1)}, u32[]{:S(2)}) copy-start(bf16[1,1024,1024]{2,1,0:T(8,128)(2,1)} %param.14) | copy-start | bytes 6291460
  48.4 1.4 copy-start.3
  56.7 112.7 %all-gather.3.cloned.1.call-start = ((), (), s32[]{:S(2)}) async-start(), calls=%async_computation.7 | async-start | bytes 2621440 | tf_op jit(solution)/shard_map/all_gather | solution.py:63
  174.6 7.9 %copy-start.9 = (f32[256,2]{0,1:T(2,128)S(1)}, f32[256,2]{0,1:T(2,128)}, u32[]{:S(2)}) copy-start(f32[256,2]{0,1:T(2,128)} %param.11) | copy-start | bytes 6148
  174.6 36.3 %all-to-all-start.1 = ((bf16[32,32,1024]{2,1,0:T(8,128)(2,1)}), bf16[32,32,1024]{2,1,0:T(8,128)(2,1)}, u32[]{:S(2)}, u32[]{:S(2)}) async-start(bf16[32,32,1024]{2,1,0:T(8,128)(2,1)} %bitcast.48), calls=%async_computation.2 | async-start | bytes 4194304 | tf_op jit(solution)/shard_map/all_to_all | solution.py:67
  182.5 115.1 %reduce-scatter.5.cloned.1.call-start = ((), (), s32[]{:S(2)}) async-start(), calls=%async_computation.8 | async-start | bytes 5242880 | tf_op jit(solution)/shard_map/reduce_scatter | solution.py:88
  210.9 3.0 copy-start.7
  210.9 3.0 copy-start.8
  248.5 1.3 copy-start.6
  254.3 43.4 %copy-start.2 = (f32[256,2048]{1,0:T(8,128)S(1)}, f32[256,2048]{1,0:T(8,128)}, u32[]{:S(2)}) copy-start(f32[256,2048]{1,0:T(8,128)} %reduce-scatter.3.cloned.1.call-done) | copy-start | bytes 6291460
  254.3 94.4 %all-gather.5.cloned.1.call-start = ((), (), s32[]{:S(2)}) async-start(), calls=%async_computation.9 | async-start | bytes 5242880 | tf_op jit(solution)/shard_map/all_gather | solution.py:92
  299.5 49.2 %copy-start.13 = (bf16[1,1024,1024]{2,1,0:T(8,128)(2,1)S(1)}, bf16[1,1024,1024]{2,1,0:T(8,128)(2,1)}, u32[]{:S(2)}) copy-start(bf16[1,1024,1024]{2,1,0:T(8,128)(2,1)} %param.13) | copy-start | bytes 6291460
  348.7 4.1 %copy-start.10 = (bf16[1024,2048]{1,0:T(8,128)(2,1)S(1)}, bf16[1024,2048]{1,0:T(8,128)(2,1)}, u32[]{:S(2)}) copy-start(bf16[1024,2048]{1,0:T(8,128)(2,1)} %all-gather.5.cloned.1.call-done) | copy-start | bytes 12582916
  348.7 4.1 %copy-start.15 = (bf16[1,1024,1024]{2,1,0:T(8,128)(2,1)S(1)}, bf16[1,1024,1024]{2,1,0:T(8,128)(2,1)}, u32[]{:S(2)}) copy-start(bf16[1,1024,1024]{2,1,0:T(8,128)(2,1)} %param.14) | copy-start | bytes 6291460
  356.6 7.9 %copy-start.4 = (bf16[32,32,1024]{2,1,0:T(8,128)(2,1)S(1)}, bf16[32,32,1024]{2,1,0:T(8,128)(2,1)}, u32[]{:S(2)}) copy-start(bf16[32,32,1024]{2,1,0:T(8,128)(2,1)} %copy-done.3) | copy-start | bytes 6291460
  356.6 36.3 %all-to-all-start.3 = ((bf16[32,32,1024]{2,1,0:T(8,128)(2,1)}), bf16[32,32,1024]{2,1,0:T(8,128)(2,1)}, u32[]{:S(2)}, u32[]{:S(2)}) async-start(bf16[32,32,1024]{2,1,0:T(8,128)(2,1)} %bitcast.49), calls=%async_computation.5 | async-start | bytes 4194304 | tf_op jit(solution)/shard_map/all_to_all | solution.py:104
  364.5 6.2 %copy-start.5 = (bf16[32,32,1024]{2,1,0:T(8,128)(2,1)S(1)}, bf16[32,32,1024]{2,1,0:T(8,128)(2,1)}, u32[]{:S(2)}) copy-start(bf16[32,32,1024]{2,1,0:T(8,128)(2,1)} %copy-done.3) | copy-start | bytes 6291460
  364.5 6.2 %copy-start.11 = (bf16[1024,2048]{1,0:T(8,128)(2,1)S(1)}, bf16[1024,2048]{1,0:T(8,128)(2,1)}, u32[]{:S(2)}) copy-start(bf16[1024,2048]{1,0:T(8,128)(2,1)} %all-gather.5.cloned.1.call-done) | copy-start | bytes 12582916
  370.7 25.3 %copy-start.1 = (bf16[1,1024,1024]{2,1,0:T(8,128)(2,1)S(1)}, bf16[1,1024,1024]{2,1,0:T(8,128)(2,1)}, u32[]{:S(2)}) copy-start(bf16[1,1024,1024]{2,1,0:T(8,128)(2,1)} %param.15) | copy-start | bytes 6291460
Sparse Core Ops, SparseCore 0:
  56.8 79.2 reduce-scatter.2
  138.9 30.4 all-gather.2
  254.4 43.2 reduce-scatter.4
  300.7 47.9 all-gather.4

commit v8 on v6

--- a/solution.py
+++ b/solution.py
@@ -13,14 +13,6 @@
 def activate(gate_pre, up_pre):
     sigmoid_gate = jax.nn.sigmoid(gate_pre)
     return (sigmoid_gate, (gate_pre * sigmoid_gate * up_pre).astype(jnp.bfloat16))
-
-
-def derivatives(hidden_grad, gate_pre, up_pre, sigmoid_gate):
-    gate_delta = (
-        hidden_grad * up_pre * sigmoid_gate * (1.0 + gate_pre * (1.0 - sigmoid_gate))
-    ).astype(jnp.bfloat16)
-    up_delta = (hidden_grad * gate_pre * sigmoid_gate).astype(jnp.bfloat16)
-    return (gate_delta, up_delta)
 
 
 def shards(tokens, targets, expert_ids, gate_weights, level_weights, w_gate, w_up, w_down):
@@ -88,8 +80,16 @@
     hidden_grad = lax.psum_scatter(
         contract(grad_slots, down_mat, 1, 1), "dp", scatter_dimension=0, tiled=True
     )
+    twice = jnp.concatenate([hidden_grad, hidden_grad], axis=1)
     deltas = lax.all_gather(
-        jnp.concatenate(derivatives(hidden_grad, gate_pre, up_pre, sigmoid_gate), axis=1),
+        (
+            twice
+            * jnp.concatenate([up_pre, gate_pre], axis=1)
+            * jnp.concatenate([sigmoid_gate, sigmoid_gate], axis=1)
+            * jnp.concatenate(
+                [1.0 + gate_pre * (1.0 - sigmoid_gate), jnp.ones_like(gate_pre)], axis=1
+            )
+        ).astype(jnp.bfloat16),
         "dp",
         axis=0,
         tiled=True,

time: 403 us -> 405 us (level)
  no operation moved by 1% of the time
where the time goes in v8:
time: 405 us
  waiting for transfers between devices  243 us (60%)
  blocking collectives  68.5 us (17%)
  matrix products  49.9 us (12%)
  starting transfers between devices  15.9 us (4%)
  between operations  14 us (3%)
  other arithmetic  9.38 us (2%)
    reduce_scatter x1, waiting for transfers between devices, shards(): lax.psum_scatter(contract(arrived, jnp.concatenate([gate_mat, up_mat], ax...  79.3 us
    dot_general x13, matrix products, contract(): lax.dot_general(left, right, (((left_dim,), (right_dim,)), ((), ())), pre...  49.9 us
    all_gather x1, waiting for transfers between devices, shards(): lax.all_gather((twice * jnp.concatenate([up_pre, gate_pre], axis=1) * jnp...  48 us
    reduce_scatter x1, waiting for transfers between devices, shards(): lax.psum_scatter(contract(grad_slots, down_mat, 1, 1), 'dp', scatter_dime...  43.4 us
    all_to_all x1, blocking collectives, shards(): lax.all_to_all(outgoing.reshape(experts, capacity, quarter), 'expert', sp...  36.8 us
    all_to_all x1, blocking collectives, shards(): lax.all_to_all(grad_out.reshape(experts, capacity, quarter), 'expert', sp...  31.8 us
    all_gather x1, waiting for transfers between devices, shards(): hidden = lax.all_gather(hidden_part, 'dp', axis=0, tiled=True)  30.6 us
    all_to_all x1, waiting for transfers between devices, shards(): lax.all_to_all(out_slots, 'expert', split_axis=0, concat_axis=0, tiled=True)  28.3 us
  transfers between devices with their start and end apart: 6, of which 6 were waited for; matrix products, arithmetic and copies ran while one was open for 4% of the time, Pallas kernels for 0%

profile of v8, /device:TPU:1, one launch (start us, length us, event | category | flops | bytes accessed | tf_op | source)
XLA Modules:
  0.0 404.9 jit_solution(2302479639005212810)
XLA Ops:
  7.2 0.9 copy.20
  8.3 0.3 fusion.23
  8.8 0.7 add_bitcast_fusion
  9.5 0.2 fusion.13
  9.8 2.2 convolution_convert_fusion
  12.0 36.8 %all_to_all.20 = bf16[32,32,1024]{2,1,0:T(8,128)(2,1)S(1)} all-to-all(bf16[32,32,1024]{2,1,0:T(8,128)(2,1)S(1)} %bitcast.43), channel_id=1, replica_groups=mesh['dp'=4,'expert'=32] {'expert'}, dimensions={0} | all-to-all | bytes 4194304 | tf_op jit(solution)/shard_map/all_to_all | solution.py:40
  48.8 1.3 copy-done.6
  50.1 6.9 %fusion = f32[1024,2048]{1,0:T(8,128)} fusion(bf16[1024,1024]{1,0:T(8,128)(2,1)S(1)} %bitcast.44, bf16[1024,1024]{1,0:T(8,128)(2,1)S(1)} %bitcast.59, bf16[1024,1024]{1,0:T(8,128)(2,1)S(1)} %bitcast.58), kind=kOutput, calls=%fused_computation | convolution fusion | flops 4303355904 | bytes 14680064 | tf_op jit(solution)/shard_map/dot_general | solution.py:8
  57.1 79.3 %reduce-scatter.3.cloned.1.call-done = f32[256,2048]{1,0:T(8,128)} async-done(((f32[1024,2048]{1,0:T(8,128)}), f32[256,2048]{1,0:T(8,128)}) %reduce-scatter.3.cloned.1.call-update) | async-done | bytes 2097168 | tf_op jit(solution)/shard_map/reduce_scatter | solution.py:47
  136.4 3.6 multiply_add_fusion
  140.1 30.6 %all-gather.3.cloned.1.call-done = bf16[1024,1024]{1,0:T(8,128)(2,1)} async-done(((bf16[256,1024]{1,0:T(8,128)(2,1)}), bf16[1024,1024]{1,0:T(8,128)(2,1)}) %all-gather.3.cloned.1.call-update) | async-done | bytes 2097168 | tf_op jit(solution)/shard_map/all_gather | solution.py:55
  170.7 5.2 %fusion.15 = bf16[1024,1024]{1,0:T(8,128)(2,1)} fusion(bf16[1024,1024]{1,0:T(8,128)(2,1)} %all-gather.3.cloned.1.call-done, bf16[1,1024,1024]{2,1,0:T(8,128)(2,1)S(1)} %copy-done), kind=kOutput, calls=%fused_computation.21 | convolution fusion | flops 2148532224 | bytes 6291456 | tf_op jit(solution)/shard_map/dot_general | solution.py:8
  175.9 7.9 %all-to-all-start.1 = ((bf16[32,32,1024]{2,1,0:T(8,128)(2,1)}), bf16[32,32,1024]{2,1,0:T(8,128)(2,1)}, u32[]{:S(2)}, u32[]{:S(2)}) async-start(bf16[32,32,1024]{2,1,0:T(8,128)(2,1)} %bitcast.50), calls=%async_computation.2 | async-start | bytes 4194304 | tf_op jit(solution)/shard_map/all_to_all | solution.py:59
  183.9 28.3 %all-to-all-done.1 = bf16[32,32,1024]{2,1,0:T(8,128)(2,1)} async-done(((bf16[32,32,1024]{2,1,0:T(8,128)(2,1)}), bf16[32,32,1024]{2,1,0:T(8,128)(2,1)}, u32[]{:S(2)}, u32[]{:S(2)}) %all-to-all-start.1) | async-done | bytes 2097184 | tf_op jit(solution)/shard_map/all_to_all | solution.py:59
  212.2 2.9 fusion.12
  215.2 0.3 multiply_convert_fusion.1
  215.5 1.1 multiply_convert_fusion
  216.6 1.4 fusion.14
  218.0 31.8 %all_to_all.21 = bf16[32,32,1024]{2,1,0:T(8,128)(2,1)S(1)} all-to-all(bf16[32,32,1024]{2,1,0:T(8,128)(2,1)S(1)} %bitcast.51), channel_id=1, replica_groups=mesh['dp'=4,'expert'=32] {'expert'}, dimensions={0} | all-to-all | bytes 4194304 | tf_op jit(solution)/shard_map/all_to_all | solution.py:72
  249.8 1.3 copy-done.8
  251.1 4.4 %fusion.7 = f32[1024,1024]{1,0:T(8,128)} fusion(bf16[1024,1024]{1,0:T(8,128)(2,1)S(1)} %bitcast.47, bf16[1,1024,1024]{2,1,0:T(8,128)(2,1)S(1)} %copy-done), kind=kOutput, calls=%fused_computation.12 | convolution fusion | flops 2147483648 | bytes 8388608 | tf_op jit(solution)/shard_map/dot_general | solution.py:8
  255.6 43.4 %reduce-scatter.5.cloned.1.call-done = f32[256,1024]{1,0:T(8,128)} async-done(((f32[1024,1024]{1,0:T(8,128)}), f32[256,1024]{1,0:T(8,128)}) %reduce-scatter.5.cloned.1.call-update) | async-done | bytes 1048592 | tf_op jit(solution)/shard_map/reduce_scatter | solution.py:80
  299.0 3.4 fusion.6
  302.4 48.0 %all-gather.5.cloned.1.call-done = bf16[1024,2048]{1,0:T(8,128)(2,1)} async-done(((bf16[256,2048]{1,0:T(8,128)(2,1)}), bf16[1024,2048]{1,0:T(8,128)(2,1)}) %all-gather.5.cloned.1.call-update) | async-done | bytes 4194320 | tf_op jit(solution)/shard_map/all_gather | solution.py:84
  350.4 4.7 %fusion.21 = f32[1024,1024]{1,0:T(8,128)S(1)} fusion(bf16[1024,2048]{1,0:T(8,128)(2,1)} %all-gather.5.cloned.1.call-done, bf16[1,1024,1024]{2,1,0:T(8,128)(2,1)} %param.13), kind=kOutput, calls=%fused_computation.26 | convolution fusion | flops 2147483648 | bytes 8388608 | tf_op jit(solution)/shard_map/dot_general | solution.py:8
  355.2 3.8 add_convert_fusion
  359.0 7.9 %all-to-all-start.3 = ((bf16[32,32,1024]{2,1,0:T(8,128)(2,1)}), bf16[32,32,1024]{2,1,0:T(8,128)(2,1)}, u32[]{:S(2)}, u32[]{:S(2)}) async-start(bf16[32,32,1024]{2,1,0:T(8,128)(2,1)} %bitcast.49), calls=%async_computation.5 | async-start | bytes 4194304 | tf_op jit(solution)/shard_map/all_to_all | solution.py:103
  366.9 6.1 %convolution_bitcast_fusion = f32[1,1024,1024]{2,1,0:T(8,128)} fusion(bf16[1024,1024]{1,0:T(8,128)(2,1)} %all-gather.3.cloned.1.call-done, bf16[1024,1024]{1,0:T(8,128)(2,1)S(1)} %bitcast.48), kind=kOutput, calls=%fused_computation.5 | convolution fusion | flops 2147483648 | bytes 8388608 | tf_op jit(solution)/shard_map/dot_general | solution.py:8
  373.0 4.4 %convolution_bitcast_fusion.2 = f32[1,1024,1024]{2,1,0:T(8,128)} fusion(bf16[1024,1024]{1,0:T(8,128)(2,1)S(1)} %bitcast.45, bf16[1024,2048]{1,0:T(8,128)(2,1)S(1)} %copy-done.14), kind=kOutput, calls=%fused_computation.7 | convolution fusion | flops 2147483648 | bytes 8388608 | tf_op jit(solution)/shard_map/dot_general | solution.py:8
  377.5 4.4 %convolution_bitcast_fusion.1 = f32[1,1024,1024]{2,1,0:T(8,128)} fusion(bf16[1024,1024]{1,0:T(8,128)(2,1)S(1)} %bitcast.46, bf16[1024,2048]{1,0:T(8,128)(2,1)S(1)} %copy-done.14), kind=kOutput, calls=%fused_computation.6 | convolution fusion | flops 2147483648 | bytes 8388608 | tf_op jit(solution)/shard_map/dot_general | solution.py:8
  381.9 13.3 %all-to-all-done.3 = bf16[32,32,1024]{2,1,0:T(8,128)(2,1)} async-done(((bf16[32,32,1024]{2,1,0:T(8,128)(2,1)}), bf16[32,32,1024]{2,1,0:T(8,128)(2,1)}, u32[]{:S(2)}, u32[]{:S(2)}) %all-to-all-start.3) | async-done | bytes 2097184 | tf_op jit(solution)/shard_map/all_to_all | solution.py:103
  395.2 3.1 convolution_convert_fusion.1
  (48 shorter events, 0.7 us)
Async XLA Ops:
  7.2 163.5 %copy-start = (bf16[1,1024,1024]{2,1,0:T(8,128)(2,1)S(1)}, bf16[1,1024,1024]{2,1,0:T(8,128)(2,1)}, u32[]{:S(2)}) copy-start(bf16[1,1024,1024]{2,1,0:T(8,128)(2,1)} %param.15) | copy-start | bytes 6291460
  7.2 129.2 %reduce-scatter.3.cloned.1.call-start = ((), (), s32[]{:S(2)}) async-start(), calls=%async_computation.6 | async-start | bytes 10485760 | tf_op jit(solution)/shard_map/reduce_scatter | solution.py:47
  9.8 39.0 %copy-start.4 = (bf16[512,1024]{1,0:T(8,128)(2,1)}, bf16[512,1024]{1,0:T(8,128)(2,1)S(1)}, u32[]{:S(2)}) copy-start(bf16[512,1024]{1,0:T(8,128)(2,1)S(1)} %fusion.13) | copy-start | bytes 3145732
  12.0 38.1 %copy-start.15 = (bf16[1,1024,1024]{2,1,0:T(8,128)(2,1)S(1)}, bf16[1,1024,1024]{2,1,0:T(8,128)(2,1)}, u32[]{:S(2)}) copy-start(bf16[1,1024,1024]{2,1,0:T(8,128)(2,1)} %param.13) | copy-start | bytes 6291460
  12.0 38.1 %copy-start.16 = (bf16[1,1024,1024]{2,1,0:T(8,128)(2,1)S(1)}, bf16[1,1024,1024]{2,1,0:T(8,128)(2,1)}, u32[]{:S(2)}) copy-start(bf16[1,1024,1024]{2,1,0:T(8,128)(2,1)} %param.14) | copy-start | bytes 6291460
  48.8 1.3 copy-start.6
  57.0 113.7 %all-gather.3.cloned.1.call-start = ((), (), s32[]{:S(2)}) async-start(), calls=%async_computation.7 | async-start | bytes 2621440 | tf_op jit(solution)/shard_map/all_gather | solution.py:55
  175.9 7.9 %copy-start.12 = (f32[256,2]{0,1:T(2,128)S(1)}, f32[256,2]{0,1:T(2,128)}, u32[]{:S(2)}) copy-start(f32[256,2]{0,1:T(2,128)} %param.11) | copy-start | bytes 6148
  175.9 36.3 %all-to-all-start.1 = ((bf16[32,32,1024]{2,1,0:T(8,128)(2,1)}), bf16[32,32,1024]{2,1,0:T(8,128)(2,1)}, u32[]{:S(2)}, u32[]{:S(2)}) async-start(bf16[32,32,1024]{2,1,0:T(8,128)(2,1)} %bitcast.50), calls=%async_computation.2 | async-start | bytes 4194304 | tf_op jit(solution)/shard_map/all_to_all | solution.py:59
  183.8 115.1 %reduce-scatter.5.cloned.1.call-start = ((), (), s32[]{:S(2)}) async-start(), calls=%async_computation.8 | async-start | bytes 5242880 | tf_op jit(solution)/shard_map/reduce_scatter | solution.py:80
  212.2 3.0 copy-start.10
  212.2 3.0 copy-start.11
  249.8 1.3 copy-start.8
  255.5 43.4 %copy-start.2 = (f32[256,1024]{1,0:T(8,128)S(1)}, f32[256,1024]{1,0:T(8,128)}, u32[]{:S(2)}) copy-start(f32[256,1024]{1,0:T(8,128)} %get-tuple-element.8) | copy-start | bytes 3145732
  255.5 43.4 %copy-start.3 = (f32[256,1024]{1,0:T(8,128)S(1)}, f32[256,1024]{1,0:T(8,128)}, u32[]{:S(2)}) copy-start(f32[256,1024]{1,0:T(8,128)} %get-tuple-element.10) | copy-start | bytes 3145732
  255.6 94.9 %all-gather.5.cloned.1.call-start = ((), (), s32[]{:S(2)}) async-start(), calls=%async_computation.9 | async-start | bytes 5242880 | tf_op jit(solution)/shard_map/all_gather | solution.py:84
  302.4 52.8 %copy-start.17 = (bf16[1,1024,1024]{2,1,0:T(8,128)(2,1)S(1)}, bf16[1,1024,1024]{2,1,0:T(8,128)(2,1)}, u32[]{:S(2)}) copy-start(bf16[1,1024,1024]{2,1,0:T(8,128)(2,1)} %param.14) | copy-start | bytes 6291460
  350.4 4.8 %copy-start.13 = (bf16[1024,2048]{1,0:T(8,128)(2,1)S(1)}, bf16[1024,2048]{1,0:T(8,128)(2,1)}, u32[]{:S(2)}) copy-start(bf16[1024,2048]{1,0:T(8,128)(2,1)} %all-gather.5.cloned.1.call-done) | copy-start | bytes 12582916
  359.0 7.9 %copy-start.9 = (bf16[32,32,1024]{2,1,0:T(8,128)(2,1)S(1)}, bf16[32,32,1024]{2,1,0:T(8,128)(2,1)}, u32[]{:S(2)}) copy-start(bf16[32,32,1024]{2,1,0:T(8,128)(2,1)} %copy-done.8) | copy-start | bytes 6291460
  359.0 36.3 %all-to-all-start.3 = ((bf16[32,32,1024]{2,1,0:T(8,128)(2,1)}), bf16[32,32,1024]{2,1,0:T(8,128)(2,1)}, u32[]{:S(2)}, u32[]{:S(2)}) async-start(bf16[32,32,1024]{2,1,0:T(8,128)(2,1)} %bitcast.49), calls=%async_computation.5 | async-start | bytes 4194304 | tf_op jit(solution)/shard_map/all_to_all | solution.py:103
  366.9 6.2 %copy-start.7 = (bf16[32,32,1024]{2,1,0:T(8,128)(2,1)S(1)}, bf16[32,32,1024]{2,1,0:T(8,128)(2,1)}, u32[]{:S(2)}) copy-start(bf16[32,32,1024]{2,1,0:T(8,128)(2,1)} %copy-done.6) | copy-start | bytes 6291460
  366.9 6.2 %copy-start.14 = (bf16[1024,2048]{1,0:T(8,128)(2,1)S(1)}, bf16[1024,2048]{1,0:T(8,128)(2,1)}, u32[]{:S(2)}) copy-start(bf16[1024,2048]{1,0:T(8,128)(2,1)} %all-gather.5.cloned.1.call-done) | copy-start | bytes 12582916
  377.5 17.8 %copy-start.5 = (bf16[512,1024]{1,0:T(8,128)(2,1)S(1)}, bf16[512,1024]{1,0:T(8,128)(2,1)}, u32[]{:S(2)}) copy-start(bf16[512,1024]{1,0:T(8,128)(2,1)} %copy-done.4) | copy-start | bytes 3145732
  377.5 20.9 %copy-start.1 = (bf16[1,1024,1024]{2,1,0:T(8,128)(2,1)S(1)}, bf16[1,1024,1024]{2,1,0:T(8,128)(2,1)}, u32[]{:S(2)}) copy-start(bf16[1,1024,1024]{2,1,0:T(8,128)(2,1)} %param.15) | copy-start | bytes 6291460
Sparse Core Ops, SparseCore 0:
  57.1 79.2 reduce-scatter.2
  140.2 30.4 all-gather.2
  255.7 43.2 reduce-scatter.4
  302.5 47.8 all-gather.4

commit v9 on v6

--- a/solution.py
+++ b/solution.py
@@ -44,6 +44,7 @@
         jnp.bfloat16
     )
     per_token = select[:tok_rows] + select[tok_rows:]
+    select, per_token = lax.optimization_barrier((select, per_token))
     outgoing = contract(per_token, tokens, 0, 0).astype(jnp.bfloat16)
     arrived = lax.all_to_all(
         outgoing.reshape(experts, capacity, quarter),

time: 403 us -> 402 us (level)
  no operation moved by 1% of the time
where the time goes in v9:
time: 402 us; the launch traced here: 401 us
  waiting for transfers between devices  243 us (60%)
  blocking collectives  68.5 us (17%)
  matrix products  47.9 us (12%)
  starting transfers between devices  15.9 us (4%)
  between operations  14 us (3%)
  other arithmetic  8.02 us (2%)
  local copies, waits for them, and re-layouts  4.03 us (1%)
    reduce_scatter x1, waiting for transfers between devices, shards(): lax.psum_scatter(contract(arrived, jnp.concatenate([gate_mat, up_mat], ax...  79.3 us
    all_gather x1, waiting for transfers between devices, shards(): lax.all_gather(jnp.concatenate(derivatives(hidden_grad, gate_pre, up_pre,...  48 us
    dot_general x13, matrix products, contract(): lax.dot_general(left, right, (((left_dim,), (right_dim,)), ((), ())), pre...  47.9 us
    reduce_scatter x1, waiting for transfers between devices, shards(): lax.psum_scatter(contract(grad_slots, down_mat, 1, 1), 'dp', scatter_dime...  43.4 us
    all_to_all x1, blocking collectives, shards(): lax.all_to_all(outgoing.reshape(experts, capacity, quarter), 'expert', sp...  36.8 us
    all_to_all x1, blocking collectives, shards(): lax.all_to_all(grad_out.reshape(experts, capacity, quarter), 'expert', sp...  31.8 us
    all_gather x1, waiting for transfers between devices, shards(): hidden = lax.all_gather(hidden_part, 'dp', axis=0, tiled=True)  30.6 us
    all_to_all x1, waiting for transfers between devices, shards(): lax.all_to_all(out_slots, 'expert', split_axis=0, concat_axis=0, tiled=True)  28.3 us
  transfers between devices with their start and end apart: 6, of which 6 were waited for; matrix products, arithmetic and copies ran while one was open for 4% of the time, Pallas kernels for 0%

profile of v9, /device:TPU:1, one launch (start us, length us, event | category | flops | bytes accessed | tf_op | source)
XLA Modules:
  0.0 401.4 jit_solution(17195756490680356521)
XLA Ops:
  7.2 0.9 copy.20
  8.3 0.3 fusion.17
  8.8 0.8 add_bitcast_fusion
  9.9 0.7 convolution_convert_fusion.1
  10.7 36.8 %all_to_all.20 = bf16[32,32,1024]{2,1,0:T(8,128)(2,1)S(1)} all-to-all(bf16[32,32,1024]{2,1,0:T(8,128)(2,1)S(1)} %bitcast.47), channel_id=1, replica_groups=mesh['dp'=4,'expert'=32] {'expert'}, dimensions={0} | all-to-all | bytes 4194304 | tf_op jit(solution)/shard_map/all_to_all | solution.py:49
  47.5 1.3 copy-done.3
  48.8 7.0 %fusion = f32[1024,2048]{1,0:T(8,128)} fusion(bf16[1024,1024]{1,0:T(8,128)(2,1)S(1)} %bitcast.48, bf16[1024,1024]{1,0:T(8,128)(2,1)S(1)} %bitcast.61, bf16[1024,1024]{1,0:T(8,128)(2,1)S(1)} %bitcast.60), kind=kOutput, calls=%fused_computation | convolution fusion | flops 4303355904 | bytes 14680064 | tf_op jit(solution)/shard_map/dot_general | solution.py:8
  55.9 79.3 %reduce-scatter.3.cloned.1.call-done = f32[256,2048]{1,0:T(8,128)} async-done(((f32[1024,2048]{1,0:T(8,128)}), f32[256,2048]{1,0:T(8,128)}) %reduce-scatter.3.cloned.1.call-update) | async-done | bytes 2097168 | tf_op jit(solution)/shard_map/reduce_scatter | solution.py:56
  135.2 2.6 multiply_convert_fusion.4
  137.9 30.6 %all-gather.3.cloned.1.call-done = bf16[1024,1024]{1,0:T(8,128)(2,1)} async-done(((bf16[256,1024]{1,0:T(8,128)(2,1)}), bf16[1024,1024]{1,0:T(8,128)(2,1)}) %all-gather.3.cloned.1.call-update) | async-done | bytes 2097168 | tf_op jit(solution)/shard_map/all_gather | solution.py:64
  168.5 5.2 %fusion.9 = bf16[1024,1024]{1,0:T(8,128)(2,1)} fusion(bf16[1024,1024]{1,0:T(8,128)(2,1)} %all-gather.3.cloned.1.call-done, bf16[1,1024,1024]{2,1,0:T(8,128)(2,1)S(1)} %copy-done), kind=kOutput, calls=%fused_computation.14 | convolution fusion | flops 2148532224 | bytes 6291456 | tf_op jit(solution)/shard_map/dot_general | solution.py:8
  173.7 7.9 %all-to-all-start.1 = ((bf16[32,32,1024]{2,1,0:T(8,128)(2,1)}), bf16[32,32,1024]{2,1,0:T(8,128)(2,1)}, u32[]{:S(2)}, u32[]{:S(2)}) async-start(bf16[32,32,1024]{2,1,0:T(8,128)(2,1)} %bitcast.54), calls=%async_computation.2 | async-start | bytes 4194304 | tf_op jit(solution)/shard_map/all_to_all | solution.py:68
  181.7 28.3 %all-to-all-done.1 = bf16[32,32,1024]{2,1,0:T(8,128)(2,1)} async-done(((bf16[32,32,1024]{2,1,0:T(8,128)(2,1)}), bf16[32,32,1024]{2,1,0:T(8,128)(2,1)}, u32[]{:S(2)}, u32[]{:S(2)}) %all-to-all-start.1) | async-done | bytes 2097184 | tf_op jit(solution)/shard_map/all_to_all | solution.py:68
  210.0 2.9 fusion.30
  212.9 0.3 multiply_convert_fusion.3
  213.3 1.1 multiply_convert_fusion.2
  214.4 1.3 convolution_convert_fusion
  215.7 31.8 %all_to_all.21 = bf16[32,32,1024]{2,1,0:T(8,128)(2,1)S(1)} all-to-all(bf16[32,32,1024]{2,1,0:T(8,128)(2,1)S(1)} %bitcast.55), channel_id=1, replica_groups=mesh['dp'=4,'expert'=32] {'expert'}, dimensions={0} | all-to-all | bytes 4194304 | tf_op jit(solution)/shard_map/all_to_all | solution.py:81
  247.4 1.3 copy-done.5
  248.7 4.5 %fusion.4 = f32[1024,1024]{1,0:T(8,128)} fusion(bf16[1024,1024]{1,0:T(8,128)(2,1)S(1)} %bitcast.51, bf16[1,1024,1024]{2,1,0:T(8,128)(2,1)S(1)} %copy-done), kind=kOutput, calls=%fused_computation.8 | convolution fusion | flops 2147483648 | bytes 8388608 | tf_op jit(solution)/shard_map/dot_general | solution.py:8
  253.3 43.4 %reduce-scatter.5.cloned.1.call-done = f32[256,1024]{1,0:T(8,128)} async-done(((f32[1024,1024]{1,0:T(8,128)}), f32[256,1024]{1,0:T(8,128)}) %reduce-scatter.5.cloned.1.call-update) | async-done | bytes 1048592 | tf_op jit(solution)/shard_map/reduce_scatter | solution.py:89
  296.6 1.8 multiply_convert_fusion.1
  298.5 1.1 pad_maximum_fusion
  299.6 48.0 %all-gather.5.cloned.1.call-done = bf16[1024,2048]{1,0:T(8,128)(2,1)} async-done(((bf16[256,2048]{1,0:T(8,128)(2,1)}), bf16[1024,2048]{1,0:T(8,128)(2,1)}) %all-gather.5.cloned.1.call-update) | async-done | bytes 4194320 | tf_op jit(solution)/shard_map/all_gather | solution.py:92
  347.6 4.1 %fusion.15 = f32[1024,1024]{1,0:T(8,128)S(1)} fusion(bf16[1024,2048]{1,0:T(8,128)(2,1)} %all-gather.5.cloned.1.call-done, bf16[1,1024,1024]{2,1,0:T(8,128)(2,1)S(1)} %copy-done.16), kind=kOutput, calls=%fused_computation.20 | convolution fusion | flops 2147483648 | bytes 8388608 | tf_op jit(solution)/shard_map/dot_general | solution.py:8
  351.8 3.8 add_convert_fusion
  355.5 7.9 %all-to-all-start.3 = ((bf16[32,32,1024]{2,1,0:T(8,128)(2,1)}), bf16[32,32,1024]{2,1,0:T(8,128)(2,1)}, u32[]{:S(2)}, u32[]{:S(2)}) async-start(bf16[32,32,1024]{2,1,0:T(8,128)(2,1)} %bitcast.53), calls=%async_computation.5 | async-start | bytes 4194304 | tf_op jit(solution)/shard_map/all_to_all | solution.py:104
  363.5 6.1 %convolution_bitcast_fusion = f32[1,1024,1024]{2,1,0:T(8,128)} fusion(bf16[1024,1024]{1,0:T(8,128)(2,1)} %all-gather.3.cloned.1.call-done, bf16[1024,1024]{1,0:T(8,128)(2,1)S(1)} %bitcast.52), kind=kOutput, calls=%fused_computation.5 | convolution fusion | flops 2147483648 | bytes 8388608 | tf_op jit(solution)/shard_map/dot_general | solution.py:8
  369.6 4.4 %convolution_bitcast_fusion.2 = f32[1,1024,1024]{2,1,0:T(8,128)} fusion(bf16[1024,1024]{1,0:T(8,128)(2,1)S(1)} %bitcast.49, bf16[1024,2048]{1,0:T(8,128)(2,1)S(1)} %copy-done.14), kind=kOutput, calls=%fused_computation.7 | convolution fusion | flops 2147483648 | bytes 8388608 | tf_op jit(solution)/shard_map/dot_general | solution.py:8
  374.1 4.4 %convolution_bitcast_fusion.1 = f32[1,1024,1024]{2,1,0:T(8,128)} fusion(bf16[1024,1024]{1,0:T(8,128)(2,1)S(1)} %bitcast.50, bf16[1024,2048]{1,0:T(8,128)(2,1)S(1)} %copy-done.14), kind=kOutput, calls=%fused_computation.6 | convolution fusion | flops 2147483648 | bytes 8388608 | tf_op jit(solution)/shard_map/dot_general | solution.py:8
  378.5 13.3 %all-to-all-done.3 = bf16[32,32,1024]{2,1,0:T(8,128)(2,1)} async-done(((bf16[32,32,1024]{2,1,0:T(8,128)(2,1)}), bf16[32,32,1024]{2,1,0:T(8,128)(2,1)}, u32[]{:S(2)}, u32[]{:S(2)}) %all-to-all-start.3) | async-done | bytes 2097184 | tf_op jit(solution)/shard_map/all_to_all | solution.py:104
  391.8 3.1 convolution_convert_fusion.2
  (52 shorter events, 1.0 us)
Async XLA Ops:
  7.2 161.3 %copy-start = (bf16[1,1024,1024]{2,1,0:T(8,128)(2,1)S(1)}, bf16[1,1024,1024]{2,1,0:T(8,128)(2,1)}, u32[]{:S(2)}) copy-start(bf16[1,1024,1024]{2,1,0:T(8,128)(2,1)} %param.15) | copy-start | bytes 6291460
  7.2 128.0 %reduce-scatter.3.cloned.1.call-start = ((), (), s32[]{:S(2)}) async-start(), calls=%async_computation.6 | async-start | bytes 10485760 | tf_op jit(solution)/shard_map/reduce_scatter | solution.py:56
  8.8 1.1 copy-start.10
  9.9 37.6 %copy-start.8 = (bf16[256,1024]{1,0:T(8,128)(2,1)}, bf16[256,1024]{1,0:T(8,128)(2,1)S(1)}, u32[]{:S(2)}) copy-start(bf16[256,1024]{1,0:T(8,128)(2,1)S(1)} %slice_add_fusion) | copy-start | bytes 1572868
  10.7 38.1 %copy-start.15 = (bf16[1,1024,1024]{2,1,0:T(8,128)(2,1)S(1)}, bf16[1,1024,1024]{2,1,0:T(8,128)(2,1)}, u32[]{:S(2)}) copy-start(bf16[1,1024,1024]{2,1,0:T(8,128)(2,1)} %param.13) | copy-start | bytes 6291460
  10.7 38.1 %copy-start.17 = (bf16[1,1024,1024]{2,1,0:T(8,128)(2,1)S(1)}, bf16[1,1024,1024]{2,1,0:T(8,128)(2,1)}, u32[]{:S(2)}) copy-start(bf16[1,1024,1024]{2,1,0:T(8,128)(2,1)} %param.14) | copy-start | bytes 6291460
  47.5 1.3 copy-start.3
  55.8 112.7 %all-gather.3.cloned.1.call-start = ((), (), s32[]{:S(2)}) async-start(), calls=%async_computation.7 | async-start | bytes 2621440 | tf_op jit(solution)/shard_map/all_gather | solution.py:64
  173.7 7.9 %copy-start.12 = (f32[256,2]{0,1:T(2,128)S(1)}, f32[256,2]{0,1:T(2,128)}, u32[]{:S(2)}) copy-start(f32[256,2]{0,1:T(2,128)} %param.11) | copy-start | bytes 6148
  173.7 36.3 %all-to-all-start.1 = ((bf16[32,32,1024]{2,1,0:T(8,128)(2,1)}), bf16[32,32,1024]{2,1,0:T(8,128)(2,1)}, u32[]{:S(2)}, u32[]{:S(2)}) async-start(bf16[32,32,1024]{2,1,0:T(8,128)(2,1)} %bitcast.54), calls=%async_computation.2 | async-start | bytes 4194304 | tf_op jit(solution)/shard_map/all_to_all | solution.py:68
  181.6 115.0 %reduce-scatter.5.cloned.1.call-start = ((), (), s32[]{:S(2)}) async-start(), calls=%async_computation.8 | async-start | bytes 5242880 | tf_op jit(solution)/shard_map/reduce_scatter | solution.py:89
  210.0 2.9 copy-start.7
  210.0 2.9 copy-start.11
  247.4 1.3 copy-start.5
  253.2 43.4 %copy-start.2 = (f32[256,2048]{1,0:T(8,128)S(1)}, f32[256,2048]{1,0:T(8,128)}, u32[]{:S(2)}) copy-start(f32[256,2048]{1,0:T(8,128)} %reduce-scatter.3.cloned.1.call-done) | copy-start | bytes 6291460
  253.2 94.4 %all-gather.5.cloned.1.call-start = ((), (), s32[]{:S(2)}) async-start(), calls=%async_computation.9 | async-start | bytes 5242880 | tf_op jit(solution)/shard_map/all_gather | solution.py:92
  298.5 49.1 %copy-start.16 = (bf16[1,1024,1024]{2,1,0:T(8,128)(2,1)S(1)}, bf16[1,1024,1024]{2,1,0:T(8,128)(2,1)}, u32[]{:S(2)}) copy-start(bf16[1,1024,1024]{2,1,0:T(8,128)(2,1)} %param.13) | copy-start | bytes 6291460
  347.6 4.1 %copy-start.13 = (bf16[1024,2048]{1,0:T(8,128)(2,1)S(1)}, bf16[1024,2048]{1,0:T(8,128)(2,1)}, u32[]{:S(2)}) copy-start(bf16[1024,2048]{1,0:T(8,128)(2,1)} %all-gather.5.cloned.1.call-done) | copy-start | bytes 12582916
  347.6 4.1 %copy-start.18 = (bf16[1,1024,1024]{2,1,0:T(8,128)(2,1)S(1)}, bf16[1,1024,1024]{2,1,0:T(8,128)(2,1)}, u32[]{:S(2)}) copy-start(bf16[1,1024,1024]{2,1,0:T(8,128)(2,1)} %param.14) | copy-start | bytes 6291460
  355.5 7.9 %copy-start.6 = (bf16[32,32,1024]{2,1,0:T(8,128)(2,1)S(1)}, bf16[32,32,1024]{2,1,0:T(8,128)(2,1)}, u32[]{:S(2)}) copy-start(bf16[32,32,1024]{2,1,0:T(8,128)(2,1)} %copy-done.5) | copy-start | bytes 6291460
  355.5 36.3 %all-to-all-start.3 = ((bf16[32,32,1024]{2,1,0:T(8,128)(2,1)}), bf16[32,32,1024]{2,1,0:T(8,128)(2,1)}, u32[]{:S(2)}, u32[]{:S(2)}) async-start(bf16[32,32,1024]{2,1,0:T(8,128)(2,1)} %bitcast.53), calls=%async_computation.5 | async-start | bytes 4194304 | tf_op jit(solution)/shard_map/all_to_all | solution.py:104
  363.4 6.2 %copy-start.4 = (bf16[32,32,1024]{2,1,0:T(8,128)(2,1)S(1)}, bf16[32,32,1024]{2,1,0:T(8,128)(2,1)}, u32[]{:S(2)}) copy-start(bf16[32,32,1024]{2,1,0:T(8,128)(2,1)} %copy-done.3) | copy-start | bytes 6291460
  363.5 6.2 %copy-start.14 = (bf16[1024,2048]{1,0:T(8,128)(2,1)S(1)}, bf16[1024,2048]{1,0:T(8,128)(2,1)}, u32[]{:S(2)}) copy-start(bf16[1024,2048]{1,0:T(8,128)(2,1)} %all-gather.5.cloned.1.call-done) | copy-start | bytes 12582916
  374.1 17.8 %copy-start.9 = (bf16[256,1024]{1,0:T(8,128)(2,1)S(1)}, bf16[256,1024]{1,0:T(8,128)(2,1)}, u32[]{:S(2)}) copy-start(bf16[256,1024]{1,0:T(8,128)(2,1)} %copy-done.8) | copy-start | bytes 1572868
  374.1 20.9 %copy-start.1 = (bf16[1,1024,1024]{2,1,0:T(8,128)(2,1)S(1)}, bf16[1,1024,1024]{2,1,0:T(8,128)(2,1)}, u32[]{:S(2)}) copy-start(bf16[1,1024,1024]{2,1,0:T(8,128)(2,1)} %param.15) | copy-start | bytes 6291460
Sparse Core Ops, SparseCore 0:
  55.9 79.2 reduce-scatter.2
  138.0 30.4 all-gather.2
  253.3 43.2 reduce-scatter.4
  299.7 47.8 all-gather.4

commit v10 on v9

--- a/solution.py
+++ b/solution.py
@@ -33,13 +33,14 @@
     up_mat = w_up[0]
     down_mat = w_down[0]
     ff = gate_mat.shape[1]
-    listed = expert_ids.reshape(-1)
-    order = jnp.arange(2 * tok_rows, dtype=jnp.int32)
+    listed = expert_ids.T.reshape(-1)
+    place = jnp.arange(2 * tok_rows, dtype=jnp.int32)
+    order = 2 * (place % tok_rows) + place // tok_rows
     onehot = (listed[:, None] == jnp.arange(experts, dtype=jnp.int32)[None, :]).astype(jnp.bfloat16)
     before = (order[None, :] < order[:, None]).astype(jnp.bfloat16)
     counts = contract(before, onehot, 1, 0)
     ranks = jnp.sum(counts * onehot.astype(jnp.float32), axis=1).astype(jnp.int32)
-    slot_rows = (listed * capacity + ranks).reshape(tok_rows, 2).T.reshape(-1)
+    slot_rows = listed * capacity + ranks
     select = (slot_rows[:, None] == jnp.arange(rows_all, dtype=slot_rows.dtype)[None, :]).astype(
         jnp.bfloat16
     )

time: 402 us -> 401 us (level)
  no operation moved by 1% of the time
where the time goes in v10:
time: 401 us; the launch traced here: 400 us
  waiting for transfers between devices  243 us (61%)
  blocking collectives  68.5 us (17%)
  matrix products  48 us (12%)
  starting transfers between devices  16.1 us (4%)
  between operations  14 us (3%)
  other arithmetic  7.27 us (2%)
    reduce_scatter x1, waiting for transfers between devices, shards(): lax.psum_scatter(contract(arrived, jnp.concatenate([gate_mat, up_mat], ax...  79.3 us
    all_gather x1, waiting for transfers between devices, shards(): lax.all_gather(jnp.concatenate(derivatives(hidden_grad, gate_pre, up_pre,...  48 us
    dot_general x13, matrix products, contract(): lax.dot_general(left, right, (((left_dim,), (right_dim,)), ((), ())), pre...  48 us
    reduce_scatter x1, waiting for transfers between devices, shards(): lax.psum_scatter(contract(grad_slots, down_mat, 1, 1), 'dp', scatter_dime...  43.2 us
    all_to_all x1, blocking collectives, shards(): lax.all_to_all(outgoing.reshape(experts, capacity, quarter), 'expert', sp...  36.8 us
    all_to_all x1, blocking collectives, shards(): lax.all_to_all(grad_out.reshape(experts, capacity, quarter), 'expert', sp...  31.8 us
    all_gather x1, waiting for transfers between devices, shards(): hidden = lax.all_gather(hidden_part, 'dp', axis=0, tiled=True)  30.6 us
    all_to_all x1, waiting for transfers between devices, shards(): lax.all_to_all(out_slots, 'expert', split_axis=0, concat_axis=0, tiled=True)  28.3 us
  transfers between devices with their start and end apart: 6, of which 6 were waited for; matrix products, arithmetic and copies ran while one was open for 4% of the time, Pallas kernels for 0%

profile of v10, /device:TPU:1, one launch (start us, length us, event | category | flops | bytes accessed | tf_op | source)
XLA Modules:
  0.0 400.3 jit_solution(288568324781548726)
XLA Ops:
  7.2 0.8 copy.13
  8.1 0.4 fusion.17
  8.5 0.2 fusion.8
  8.8 0.7 convolution_convert_fusion.1
  9.6 36.8 %all_to_all.20 = bf16[32,32,1024]{2,1,0:T(8,128)(2,1)S(1)} all-to-all(bf16[32,32,1024]{2,1,0:T(8,128)(2,1)S(1)} %bitcast.46), channel_id=1, replica_groups=mesh['dp'=4,'expert'=32] {'expert'}, dimensions={0} | all-to-all | bytes 4194304 | tf_op jit(solution)/shard_map/all_to_all | solution.py:50
  46.4 1.3 copy-done.3
  47.7 7.0 %fusion = f32[1024,2048]{1,0:T(8,128)} fusion(bf16[1024,1024]{1,0:T(8,128)(2,1)S(1)} %bitcast.47, bf16[1024,1024]{1,0:T(8,128)(2,1)S(1)} %bitcast.62, bf16[1024,1024]{1,0:T(8,128)(2,1)S(1)} %bitcast.61), kind=kOutput, calls=%fused_computation | convolution fusion | flops 4303355904 | bytes 14680064 | tf_op jit(solution)/shard_map/dot_general | solution.py:8
  54.8 79.3 %reduce-scatter.3.cloned.1.call-done = f32[256,2048]{1,0:T(8,128)} async-done(((f32[1024,2048]{1,0:T(8,128)}), f32[256,2048]{1,0:T(8,128)}) %reduce-scatter.3.cloned.1.call-update) | async-done | bytes 2097168 | tf_op jit(solution)/shard_map/reduce_scatter | solution.py:57
  134.1 2.6 multiply_convert_fusion.4
  136.8 30.6 %all-gather.3.cloned.1.call-done = bf16[1024,1024]{1,0:T(8,128)(2,1)} async-done(((bf16[256,1024]{1,0:T(8,128)(2,1)}), bf16[1024,1024]{1,0:T(8,128)(2,1)}) %all-gather.3.cloned.1.call-update) | async-done | bytes 2097168 | tf_op jit(solution)/shard_map/all_gather | solution.py:65
  167.4 5.2 %fusion.9 = bf16[1024,1024]{1,0:T(8,128)(2,1)} fusion(bf16[1024,1024]{1,0:T(8,128)(2,1)} %all-gather.3.cloned.1.call-done, bf16[1,1024,1024]{2,1,0:T(8,128)(2,1)S(1)} %copy-done), kind=kOutput, calls=%fused_computation.14 | convolution fusion | flops 2148532224 | bytes 6291456 | tf_op jit(solution)/shard_map/dot_general | solution.py:8
  172.6 7.9 %all-to-all-start.1 = ((bf16[32,32,1024]{2,1,0:T(8,128)(2,1)}), bf16[32,32,1024]{2,1,0:T(8,128)(2,1)}, u32[]{:S(2)}, u32[]{:S(2)}) async-start(bf16[32,32,1024]{2,1,0:T(8,128)(2,1)} %bitcast.53), calls=%async_computation.2 | async-start | bytes 4194304 | tf_op jit(solution)/shard_map/all_to_all | solution.py:69
  180.6 28.3 %all-to-all-done.1 = bf16[32,32,1024]{2,1,0:T(8,128)(2,1)} async-done(((bf16[32,32,1024]{2,1,0:T(8,128)(2,1)}), bf16[32,32,1024]{2,1,0:T(8,128)(2,1)}, u32[]{:S(2)}, u32[]{:S(2)}) %all-to-all-start.1) | async-done | bytes 2097184 | tf_op jit(solution)/shard_map/all_to_all | solution.py:69
  208.9 2.9 fusion.42
  211.8 0.3 multiply_convert_fusion.3
  212.2 1.1 multiply_convert_fusion.2
  213.2 1.3 convolution_convert_fusion
  214.6 31.8 %all_to_all.21 = bf16[32,32,1024]{2,1,0:T(8,128)(2,1)S(1)} all-to-all(bf16[32,32,1024]{2,1,0:T(8,128)(2,1)S(1)} %bitcast.54), channel_id=1, replica_groups=mesh['dp'=4,'expert'=32] {'expert'}, dimensions={0} | all-to-all | bytes 4194304 | tf_op jit(solution)/shard_map/all_to_all | solution.py:82
  246.3 1.3 copy-done.5
  247.6 4.4 %fusion.4 = f32[1024,1024]{1,0:T(8,128)} fusion(bf16[1024,1024]{1,0:T(8,128)(2,1)S(1)} %bitcast.50, bf16[1,1024,1024]{2,1,0:T(8,128)(2,1)S(1)} %copy-done), kind=kOutput, calls=%fused_computation.8 | convolution fusion | flops 2147483648 | bytes 8388608 | tf_op jit(solution)/shard_map/dot_general | solution.py:8
  252.3 43.2 %reduce-scatter.5.cloned.1.call-done = f32[256,1024]{1,0:T(8,128)} async-done(((f32[1024,1024]{1,0:T(8,128)}), f32[256,1024]{1,0:T(8,128)}) %reduce-scatter.5.cloned.1.call-update) | async-done | bytes 1048592 | tf_op jit(solution)/shard_map/reduce_scatter | solution.py:90
  295.5 1.8 multiply_convert_fusion.1
  297.4 1.1 pad_maximum_fusion
  298.5 48.0 %all-gather.5.cloned.1.call-done = bf16[1024,2048]{1,0:T(8,128)(2,1)} async-done(((bf16[256,2048]{1,0:T(8,128)(2,1)}), bf16[1024,2048]{1,0:T(8,128)(2,1)}) %all-gather.5.cloned.1.call-update) | async-done | bytes 4194320 | tf_op jit(solution)/shard_map/all_gather | solution.py:93
  346.5 4.1 %fusion.15 = f32[1024,1024]{1,0:T(8,128)S(1)} fusion(bf16[1024,2048]{1,0:T(8,128)(2,1)} %all-gather.5.cloned.1.call-done, bf16[1,1024,1024]{2,1,0:T(8,128)(2,1)S(1)} %copy-done.16), kind=kOutput, calls=%fused_computation.20 | convolution fusion | flops 2147483648 | bytes 8388608 | tf_op jit(solution)/shard_map/dot_general | solution.py:8
  350.7 3.8 add_convert_fusion
  354.4 7.9 %all-to-all-start.3 = ((bf16[32,32,1024]{2,1,0:T(8,128)(2,1)}), bf16[32,32,1024]{2,1,0:T(8,128)(2,1)}, u32[]{:S(2)}, u32[]{:S(2)}) async-start(bf16[32,32,1024]{2,1,0:T(8,128)(2,1)} %bitcast.52), calls=%async_computation.5 | async-start | bytes 4194304 | tf_op jit(solution)/shard_map/all_to_all | solution.py:105
  362.3 6.1 %convolution_bitcast_fusion = f32[1,1024,1024]{2,1,0:T(8,128)} fusion(bf16[1024,1024]{1,0:T(8,128)(2,1)} %all-gather.3.cloned.1.call-done, bf16[1024,1024]{1,0:T(8,128)(2,1)S(1)} %bitcast.51), kind=kOutput, calls=%fused_computation.5 | convolution fusion | flops 2147483648 | bytes 8388608 | tf_op jit(solution)/shard_map/dot_general | solution.py:8
  368.5 4.4 %convolution_bitcast_fusion.2 = f32[1,1024,1024]{2,1,0:T(8,128)} fusion(bf16[1024,1024]{1,0:T(8,128)(2,1)S(1)} %bitcast.48, bf16[1024,2048]{1,0:T(8,128)(2,1)S(1)} %copy-done.14), kind=kOutput, calls=%fused_computation.7 | convolution fusion | flops 2147483648 | bytes 8388608 | tf_op jit(solution)/shard_map/dot_general | solution.py:8
  372.9 4.4 %convolution_bitcast_fusion.1 = f32[1,1024,1024]{2,1,0:T(8,128)} fusion(bf16[1024,1024]{1,0:T(8,128)(2,1)S(1)} %bitcast.49, bf16[1024,2048]{1,0:T(8,128)(2,1)S(1)} %copy-done.14), kind=kOutput, calls=%fused_computation.6 | convolution fusion | flops 2147483648 | bytes 8388608 | tf_op jit(solution)/shard_map/dot_general | solution.py:8
  377.4 13.3 %all-to-all-done.3 = bf16[32,32,1024]{2,1,0:T(8,128)(2,1)} async-done(((bf16[32,32,1024]{2,1,0:T(8,128)(2,1)}), bf16[32,32,1024]{2,1,0:T(8,128)(2,1)}, u32[]{:S(2)}, u32[]{:S(2)}) %all-to-all-start.3) | async-done | bytes 2097184 | tf_op jit(solution)/shard_map/all_to_all | solution.py:105
  390.7 3.1 convolution_convert_fusion.2
  (48 shorter events, 0.6 us)
Async XLA Ops:
  7.2 160.2 %copy-start = (bf16[1,1024,1024]{2,1,0:T(8,128)(2,1)S(1)}, bf16[1,1024,1024]{2,1,0:T(8,128)(2,1)}, u32[]{:S(2)}) copy-start(bf16[1,1024,1024]{2,1,0:T(8,128)(2,1)} %param.15) | copy-start | bytes 6291460
  7.2 126.9 %reduce-scatter.3.cloned.1.call-start = ((), (), s32[]{:S(2)}) async-start(), calls=%async_computation.6 | async-start | bytes 10485760 | tf_op jit(solution)/shard_map/reduce_scatter | solution.py:57
  7.2 1.6 copy-start.10
  8.8 37.6 %copy-start.8 = (bf16[256,1024]{1,0:T(8,128)(2,1)}, bf16[256,1024]{1,0:T(8,128)(2,1)S(1)}, u32[]{:S(2)}) copy-start(bf16[256,1024]{1,0:T(8,128)(2,1)S(1)} %slice_add_fusion) | copy-start | bytes 1572868
  9.6 38.1 %copy-start.15 = (bf16[1,1024,1024]{2,1,0:T(8,128)(2,1)S(1)}, bf16[1,1024,1024]{2,1,0:T(8,128)(2,1)}, u32[]{:S(2)}) copy-start(bf16[1,1024,1024]{2,1,0:T(8,128)(2,1)} %param.13) | copy-start | bytes 6291460
  9.6 38.1 %copy-start.17 = (bf16[1,1024,1024]{2,1,0:T(8,128)(2,1)S(1)}, bf16[1,1024,1024]{2,1,0:T(8,128)(2,1)}, u32[]{:S(2)}) copy-start(bf16[1,1024,1024]{2,1,0:T(8,128)(2,1)} %param.14) | copy-start | bytes 6291460
  46.4 1.3 copy-start.3
  54.7 112.7 %all-gather.3.cloned.1.call-start = ((), (), s32[]{:S(2)}) async-start(), calls=%async_computation.7 | async-start | bytes 2621440 | tf_op jit(solution)/shard_map/all_gather | solution.py:65
  172.6 7.9 %copy-start.12 = (f32[256,2]{0,1:T(2,128)S(1)}, f32[256,2]{0,1:T(2,128)}, u32[]{:S(2)}) copy-start(f32[256,2]{0,1:T(2,128)} %param.11) | copy-start | bytes 6148
  172.6 36.3 %all-to-all-start.1 = ((bf16[32,32,1024]{2,1,0:T(8,128)(2,1)}), bf16[32,32,1024]{2,1,0:T(8,128)(2,1)}, u32[]{:S(2)}, u32[]{:S(2)}) async-start(bf16[32,32,1024]{2,1,0:T(8,128)(2,1)} %bitcast.53), calls=%async_computation.2 | async-start | bytes 4194304 | tf_op jit(solution)/shard_map/all_to_all | solution.py:69
  180.5 115.0 %reduce-scatter.5.cloned.1.call-start = ((), (), s32[]{:S(2)}) async-start(), calls=%async_computation.8 | async-start | bytes 5242880 | tf_op jit(solution)/shard_map/reduce_scatter | solution.py:90
  208.9 2.9 copy-start.7
  208.9 2.9 copy-start.11
  246.3 1.3 copy-start.5
  252.1 43.4 %copy-start.2 = (f32[256,2048]{1,0:T(8,128)S(1)}, f32[256,2048]{1,0:T(8,128)}, u32[]{:S(2)}) copy-start(f32[256,2048]{1,0:T(8,128)} %reduce-scatter.3.cloned.1.call-done) | copy-start | bytes 6291460
  252.1 94.4 %all-gather.5.cloned.1.call-start = ((), (), s32[]{:S(2)}) async-start(), calls=%async_computation.9 | async-start | bytes 5242880 | tf_op jit(solution)/shard_map/all_gather | solution.py:93
  297.4 49.1 %copy-start.16 = (bf16[1,1024,1024]{2,1,0:T(8,128)(2,1)S(1)}, bf16[1,1024,1024]{2,1,0:T(8,128)(2,1)}, u32[]{:S(2)}) copy-start(bf16[1,1024,1024]{2,1,0:T(8,128)(2,1)} %param.13) | copy-start | bytes 6291460
  346.5 4.1 %copy-start.13 = (bf16[1024,2048]{1,0:T(8,128)(2,1)S(1)}, bf16[1024,2048]{1,0:T(8,128)(2,1)}, u32[]{:S(2)}) copy-start(bf16[1024,2048]{1,0:T(8,128)(2,1)} %all-gather.5.cloned.1.call-done) | copy-start | bytes 12582916
  346.5 4.1 %copy-start.18 = (bf16[1,1024,1024]{2,1,0:T(8,128)(2,1)S(1)}, bf16[1,1024,1024]{2,1,0:T(8,128)(2,1)}, u32[]{:S(2)}) copy-start(bf16[1,1024,1024]{2,1,0:T(8,128)(2,1)} %param.14) | copy-start | bytes 6291460
  354.4 7.9 %copy-start.6 = (bf16[32,32,1024]{2,1,0:T(8,128)(2,1)S(1)}, bf16[32,32,1024]{2,1,0:T(8,128)(2,1)}, u32[]{:S(2)}) copy-start(bf16[32,32,1024]{2,1,0:T(8,128)(2,1)} %copy-done.5) | copy-start | bytes 6291460
  354.4 36.3 %all-to-all-start.3 = ((bf16[32,32,1024]{2,1,0:T(8,128)(2,1)}), bf16[32,32,1024]{2,1,0:T(8,128)(2,1)}, u32[]{:S(2)}, u32[]{:S(2)}) async-start(bf16[32,32,1024]{2,1,0:T(8,128)(2,1)} %bitcast.52), calls=%async_computation.5 | async-start | bytes 4194304 | tf_op jit(solution)/shard_map/all_to_all | solution.py:105
  362.3 6.2 %copy-start.4 = (bf16[32,32,1024]{2,1,0:T(8,128)(2,1)S(1)}, bf16[32,32,1024]{2,1,0:T(8,128)(2,1)}, u32[]{:S(2)}) copy-start(bf16[32,32,1024]{2,1,0:T(8,128)(2,1)} %copy-done.3) | copy-start | bytes 6291460
  362.3 6.2 %copy-start.14 = (bf16[1024,2048]{1,0:T(8,128)(2,1)S(1)}, bf16[1024,2048]{1,0:T(8,128)(2,1)}, u32[]{:S(2)}) copy-start(bf16[1024,2048]{1,0:T(8,128)(2,1)} %all-gather.5.cloned.1.call-done) | copy-start | bytes 12582916
  372.9 17.8 %copy-start.9 = (bf16[256,1024]{1,0:T(8,128)(2,1)S(1)}, bf16[256,1024]{1,0:T(8,128)(2,1)}, u32[]{:S(2)}) copy-start(bf16[256,1024]{1,0:T(8,128)(2,1)} %copy-done.8) | copy-start | bytes 1572868
  372.9 20.9 %copy-start.1 = (bf16[1,1024,1024]{2,1,0:T(8,128)(2,1)S(1)}, bf16[1,1024,1024]{2,1,0:T(8,128)(2,1)}, u32[]{:S(2)}) copy-start(bf16[1,1024,1024]{2,1,0:T(8,128)(2,1)} %param.15) | copy-start | bytes 6291460
Sparse Core Ops, SparseCore 0:
  54.8 79.2 reduce-scatter.2
  136.9 30.4 all-gather.2
  252.2 43.2 reduce-scatter.4
  298.6 47.8 all-gather.4
